TPU v7x, 32 devices: a whole 2x2x4 slice. The times are simulated.
32 devices in a mesh: rep: 2 (over y), seq: 4 (over z), head: 4 (over x, core).
Axes of the slice: x: 2, y: 2, z: 4, core: 2. Of those that a mesh axis runs over, the one named last changes fastest.
Arguments:
- queries: bfloat16 [3072, 2560], P(('rep', 'seq'), 'head'), parts along dimension 0, may hold values from -16 to 16
- keys: bfloat16 [3072, 2560], P(('rep', 'seq'), 'head'), parts along dimension 0, may hold values from -6 to 6
- values: bfloat16 [3072, 2560], P(('rep', 'seq'), 'head'), parts along dimension 0, may hold values from -6 to 6
- out_weight: bfloat16 [2560, 5120], P('seq', 'head'), may hold values from -0.3125 to 0.3125
- neighbours: int32 [8, 27], P('rep'), parts along dimension 0, may hold values from -1 to 3, as said below
- clip_ids: int32 [3072], P(('rep', 'seq')), parts along dimension 0, may hold values from 0 to 1
Outputs:
- output: bfloat16 [3072, 5120], P(('rep', 'seq'), 'head'), parts along dimension 0
There are 2 independent parts, one for each index of `rep`. A program takes and returns all parts, laid end to end along the dimension named above; an argument that names none is the same for every part. Nothing has to cross between parts.
Inputs may be any that keep to these rules, and one draw needn't show every extreme that they name: `neighbours`: column 9 (a + 1) + 3 (b + 1) + (c + 1) of row s, for a, b, c each -1, 0 or 1, is either -1 or s + a * 4 * 7 + b * 7 + c; column 13 of row s is s.
All inputs are finite; a program needn't handle non-finite values.
Results may differ from a plain program's by a relative error of at most 0.0058.
Values may be sent and summed in bfloat16 or wider, within the bound.
No kernel may reach another device: no remote copies, remote signals or barrier semaphores. Data moves between devices by JAX's collectives and lax.ppermute only.
A program may use at most 192 MiB of HBM per device.

v0:
```python
import math

import jax
import jax.numpy as jnp
from jax import lax
from jax.sharding import PartitionSpec as P

HD = 128
TGH = 4
TGW = 7


def from_behind(value, axis, by):
    peers = lax.axis_size(axis)
    pairs = [(i, i + by) for i in range(peers) if 0 <= i + by < peers]
    return lax.ppermute(value, axis, pairs)


def attend_head(query_head, key_head, value_head, allowed):
    scores = lax.dot_general(
        query_head, key_head, (((1,), (1,)), ((), ())), preferred_element_type=jnp.float32
    ) * (1.0 / math.sqrt(query_head.shape[1]))
    masked = jnp.where(allowed, scores, -1e30)
    highest = jnp.max(masked, axis=1, keepdims=True)
    raised = jnp.where(allowed, jnp.exp(masked - highest), 0.0)
    summed = jnp.sum(raised, axis=1, keepdims=True)
    weights = (raised / summed).astype(jnp.bfloat16)
    return jnp.dot(weights, value_head, preferred_element_type=jnp.float32).astype(jnp.bfloat16)


def on_device(queries, keys, values, out_weight, neighbours, clip_ids):
    tile_rows = queries.shape[0]
    feature_width = queries.shape[1]
    seq_count = lax.axis_size("seq")
    layer_tiles = TGH * TGW
    every_offset = set()
    for layer_step in (-1, 0, 1):
        for row_step in (-1, 0, 1):
            for col_step in (-1, 0, 1):
                every_offset.add(layer_step * layer_tiles + row_step * TGW + col_step)
    distances = [offset for offset in sorted(every_offset) if 0 < offset < seq_count]
    key_list = [keys]
    value_list = [values]
    clip_list = [clip_ids]
    offsets = [0]
    for distance in distances:
        below_keys, below_values, below_clips = from_behind(
            (keys, values, clip_ids), "seq", distance
        )
        above_keys, above_values, above_clips = from_behind(
            (keys, values, clip_ids), "seq", -distance
        )
        key_list += [below_keys, above_keys]
        value_list += [below_values, above_values]
        clip_list += [below_clips, above_clips]
        offsets += [distance, -distance]
    key_stack = jnp.stack(key_list)
    value_stack = jnp.stack(value_list)
    clip_stack = jnp.stack(clip_list)
    blocks = key_stack.shape[0]
    position = lax.axis_index("seq")
    window_row = lax.dynamic_index_in_dim(neighbours, position, 0, keepdims=False)
    sources = position - jnp.asarray(offsets, dtype=jnp.int32)
    present = jnp.any(
        (window_row[None, :] == sources[:, None]) & (window_row[None, :] >= 0), axis=1
    )
    key_clips = clip_stack.reshape(blocks * tile_rows)
    allowed = jnp.repeat(present, tile_rows)[None, :] & (clip_ids[:, None] == key_clips[None, :])
    key_rows = key_stack.reshape(blocks * tile_rows, feature_width)
    value_rows = value_stack.reshape(blocks * tile_rows, feature_width)
    head_outputs = []
    for head_index in range(feature_width // HD):
        first_col = head_index * HD
        head_outputs.append(
            attend_head(
                queries[:, first_col : first_col + HD],
                key_rows[:, first_col : first_col + HD],
                value_rows[:, first_col : first_col + HD],
                allowed,
            )
        )
    attended = jnp.concatenate(head_outputs, axis=1)
    all_features = lax.all_gather(attended, "head", axis=1, tiled=True)
    empty = jnp.zeros((tile_rows, out_weight.shape[1]), jnp.float32)
    weight_piece = lax.all_gather(out_weight, "seq", axis=0, tiled=True)
    features = lax.slice_in_dim(all_features, 0, weight_piece.shape[0], axis=1)
    projected = empty + jnp.dot(features, weight_piece, preferred_element_type=jnp.float32)
    return projected.astype(jnp.bfloat16)


def solution(mesh):
    in_specs = (
        P(("rep", "seq"), "head"),
        P(("rep", "seq"), "head"),
        P(("rep", "seq"), "head"),
        P("seq", "head"),
        P("rep", None),
        P(("rep", "seq")),
    )
    out_specs = P(("rep", "seq"), "head")
    return jax.shard_map(
        on_device, mesh=mesh, in_specs=in_specs, out_specs=out_specs, check_vma=False
    )
```

profile of v0, /device:TPU:0, one launch (start us, length us, event | category | flops | bytes accessed | tf_op | source)
XLA Modules:
  0.0 208.0 jit_solution(14518805611755408136)
XLA Ops:
  6.5 0.0 copy-start.2
  6.5 0.0 copy-start.3
  6.5 0.0 all-gather.3.cloned.1.call-start
  6.5 5.0 %collective-permute-start = (s32[384]{0:T(512)}, s32[384]{0:T(512)S(1)}, u32[]{:S(2)}, u32[]{:S(2)}) collective-permute-start(s32[384]{0:T(512)} %param.12), channel_id=1, source_target_pairs={{0,4},{4,8},{8,12},{1,5},{5,9},{9,13},{2,6},{6,10},{10,14},{3,7},{... | collective-permute-start | bytes 4616 | tf_op jit(solution)/shard_map/ppermute | solution.py:16
  11.6 1.3 collective-permute-start.1
  12.9 4.6 %collective-permute-start.2 = (bf16[384,640]{1,0:T(8,128)(2,1)}, bf16[384,640]{1,0:T(8,128)(2,1)S(1)}, u32[]{:S(2)}, u32[]{:S(2)}) collective-permute-start(bf16[384,640]{1,0:T(8,128)(2,1)} %param.8), channel_id=1, source_target_pairs={{0,4},{4,8},{8,12},{1,5},{5,9},{9,13},{2,6},{6,10},{10,14},{3,7},{... | collective-permute-start | bytes 1474568 | tf_op jit(solution)/shard_map/ppermute | solution.py:16
  17.5 1.3 collective-permute-start.3
  18.8 4.6 %collective-permute-start.4 = (bf16[384,640]{1,0:T(8,128)(2,1)}, bf16[384,640]{1,0:T(8,128)(2,1)S(1)}, u32[]{:S(2)}, u32[]{:S(2)}) collective-permute-start(bf16[384,640]{1,0:T(8,128)(2,1)} %param.9), channel_id=1, source_target_pairs={{0,4},{4,8},{8,12},{1,5},{5,9},{9,13},{2,6},{6,10},{10,14},{3,7},{... | collective-permute-start | bytes 1474568 | tf_op jit(solution)/shard_map/ppermute | solution.py:16
  23.4 0.7 compare_bitcast_fusion
  24.1 0.7 fusion.35
  24.8 0.7 broadcast_add_fusion
  25.4 0.2 and_reduce_fusion
  25.6 0.7 stack.36
  26.3 0.1 broadcast_in_dim.32
  26.4 0.0 collective-permute-done
  26.4 1.3 collective-permute-start.5
  27.7 0.0 collective-permute-done.1
  27.8 1.7 collective-permute-done.2
  29.4 4.3 %collective-permute-done.3 = bf16[384,640]{1,0:T(8,128)(2,1)S(1)} collective-permute-done((bf16[384,640]{1,0:T(8,128)(2,1)}, bf16[384,640]{1,0:T(8,128)(2,1)S(1)}, u32[]{:S(2)}, u32[]{:S(2)}) %collective-permute-start.3) | collective-permute-done | bytes 491552 | tf_op jit(solution)/shard_map/ppermute | solution.py:16
  33.8 1.2 pad_maximum_fusion
  35.0 0.0 copy-done.2
  35.0 0.0 copy-done.3
  35.0 0.6 fusion.41
  35.6 0.6 fusion.42
  36.3 0.6 fusion.43
  36.9 0.6 fusion.44
  37.5 0.0 copy-start
  37.5 0.6 fusion.45
  38.2 0.1 collective-permute-done.4
  38.2 4.0 %collective-permute-done.5 = bf16[384,640]{1,0:T(8,128)(2,1)S(1)} collective-permute-done((bf16[384,640]{1,0:T(8,128)(2,1)}, bf16[384,640]{1,0:T(8,128)(2,1)S(1)}, u32[]{:S(2)}, u32[]{:S(2)}) %collective-permute-start.5) | collective-permute-done | bytes 491552 | tf_op jit(solution)/shard_map/ppermute | solution.py:16
  42.2 0.0 copy-done
  42.3 0.2 pad_maximum_fusion.1
  42.4 2.3 %fusion.14 = (f32[384]{0:T(512)S(1)}, f32[384]{0:T(512)S(1)}, f32[384]{0:T(512)S(1)}, f32[384]{0:T(512)S(1)}, f32[384]{0:T(512)S(1)}) fusion(f32[384,1152]{0,1:T(8,128)S(1)} %get-tuple-element.11, f32[384]{0:T(512)S(1)} %get-tuple-element.10, s32[384]{0:T(512)S(1)} %copy-done.2, s32[1152]{0:T(1024)S(1)} %eq.35, pred[1152]{0:T(1024)(128)(4,1)S(1)} %and.24, ...), kind=kLoop, calls=%fused_computation.33 | loop fusion | flops 7518336 | bytes 8870016 | tf_op jit(solution)/shard_map/reduce_sum | solution.py:26
  44.7 1.0 fusion.15
  45.7 1.0 fusion.16
  46.8 1.0 fusion.17
  47.8 1.0 fusion.18
  48.8 1.0 fusion.19
  49.8 0.0 copy-start.1
  49.8 0.8 copy-done.1
  50.6 0.0 all-gather.3.cloned.1.call-update
  50.6 0.0 all-gather.5.cloned.1.call-start
  50.7 0.7 all-gather.5.cloned.1.call-update
  51.4 21.5 %all-gather.3.cloned.1.call-done = bf16[384,2560]{1,0:T(8,128)(2,1)} async-done(((bf16[384,640]{1,0:T(8,128)(2,1)}), bf16[384,2560]{1,0:T(8,128)(2,1)}) %all-gather.3.cloned.1.call-update) | async-done | bytes 1966096 | tf_op jit(solution)/shard_map/all_gather | solution.py:83
  72.8 121.2 %all-gather.5.cloned.1.call-done = bf16[2560,1280]{1,0:T(8,128)(2,1)} async-done(((bf16[640,1280]{1,0:T(8,128)(2,1)}), bf16[2560,1280]{1,0:T(8,128)(2,1)}) %all-gather.5.cloned.1.call-update) | async-done | bytes 6553616 | tf_op jit(solution)/shard_map/all_gather | solution.py:85
  194.1 7.1 %convolution_convert_fusion = bf16[384,1280]{1,0:T(8,128)(2,1)} fusion(bf16[384,2560]{1,0:T(8,128)(2,1)} %all-gather.3.cloned.1.call-done, bf16[2560,1280]{1,0:T(8,128)(2,1)} %all-gather.5.cloned.1.call-done), kind=kOutput, calls=%fused_computation.15 | convolution fusion | flops 2517073920 | bytes 9502720 | tf_op jit(solution)/shard_map/dot_general | solution.py:87
  (5 shorter events, 0.0 us)
Async XLA Ops:
  6.5 28.4 %copy-start.2 = (s32[384]{0:T(512)S(1)}, s32[384]{0:T(512)}, u32[]{:S(2)}) copy-start(s32[384]{0:T(512)} %param.12) | copy-start | bytes 4612
  6.5 28.5 %copy-start.3 = (bf16[384,640]{1,0:T(8,128)(2,1)S(1)}, bf16[384,640]{1,0:T(8,128)(2,1)}, u32[]{:S(2)}) copy-start(bf16[384,640]{1,0:T(8,128)(2,1)} %param.7) | copy-start | bytes 1474564
  6.5 66.3 %all-gather.3.cloned.1.call-start = ((), (), s32[]{:S(2)}) async-start(), calls=%async_computation | async-start | bytes 2457600 | tf_op jit(solution)/shard_map/all_gather | solution.py:83
  6.5 19.8 %collective-permute-start = (s32[384]{0:T(512)}, s32[384]{0:T(512)S(1)}, u32[]{:S(2)}, u32[]{:S(2)}) collective-permute-start(s32[384]{0:T(512)} %param.12), channel_id=1, source_target_pairs={{0,4},{4,8},{8,12},{1,5},{5,9},{9,13},{2,6},{6,10},{10,14},{3,7},{... | collective-permute-start | bytes 4616 | tf_op jit(solution)/shard_map/ppermute | solution.py:16
  11.6 16.1 %collective-permute-start.1 = (s32[384]{0:T(512)}, s32[384]{0:T(512)S(1)}, u32[]{:S(2)}, u32[]{:S(2)}) collective-permute-start(s32[384]{0:T(512)} %param.12), channel_id=1, source_target_pairs={{4,0},{8,4},{12,8},{5,1},{9,5},{13,9},{6,2},{10,6},{14,10},{7,3},{... | collective-permute-start | bytes 4616 | tf_op jit(solution)/shard_map/ppermute | solution.py:16
  12.9 16.5 %collective-permute-start.2 = (bf16[384,640]{1,0:T(8,128)(2,1)}, bf16[384,640]{1,0:T(8,128)(2,1)S(1)}, u32[]{:S(2)}, u32[]{:S(2)}) collective-permute-start(bf16[384,640]{1,0:T(8,128)(2,1)} %param.8), channel_id=1, source_target_pairs={{0,4},{4,8},{8,12},{1,5},{5,9},{9,13},{2,6},{6,10},{10,14},{3,7},{... | collective-permute-start | bytes 1474568 | tf_op jit(solution)/shard_map/ppermute | solution.py:16
  17.5 16.3 %collective-permute-start.3 = (bf16[384,640]{1,0:T(8,128)(2,1)}, bf16[384,640]{1,0:T(8,128)(2,1)S(1)}, u32[]{:S(2)}, u32[]{:S(2)}) collective-permute-start(bf16[384,640]{1,0:T(8,128)(2,1)} %param.8), channel_id=1, source_target_pairs={{4,0},{8,4},{12,8},{5,1},{9,5},{13,9},{6,2},{10,6},{14,10},{7,3},{... | collective-permute-start | bytes 1474568 | tf_op jit(solution)/shard_map/ppermute | solution.py:16
  18.8 19.4 %collective-permute-start.4 = (bf16[384,640]{1,0:T(8,128)(2,1)}, bf16[384,640]{1,0:T(8,128)(2,1)S(1)}, u32[]{:S(2)}, u32[]{:S(2)}) collective-permute-start(bf16[384,640]{1,0:T(8,128)(2,1)} %param.9), channel_id=1, source_target_pairs={{0,4},{4,8},{8,12},{1,5},{5,9},{9,13},{2,6},{6,10},{10,14},{3,7},{... | collective-permute-start | bytes 1474568 | tf_op jit(solution)/shard_map/ppermute | solution.py:16
  26.4 15.9 %collective-permute-start.5 = (bf16[384,640]{1,0:T(8,128)(2,1)}, bf16[384,640]{1,0:T(8,128)(2,1)S(1)}, u32[]{:S(2)}, u32[]{:S(2)}) collective-permute-start(bf16[384,640]{1,0:T(8,128)(2,1)} %param.9), channel_id=1, source_target_pairs={{4,0},{8,4},{12,8},{5,1},{9,5},{13,9},{6,2},{10,6},{14,10},{7,3},{... | collective-permute-start | bytes 1474568 | tf_op jit(solution)/shard_map/ppermute | solution.py:16
  37.5 4.7 %copy-start = (bf16[384,640]{1,0:T(8,128)(2,1)S(1)}, bf16[384,640]{1,0:T(8,128)(2,1)}, u32[]{:S(2)}) copy-start(bf16[384,640]{1,0:T(8,128)(2,1)} %param.9) | copy-start | bytes 1474564
  49.8 0.8 copy-start.1
  50.6 143.4 %all-gather.5.cloned.1.call-start = ((), (), s32[]{:S(2)}) async-start(), calls=%async_computation.1 | async-start | bytes 8192000 | tf_op jit(solution)/shard_map/all_gather | solution.py:85
Sparse Core Ops, SparseCore 0:
  50.7 22.0 all-gather.2
  74.4 119.6 all-gather.4
where the time goes:
time: 208 us
  waiting for transfers between devices  154 us (74%)
  starting transfers between devices  18.1 us (9%)
  matrix products  15.3 us (7%)
  between operations  13.6 us (7%)
  other arithmetic  5.25 us (3%)
  local copies, waits for them, and re-layouts  2.27 us (1%)
    all_gather x1, waiting for transfers between devices, on_device(): weight_piece = lax.all_gather(out_weight, 'seq', axis=0, tiled=True)  121 us
    all_gather x1, waiting for transfers between devices, on_device(): all_features = lax.all_gather(attended, 'head', axis=1, tiled=True)  21.5 us
    ppermute x6, starting transfers between devices, from_behind(): return lax.ppermute(value, axis, pairs)  18.1 us
    ppermute x6, waiting for transfers between devices, from_behind(): return lax.ppermute(value, axis, pairs)  10.1 us
    dot_general x1, matrix products, on_device(): jnp.dot(features, weight_piece, preferred_element_type=jnp.float32)  7.1 us
    dot_general x5, matrix products, attend_head(): jnp.dot(weights, value_head, preferred_element_type=jnp.float32)  5.04 us
  transfers between devices with their start and end apart: 8, of which 6 were waited for; matrix products, arithmetic and copies ran while one was open for 4% of the time, Pallas kernels for 0%

commit v1 on v0

--- a/solution.py
+++ b/solution.py
@@ -39,6 +39,7 @@
             for col_step in (-1, 0, 1):
                 every_offset.add(layer_step * layer_tiles + row_step * TGW + col_step)
     distances = [offset for offset in sorted(every_offset) if 0 < offset < seq_count]
+    weight_piece = lax.all_gather(out_weight, "seq", axis=0, tiled=True)
     key_list = [keys]
     value_list = [values]
     clip_list = [clip_ids]
@@ -80,11 +81,18 @@
             )
         )
     attended = jnp.concatenate(head_outputs, axis=1)
-    all_features = lax.all_gather(attended, "head", axis=1, tiled=True)
-    empty = jnp.zeros((tile_rows, out_weight.shape[1]), jnp.float32)
-    weight_piece = lax.all_gather(out_weight, "seq", axis=0, tiled=True)
-    features = lax.slice_in_dim(all_features, 0, weight_piece.shape[0], axis=1)
-    projected = empty + jnp.dot(features, weight_piece, preferred_element_type=jnp.float32)
+    head_count = lax.axis_size("head")
+    head_position = lax.axis_index("head")
+    projected = jnp.zeros((tile_rows, weight_piece.shape[1]), jnp.float32)
+    for shift in range(head_count):
+        if shift == 0:
+            piece = attended
+        else:
+            pairs = [(j, (j + shift) % head_count) for j in range(head_count)]
+            piece = lax.ppermute(attended, "head", pairs)
+        block = (head_position - shift) % head_count
+        rows = lax.dynamic_slice_in_dim(weight_piece, block * feature_width, feature_width, axis=0)
+        projected = projected + jnp.dot(piece, rows, preferred_element_type=jnp.float32)
     return projected.astype(jnp.bfloat16)
 
 

time: 208 us -> 160 us (0.77)
  waiting for transfers between devices: 154 us -> 104 us
    all_gather x1, waiting for transfers between devices: 121 us -> 63.2 us  [on_device(): weight_piece = lax.all_gather(out_weight, 'seq', axis=0, tiled=True)]
    ppermute x6, waiting for transfers between devices: 10.1 us -> 39.6 us  [from_behind(): return lax.ppermute(value, axis, pairs)]
    all_gather x1 -> x0, waiting for transfers between devices: 21.5 us -> none  [on_device(): all_features = lax.all_gather(attended, 'head', axis=1, tiled=True)]
    dot_general x1 -> x4, matrix products: 7.1 us -> 7.91 us  [on_device(): jnp.dot(piece, rows, preferred_element_type=jnp.float32)]
  transfers between devices with their start and end apart: 8 -> 10, of which waited for: 6 -> 3; matrix products, arithmetic and copies ran while one was open for 4% -> 12% of each run, Pallas kernels for 0% -> 0%
where the time goes in v1:
time: 160 us
  waiting for transfers between devices  104 us (65%)
  starting transfers between devices  20.1 us (13%)
  matrix products  15.7 us (10%)
  between operations  13.7 us (9%)
  other arithmetic  4.2 us (3%)
  local copies, waits for them, and re-layouts  2.29 us (1%)
    all_gather x1, waiting for transfers between devices, on_device(): weight_piece = lax.all_gather(out_weight, 'seq', axis=0, tiled=True)  63.2 us
    ppermute x6, waiting for transfers between devices, from_behind(): return lax.ppermute(value, axis, pairs)  39.6 us
    ppermute x6, starting transfers between devices, from_behind(): return lax.ppermute(value, axis, pairs)  18.1 us
    dot_general x4, matrix products, on_device(): jnp.dot(piece, rows, preferred_element_type=jnp.float32)  7.91 us
    dot_general x5, matrix products, attend_head(): jnp.dot(weights, value_head, preferred_element_type=jnp.float32)  4.61 us
  transfers between devices with their start and end apart: 10, of which 3 were waited for; matrix products, arithmetic and copies ran while one was open for 12% of the time, Pallas kernels for 0%

profile of v1, /device:TPU:0, one launch (start us, length us, event | category | flops | bytes accessed | tf_op | source)
XLA Modules:
  0.0 159.5 jit_solution(2540641170040627313)
XLA Ops:
  6.5 0.0 all-gather.2.cloned.1.call-start
  6.5 0.7 all-gather.2.cloned.1.call-update
  7.3 5.1 %collective-permute-start.2 = (bf16[384,640]{1,0:T(8,128)(2,1)}, bf16[384,640]{1,0:T(8,128)(2,1)S(1)}, u32[]{:S(2)}, u32[]{:S(2)}) collective-permute-start(bf16[384,640]{1,0:T(8,128)(2,1)} %param.8), channel_id=1, source_target_pairs={{0,4},{4,8},{8,12},{1,5},{5,9},{9,13},{2,6},{6,10},{10,14},{3,7},{... | collective-permute-start | bytes 1474568 | tf_op jit(solution)/shard_map/ppermute | solution.py:16
  12.4 1.3 collective-permute-start.3
  13.7 4.6 %collective-permute-start.4 = (bf16[384,640]{1,0:T(8,128)(2,1)}, bf16[384,640]{1,0:T(8,128)(2,1)S(1)}, u32[]{:S(2)}, u32[]{:S(2)}) collective-permute-start(bf16[384,640]{1,0:T(8,128)(2,1)} %param.9), channel_id=1, source_target_pairs={{0,4},{4,8},{8,12},{1,5},{5,9},{9,13},{2,6},{6,10},{10,14},{3,7},{... | collective-permute-start | bytes 1474568 | tf_op jit(solution)/shard_map/ppermute | solution.py:16
  18.2 1.3 collective-permute-start.5
  19.5 4.5 %collective-permute-start = (s32[384]{0:T(512)}, s32[384]{0:T(512)S(1)}, u32[]{:S(2)}, u32[]{:S(2)}) collective-permute-start(s32[384]{0:T(512)} %param.12), channel_id=1, source_target_pairs={{0,4},{4,8},{8,12},{1,5},{5,9},{9,13},{2,6},{6,10},{10,14},{3,7},{... | collective-permute-start | bytes 4616 | tf_op jit(solution)/shard_map/ppermute | solution.py:16
  24.1 0.7 broadcast_add_fusion
  24.8 0.7 compare_bitcast_fusion
  25.5 0.7 fusion.47
  26.1 21.0 %collective-permute-done = s32[384]{0:T(512)S(1)} collective-permute-done((s32[384]{0:T(512)}, s32[384]{0:T(512)S(1)}, u32[]{:S(2)}, u32[]{:S(2)}) %collective-permute-start) | collective-permute-done | bytes 1568 | tf_op jit(solution)/shard_map/ppermute | solution.py:16
  47.1 1.3 collective-permute-start.1
  48.4 0.2 and_reduce_fusion
  48.6 0.7 stack.36
  49.3 0.1 broadcast_in_dim.32
  49.4 18.6 %collective-permute-done.1 = s32[384]{0:T(512)S(1)} collective-permute-done((s32[384]{0:T(512)}, s32[384]{0:T(512)S(1)}, u32[]{:S(2)}, u32[]{:S(2)}) %collective-permute-start.1) | collective-permute-done | bytes 1568 | tf_op jit(solution)/shard_map/ppermute | solution.py:16
  68.0 0.0 collective-permute-done.2
  68.0 0.0 collective-permute-done.3
  68.0 0.2 pad_maximum_fusion
  68.2 0.0 copy-start.3
  68.3 0.0 copy-start.4
  68.3 0.0 collective-permute-done.4
  68.3 0.0 collective-permute-done.5
  68.3 0.2 pad_maximum_fusion.1
  68.5 0.4 copy-done.3
  68.9 0.4 copy-done.4
  69.3 0.6 fusion.53
  69.9 0.6 fusion.54
  70.6 0.6 fusion.55
  71.2 0.6 fusion.56
  71.8 0.6 fusion.57
  72.5 2.3 %fusion.22 = (f32[384]{0:T(512)S(1)}, f32[384]{0:T(512)S(1)}, f32[384]{0:T(512)S(1)}, f32[384]{0:T(512)S(1)}, f32[384]{0:T(512)S(1)}) fusion(f32[384,1152]{0,1:T(8,128)S(1)} %get-tuple-element.11, f32[384]{0:T(512)S(1)} %get-tuple-element.10, s32[384]{0:T(512)S(1)} %copy-done.3, s32[1152]{0:T(1024)S(1)} %eq.40, pred[1152]{0:T(1024)(128)(4,1)S(1)} %and.42, ...), kind=kLoop, calls=%fused_computation.42 | loop fusion | flops 7518336 | bytes 8870016 | tf_op jit(solution)/shard_map/reduce_sum | solution.py:26
  74.7 0.9 fusion.23
  75.7 0.9 fusion.24
  76.6 0.9 fusion.25
  77.5 0.9 fusion.26
  78.4 0.9 fusion.27
  79.4 0.1 collective-permute-start.8
  79.5 0.4 collective-permute-start.6
  79.9 1.5 collective-permute-start.7
  81.5 63.2 %all-gather.2.cloned.1.call-done = bf16[2560,1280]{1,0:T(8,128)(2,1)} async-done(((bf16[640,1280]{1,0:T(8,128)(2,1)}), bf16[2560,1280]{1,0:T(8,128)(2,1)}) %all-gather.2.cloned.1.call-update) | async-done | bytes 6553616 | tf_op jit(solution)/shard_map/all_gather | solution.py:42
  144.7 2.5 %fusion.16 = f32[384,1280]{1,0:T(8,128)S(1)} fusion(bf16[384,640]{0,1:T(8,128)(2,1)S(1)} %fusion.27, bf16[2560,1280]{1,0:T(8,128)(2,1)} %all-gather.2.cloned.1.call-done, s32[]{:T(128)S(6)} %select_n.78), kind=kOutput, calls=%fused_computation.34 | convolution fusion | flops 629145600 | bytes 4096004 | tf_op jit(solution)/shard_map/dot_general | solution.py:95
  147.2 0.0 collective-permute-done.8
  147.3 2.4 %fusion.12 = f32[384,1280]{1,0:T(8,128)S(1)} fusion(bf16[384,640]{0,1:T(8,128)(2,1)S(1)} %collective-permute-done.8, bf16[2560,1280]{1,0:T(8,128)(2,1)} %all-gather.2.cloned.1.call-done, s32[]{:T(128)S(6)} %select_n.84), kind=kOutput, calls=%fused_computation.30 | convolution fusion | flops 629145600 | bytes 4096004 | tf_op jit(solution)/shard_map/dot_general | solution.py:95
  149.7 0.0 collective-permute-done.6
  149.7 1.0 convolution_add_fusion.1
  150.7 0.0 collective-permute-done.7
  150.7 2.0 %fusion.11 = bf16[384,1280]{1,0:T(8,128)(2,1)} fusion(f32[384,1280]{1,0:T(8,128)S(1)} %fusion.12, f32[384,1280]{1,0:T(8,128)S(1)} %convolution_add_fusion.1, bf16[384,640]{0,1:T(8,128)(2,1)S(1)} %collective-permute-done.7, bf16[2560,1280]{1,0:T(8,128)(2,1)S(1)} %copy-done, s32[]{:T(128)S(6)} %select_n.82), kind=kOutput, calls=%fused_computation.18 | convolution fusion | flops 630620160 | bytes 7045124 | tf_op jit(solution)/shard_map/dot_general | solution.py:95
  (11 shorter events, 0.1 us)
Async XLA Ops:
  6.5 61.5 %copy-start.1 = (bf16[384,640]{1,0:T(8,128)(2,1)S(1)}, bf16[384,640]{1,0:T(8,128)(2,1)}, u32[]{:S(2)}) copy-start(bf16[384,640]{1,0:T(8,128)(2,1)} %param.8) | copy-start | bytes 1474564
  6.5 138.2 %all-gather.2.cloned.1.call-start = ((), (), s32[]{:S(2)}) async-start(), calls=%async_computation | async-start | bytes 8192000 | tf_op jit(solution)/shard_map/all_gather | solution.py:42
  7.3 61.0 %copy-start.2 = (bf16[384,640]{1,0:T(8,128)(2,1)S(1)}, bf16[384,640]{1,0:T(8,128)(2,1)}, u32[]{:S(2)}) copy-start(bf16[384,640]{1,0:T(8,128)(2,1)} %param.9) | copy-start | bytes 1474564
  7.3 60.8 %collective-permute-start.2 = (bf16[384,640]{1,0:T(8,128)(2,1)}, bf16[384,640]{1,0:T(8,128)(2,1)S(1)}, u32[]{:S(2)}, u32[]{:S(2)}) collective-permute-start(bf16[384,640]{1,0:T(8,128)(2,1)} %param.8), channel_id=1, source_target_pairs={{0,4},{4,8},{8,12},{1,5},{5,9},{9,13},{2,6},{6,10},{10,14},{3,7},{... | collective-permute-start | bytes 1474568 | tf_op jit(solution)/shard_map/ppermute | solution.py:16
  12.4 55.7 %collective-permute-start.3 = (bf16[384,640]{1,0:T(8,128)(2,1)}, bf16[384,640]{1,0:T(8,128)(2,1)S(1)}, u32[]{:S(2)}, u32[]{:S(2)}) collective-permute-start(bf16[384,640]{1,0:T(8,128)(2,1)} %param.8), channel_id=1, source_target_pairs={{4,0},{8,4},{12,8},{5,1},{9,5},{13,9},{6,2},{10,6},{14,10},{7,3},{... | collective-permute-start | bytes 1474568 | tf_op jit(solution)/shard_map/ppermute | solution.py:16
  13.7 54.6 %collective-permute-start.4 = (bf16[384,640]{1,0:T(8,128)(2,1)}, bf16[384,640]{1,0:T(8,128)(2,1)S(1)}, u32[]{:S(2)}, u32[]{:S(2)}) collective-permute-start(bf16[384,640]{1,0:T(8,128)(2,1)} %param.9), channel_id=1, source_target_pairs={{0,4},{4,8},{8,12},{1,5},{5,9},{9,13},{2,6},{6,10},{10,14},{3,7},{... | collective-permute-start | bytes 1474568 | tf_op jit(solution)/shard_map/ppermute | solution.py:16
  18.2 50.0 %collective-permute-start.5 = (bf16[384,640]{1,0:T(8,128)(2,1)}, bf16[384,640]{1,0:T(8,128)(2,1)S(1)}, u32[]{:S(2)}, u32[]{:S(2)}) collective-permute-start(bf16[384,640]{1,0:T(8,128)(2,1)} %param.9), channel_id=1, source_target_pairs={{4,0},{8,4},{12,8},{5,1},{9,5},{13,9},{6,2},{10,6},{14,10},{7,3},{... | collective-permute-start | bytes 1474568 | tf_op jit(solution)/shard_map/ppermute | solution.py:16
  19.5 27.6 %collective-permute-start = (s32[384]{0:T(512)}, s32[384]{0:T(512)S(1)}, u32[]{:S(2)}, u32[]{:S(2)}) collective-permute-start(s32[384]{0:T(512)} %param.12), channel_id=1, source_target_pairs={{0,4},{4,8},{8,12},{1,5},{5,9},{9,13},{2,6},{6,10},{10,14},{3,7},{... | collective-permute-start | bytes 4616 | tf_op jit(solution)/shard_map/ppermute | solution.py:16
  47.1 20.9 %collective-permute-start.1 = (s32[384]{0:T(512)}, s32[384]{0:T(512)S(1)}, u32[]{:S(2)}, u32[]{:S(2)}) collective-permute-start(s32[384]{0:T(512)} %param.12), channel_id=1, source_target_pairs={{4,0},{8,4},{12,8},{5,1},{9,5},{13,9},{6,2},{10,6},{14,10},{7,3},{... | collective-permute-start | bytes 4616 | tf_op jit(solution)/shard_map/ppermute | solution.py:16
  68.2 0.7 copy-start.3
  68.3 1.0 copy-start.4
  79.4 67.9 %collective-permute-start.8 = (bf16[384,640]{0,1:T(8,128)(2,1)S(1)}, bf16[384,640]{0,1:T(8,128)(2,1)S(1)}, u32[]{:S(2)}, u32[]{:S(2)}) collective-permute-start(bf16[384,640]{0,1:T(8,128)(2,1)S(1)} %fusion.27), channel_id=1, source_target_pairs={{0,3},{1,0},{2,1},{3,2},{4,7},{5,4},{6,5},{7,6},{8,11},{9,8},{10,9... | collective-permute-start | bytes 1474568 | tf_op jit(solution)/shard_map/ppermute | solution.py:92
  79.5 70.1 %collective-permute-start.6 = (bf16[384,640]{0,1:T(8,128)(2,1)S(1)}, bf16[384,640]{0,1:T(8,128)(2,1)S(1)}, u32[]{:S(2)}, u32[]{:S(2)}) collective-permute-start(bf16[384,640]{0,1:T(8,128)(2,1)S(1)} %fusion.27), channel_id=1, source_target_pairs={{0,1},{1,2},{2,3},{3,0},{4,5},{5,6},{6,7},{7,4},{8,9},{9,10},{10,1... | collective-permute-start | bytes 1474568 | tf_op jit(solution)/shard_map/ppermute | solution.py:92
  79.9 70.8 %collective-permute-start.7 = (bf16[384,640]{0,1:T(8,128)(2,1)S(1)}, bf16[384,640]{0,1:T(8,128)(2,1)S(1)}, u32[]{:S(2)}, u32[]{:S(2)}) collective-permute-start(bf16[384,640]{0,1:T(8,128)(2,1)S(1)} %fusion.27), channel_id=1, source_target_pairs={{0,2},{1,3},{2,0},{3,1},{4,6},{5,7},{6,4},{7,5},{8,10},{9,11},{10,... | collective-permute-start | bytes 1474568 | tf_op jit(solution)/shard_map/ppermute | solution.py:92
  144.7 5.0 %copy-start = (bf16[2560,1280]{1,0:T(8,128)(2,1)S(1)}, bf16[2560,1280]{1,0:T(8,128)(2,1)}, u32[]{:S(2)}) copy-start(bf16[2560,1280]{1,0:T(8,128)(2,1)} %all-gather.2.cloned.1.call-done) | copy-start | bytes 19660804
Sparse Core Ops, SparseCore 0:
  8.9 135.7 all-gather.1

commit v2 on v0

--- a/solution.py
+++ b/solution.py
@@ -14,6 +14,20 @@
     peers = lax.axis_size(axis)
     pairs = [(i, i + by) for i in range(peers) if 0 <= i + by < peers]
     return lax.ppermute(value, axis, pairs)
+
+
+def chunk_bounds(width, lanes=128, widths=(3, 2)):
+    units = width // lanes
+    bounds = []
+    first = 0
+    for part in widths:
+        last = min(units, first // lanes + part) * lanes
+        if last > first:
+            bounds.append((first, last))
+            first = last
+    if first < width:
+        bounds.append((first, width))
+    return bounds
 
 
 def attend_head(query_head, key_head, value_head, allowed):
@@ -39,6 +53,18 @@
             for col_step in (-1, 0, 1):
                 every_offset.add(layer_step * layer_tiles + row_step * TGW + col_step)
     distances = [offset for offset in sorted(every_offset) if 0 < offset < seq_count]
+    rep_count = lax.axis_size("rep")
+    rep_position = lax.axis_index("rep")
+    half_width = out_weight.shape[1] // rep_count
+    own_half = lax.dynamic_slice_in_dim(out_weight, rep_position * half_width, half_width, axis=1)
+    gathered = []
+    for first, last in chunk_bounds(half_width):
+        chunk = lax.all_gather(own_half[:, first:last], "seq", axis=0, tiled=True)
+        copies = [chunk]
+        for shift in range(1, rep_count):
+            pairs = [(j, (j + shift) % rep_count) for j in range(rep_count)]
+            copies.append(lax.ppermute(chunk, "rep", pairs))
+        gathered.append(copies)
     key_list = [keys]
     value_list = [values]
     clip_list = [clip_ids]
@@ -80,12 +106,23 @@
             )
         )
     attended = jnp.concatenate(head_outputs, axis=1)
-    all_features = lax.all_gather(attended, "head", axis=1, tiled=True)
-    empty = jnp.zeros((tile_rows, out_weight.shape[1]), jnp.float32)
-    weight_piece = lax.all_gather(out_weight, "seq", axis=0, tiled=True)
-    features = lax.slice_in_dim(all_features, 0, weight_piece.shape[0], axis=1)
-    projected = empty + jnp.dot(features, weight_piece, preferred_element_type=jnp.float32)
-    return projected.astype(jnp.bfloat16)
+    head_count = lax.axis_size("head")
+    head_position = lax.axis_index("head")
+    received = [attended]
+    for shift in range(1, head_count):
+        pairs = [(j, (j + shift) % head_count) for j in range(head_count)]
+        received.append(lax.ppermute(attended, "head", pairs))
+    features = jnp.roll(
+        jnp.concatenate(received[::-1], axis=1), (head_position + 1) * feature_width, axis=1
+    )
+    halves = []
+    for shift in range(rep_count):
+        pieces = [
+            jnp.dot(features, chunk[shift], preferred_element_type=jnp.float32).astype(jnp.bfloat16)
+            for chunk in gathered
+        ]
+        halves.append(jnp.concatenate(pieces, axis=1))
+    return jnp.roll(jnp.concatenate(halves[::-1], axis=1), (rep_position + 1) * half_width, axis=1)
 
 
 def solution(mesh):

time: 208 us -> 179 us (0.86)
  waiting for transfers between devices: 154 us -> 96.6 us
  local copies, waits for them, and re-layouts: 2.27 us -> 17.3 us
  matrix products: 15.3 us -> 22.4 us
  starting transfers between devices: 18.1 us -> 23.5 us
    all_gather x2, waiting for transfers between devices: 143 us -> 0.01 us  [on_device(): chunk = lax.all_gather(own_half[:, first:last], 'seq', axis=0, tiled=True)]
    ppermute x0 -> x5, waiting for transfers between devices: none -> 55.1 us  [the longest x2 35 us: on_device(): copies.append(lax.ppermute(chunk, 'rep', pairs))]
    ppermute x6, waiting for transfers between devices: 10.1 us -> 41.4 us  [from_behind(): return lax.ppermute(value, axis, pairs)]
    unnamed x8 -> x38, local copies, waits for them, and re-layouts: 0.79 us -> 13.4 us
    ppermute x0 -> x5, starting transfers between devices: none -> 4.66 us  [the longest x2 2.96 us: on_device(): copies.append(lax.ppermute(chunk, 'rep', pairs))]
    dot_general x1 -> x4, matrix products: 7.1 us -> 11.5 us  [on_device(): jnp.dot(features, chunk[shift], preferred_element_type=jnp.float32)]
    dot_general x5, matrix products: 5.04 us -> 7.81 us  [attend_head(): jnp.dot(weights, value_head, preferred_element_type=jnp.float32)]
  transfers between devices with their start and end apart: 8 -> 13, of which waited for: 6 -> 7; matrix products, arithmetic and copies ran while one was open for 4% -> 18% of each run, Pallas kernels for 0% -> 0%
where the time goes in v2:
time: 179 us
  waiting for transfers between devices  96.6 us (54%)
  starting transfers between devices  23.5 us (13%)
  matrix products  22.4 us (13%)
  local copies, waits for them, and re-layouts  17.3 us (10%)
  between operations  13.7 us (8%)
  other arithmetic  5.07 us (3%)
    ppermute x6, waiting for transfers between devices, from_behind(): return lax.ppermute(value, axis, pairs)  41.4 us
    ppermute x2, waiting for transfers between devices, on_device(): copies.append(lax.ppermute(chunk, 'rep', pairs))  35 us
    ppermute x3, waiting for transfers between devices, on_device(): received.append(lax.ppermute(attended, 'head', pairs))  20.2 us
    ppermute x6, starting transfers between devices, from_behind(): return lax.ppermute(value, axis, pairs)  18.7 us
    unnamed x38, local copies, waits for them, and re-layouts  13.4 us
    dot_general x4, matrix products, on_device(): jnp.dot(features, chunk[shift], preferred_element_type=jnp.float32)  11.5 us
    dot_general x5, matrix products, attend_head(): jnp.dot(weights, value_head, preferred_element_type=jnp.float32)  7.81 us
  transfers between devices with their start and end apart: 13, of which 7 were waited for; matrix products, arithmetic and copies ran while one was open for 18% of the time, Pallas kernels for 0%

profile of v2, /device:TPU:0, one launch (start us, length us, event | category | flops | bytes accessed | tf_op | source)
XLA Modules:
  0.0 178.6 jit_solution(2171050796810348212)
XLA Ops:
  6.6 1.5 copy-done
  8.1 0.8 constant_dynamic-slice_fusion
  9.0 4.9 %collective-permute-start = (s32[384]{0:T(512)}, s32[384]{0:T(512)S(1)}, u32[]{:S(2)}, u32[]{:S(2)}) collective-permute-start(s32[384]{0:T(512)} %param.12), channel_id=1, source_target_pairs={{0,4},{4,8},{8,12},{1,5},{5,9},{9,13},{2,6},{6,10},{10,14},{3,7},{... | collective-permute-start | bytes 4616 | tf_op jit(solution)/shard_map/ppermute | solution.py:16
  14.0 1.3 collective-permute-start.1
  15.3 5.3 %collective-permute-start.2 = (bf16[384,640]{1,0:T(8,128)(2,1)}, bf16[384,640]{1,0:T(8,128)(2,1)}, u32[]{:S(2)}, u32[]{:S(2)}) collective-permute-start(bf16[384,640]{1,0:T(8,128)(2,1)} %param.8), channel_id=1, source_target_pairs={{0,4},{4,8},{8,12},{1,5},{5,9},{9,13},{2,6},{6,10},{10,14},{3,7},{... | collective-permute-start | bytes 1474568 | tf_op jit(solution)/shard_map/ppermute | solution.py:16
  20.6 1.3 collective-permute-start.3
  21.9 4.6 %collective-permute-start.4 = (bf16[384,640]{1,0:T(8,128)(2,1)}, bf16[384,640]{1,0:T(8,128)(2,1)S(1)}, u32[]{:S(2)}, u32[]{:S(2)}) collective-permute-start(bf16[384,640]{1,0:T(8,128)(2,1)} %param.9), channel_id=1, source_target_pairs={{0,4},{4,8},{8,12},{1,5},{5,9},{9,13},{2,6},{6,10},{10,14},{3,7},{... | collective-permute-start | bytes 1474568 | tf_op jit(solution)/shard_map/ppermute | solution.py:16
  26.5 0.8 constant_dynamic-slice_fusion.2
  27.7 1.3 collective-permute-start.5
  29.0 12.8 %collective-permute-done.2 = bf16[384,640]{1,0:T(8,128)(2,1)} collective-permute-done((bf16[384,640]{1,0:T(8,128)(2,1)}, bf16[384,640]{1,0:T(8,128)(2,1)}, u32[]{:S(2)}, u32[]{:S(2)}) %collective-permute-start.2) | collective-permute-done | bytes 491552 | tf_op jit(solution)/shard_map/ppermute | solution.py:16
  41.9 17.5 %collective-permute-done.3 = bf16[384,640]{1,0:T(8,128)(2,1)} collective-permute-done((bf16[384,640]{1,0:T(8,128)(2,1)}, bf16[384,640]{1,0:T(8,128)(2,1)}, u32[]{:S(2)}, u32[]{:S(2)}) %collective-permute-start.3) | collective-permute-done | bytes 491552 | tf_op jit(solution)/shard_map/ppermute | solution.py:16
  59.4 1.4 pad_maximum_fusion
  61.4 0.6 fusion.61
  63.9 11.1 %collective-permute-done.5 = bf16[384,640]{1,0:T(8,128)(2,1)} collective-permute-done((bf16[384,640]{1,0:T(8,128)(2,1)S(1)}, bf16[384,640]{1,0:T(8,128)(2,1)}, u32[]{:S(2)}, u32[]{:S(2)}) %collective-permute-start.5) | collective-permute-done | bytes 491552 | tf_op jit(solution)/shard_map/ppermute | solution.py:16
  75.0 1.2 pad_maximum_fusion.1
  76.2 2.3 %fusion.22 = (f32[384]{0:T(512)S(1)}, f32[384]{0:T(512)S(1)}, f32[384]{0:T(512)S(1)}, f32[384]{0:T(512)S(1)}, f32[384]{0:T(512)S(1)}) fusion(f32[384,1152]{0,1:T(8,128)S(1)} %get-tuple-element.11, f32[384]{0:T(512)S(1)} %get-tuple-element.10, s32[384]{0:T(512)S(1)} %copy-done.4, s32[1152]{0:T(1024)S(1)} %eq.40, pred[1152]{0:T(1024)(128)(4,1)S(1)} %and.35, ...), kind=kLoop, calls=%fused_computation.40 | loop fusion | flops 7518336 | bytes 8870016 | tf_op jit(solution)/shard_map/reduce_sum | solution.py:40
  78.5 1.6 constant_dynamic-update-slice_fusion.4
  80.0 1.6 constant_dynamic-update-slice_fusion.3
  81.6 1.6 constant_dynamic-update-slice_fusion.2
  83.2 1.6 constant_dynamic-update-slice_fusion.1
  84.7 1.6 constant_dynamic-update-slice_fusion
  86.3 0.7 collective-permute-start.6
  87.0 0.8 collective-permute-start.7
  88.0 1.5 collective-permute-start.9
  89.5 9.1 %collective-permute-done.6 = bf16[384,640]{0,1:T(8,128)(2,1)S(1)} collective-permute-done((bf16[384,640]{0,1:T(8,128)(2,1)}, bf16[384,640]{0,1:T(8,128)(2,1)S(1)}, u32[]{:S(2)}, u32[]{:S(2)}) %collective-permute-start.6) | collective-permute-done | bytes 491552 | tf_op jit(solution)/shard_map/ppermute | solution.py:114
  98.6 0.8 constant_dynamic-update-slice_fusion.20
  99.4 11.1 %collective-permute-done.7 = bf16[384,640]{0,1:T(8,128)(2,1)S(1)} collective-permute-done((bf16[384,640]{0,1:T(8,128)(2,1)}, bf16[384,640]{0,1:T(8,128)(2,1)S(1)}, u32[]{:S(2)}, u32[]{:S(2)}) %collective-permute-start.7) | collective-permute-done | bytes 491552 | tf_op jit(solution)/shard_map/ppermute | solution.py:114
  110.5 0.8 constant_dynamic-update-slice_fusion.19
  111.3 0.8 constant_dynamic-update-slice_fusion.18
  112.2 0.6 constant_dynamic-update-slice_fusion.17
  112.8 0.6 constant_dynamic-update-slice_fusion.16
  114.1 0.6 constant_dynamic-update-slice_fusion.14
  114.7 1.5 collective-permute-start.10
  116.2 1.5 constant_dynamic-update-slice_fusion.13
  117.8 0.8 constant_dynamic-update-slice_fusion.12
  118.6 0.8 constant_dynamic-update-slice_fusion.11
  119.4 0.8 constant_dynamic-update-slice_fusion.10
  120.3 0.6 constant_dynamic-update-slice_fusion.9
  121.6 0.6 constant_dynamic-update-slice_fusion.7
  122.2 0.6 constant_dynamic-update-slice_fusion.6
  122.8 0.6 constant_dynamic-update-slice_fusion.5
  123.5 10.4 %collective-permute-done.9 = bf16[2560,384]{1,0:T(8,128)(2,1)} collective-permute-done((bf16[2560,384]{1,0:T(8,128)(2,1)}, bf16[2560,384]{1,0:T(8,128)(2,1)}, u32[]{:S(2)}, u32[]{:S(2)}) %collective-permute-start.9) | collective-permute-done | bytes 1966112 | tf_op jit(solution)/shard_map/ppermute | solution.py:66
  133.9 3.4 %constant_dynamic-update-slice_fusion.28 = (bf16[384,2560]{0,1:T(8,128)(2,1)S(1)}, bf16[384,384]{0,1:T(8,128)(2,1)S(1)}) fusion(bf16[2560,384]{1,0:T(8,128)(2,1)} %collective-permute-done.9, bf16[384,5120]{0,1:T(8,128)(2,1)} %constant_dynamic-update-slice_fusion.5, s32[]{:T(128)S(6)} %select_n.73), kind=kOutput, calls=%fused_computation.93 | convolution fusion | flops 755122176 | bytes 4521988 | tf_op jit(solution)/shard_map/dot_general | solution.py:121
  137.3 24.6 %collective-permute-done.10 = bf16[2560,256]{1,0:T(8,128)(2,1)S(1)} collective-permute-done((bf16[2560,256]{1,0:T(8,128)(2,1)}, bf16[2560,256]{1,0:T(8,128)(2,1)S(1)}, u32[]{:S(2)}, u32[]{:S(2)}) %collective-permute-start.10) | collective-permute-done | bytes 1310752 | tf_op jit(solution)/shard_map/ppermute | solution.py:66
  161.8 2.6 %constant_dynamic-update-slice_fusion.27 = (bf16[384,2560]{0,1:T(8,128)(2,1)S(1)}, bf16[384,256]{0,1:T(8,128)(2,1)S(1)}) fusion(bf16[384,2560]{0,1:T(8,128)(2,1)S(1)} %get-tuple-element.30, bf16[2560,256]{1,0:T(8,128)(2,1)S(1)} %collective-permute-done.10, bf16[384,5120]{0,1:T(8,128)(2,1)} %constant_dynamic-update-slice_fusion.5, s32[]{:T(128)S(6)} %select_n.73), kind=kOutput, calls=%fused_computation.92 | convolution fusion | flops 503414784 | bytes 3670020 | tf_op jit(solution)/shard_map/dot_general | solution.py:121
  164.5 3.0 %constant_dynamic-update-slice_fusion.26 = (bf16[384,2560]{0,1:T(8,128)(2,1)S(1)}, bf16[384,384]{0,1:T(8,128)(2,1)S(1)}) fusion(bf16[384,2560]{0,1:T(8,128)(2,1)S(1)} %get-tuple-element.32, bf16[2560,384]{1,0:T(8,128)(2,1)S(1)} %copy-done.5, bf16[384,5120]{0,1:T(8,128)(2,1)} %constant_dynamic-update-slice_fusion.5, s32[]{:T(128)S(6)} %select_n.73), kind=kOutput, calls=%fused_computation.91 | convolution fusion | flops 755122176 | bytes 4521988 | tf_op jit(solution)/shard_map/dot_general | solution.py:121
  167.5 2.5 %constant_dynamic-update-slice_fusion.25 = (bf16[384,2560]{0,1:T(8,128)(2,1)S(1)}, bf16[384,256]{0,1:T(8,128)(2,1)S(1)}) fusion(bf16[384,2560]{0,1:T(8,128)(2,1)S(1)} %get-tuple-element.34, bf16[2560,256]{1,0:T(8,128)(2,1)S(1)} %copy-done.6, bf16[384,5120]{0,1:T(8,128)(2,1)} %constant_dynamic-update-slice_fusion.5, s32[]{:T(128)S(6)} %select_n.73), kind=kOutput, calls=%fused_computation.90 | convolution fusion | flops 503414784 | bytes 3670020 | tf_op jit(solution)/shard_map/dot_general | solution.py:121
  170.4 1.3 copy.9
  (52 shorter events, 4.9 us)
Async XLA Ops:
  6.5 1.6 copy-start
  6.5 20.8 %copy-start.9 = (s32[3]{0:T(128)S(1)}, s32[3]{0:T(128)}, u32[]{:S(2)}) copy-start(s32[3]{0:T(128)} %constant.73) | copy-start | bytes 40
  6.5 21.0 %copy-start.4 = (s32[384]{0:T(512)S(1)}, s32[384]{0:T(512)}, u32[]{:S(2)}) copy-start(s32[384]{0:T(512)} %param.12) | copy-start | bytes 4612
  6.5 52.8 %copy-start.1 = (bf16[384,640]{1,0:T(8,128)(2,1)S(1)}, bf16[384,640]{1,0:T(8,128)(2,1)}, u32[]{:S(2)}) copy-start(bf16[384,640]{1,0:T(8,128)(2,1)} %param.8) | copy-start | bytes 1474564
  6.5 21.1 %copy-start.2 = (bf16[384,640]{1,0:T(8,128)(2,1)S(1)}, bf16[384,640]{1,0:T(8,128)(2,1)}, u32[]{:S(2)}) copy-start(bf16[384,640]{1,0:T(8,128)(2,1)} %param.9) | copy-start | bytes 1474564
  6.6 20.7 %copy-start.8 = (s32[4,27]{1,0:T(4,128)S(1)}, s32[4,27]{1,0:T(4,128)}, u32[]{:S(2)}) copy-start(s32[4,27]{1,0:T(4,128)} %param.11) | copy-start | bytes 1300
  6.6 81.4 %all-gather.3.cloned.1.call-start = ((), (), s32[]{:S(2)}) async-start(), calls=%async_computation | async-start | bytes 2457600 | tf_op jit(solution)/shard_map/all_gather | solution.py:62
  9.0 105.8 %all-gather.5.cloned.1.call-start = ((), (), s32[]{:S(2)}) async-start(), calls=%async_computation.1 | async-start | bytes 1638400 | tf_op jit(solution)/shard_map/all_gather | solution.py:62
  9.0 18.6 %collective-permute-start = (s32[384]{0:T(512)}, s32[384]{0:T(512)S(1)}, u32[]{:S(2)}, u32[]{:S(2)}) collective-permute-start(s32[384]{0:T(512)} %param.12), channel_id=1, source_target_pairs={{0,4},{4,8},{8,12},{1,5},{5,9},{9,13},{2,6},{6,10},{10,14},{3,7},{... | collective-permute-start | bytes 4616 | tf_op jit(solution)/shard_map/ppermute | solution.py:16
  14.0 15.0 %collective-permute-start.1 = (s32[384]{0:T(512)}, s32[384]{0:T(512)S(1)}, u32[]{:S(2)}, u32[]{:S(2)}) collective-permute-start(s32[384]{0:T(512)} %param.12), channel_id=1, source_target_pairs={{4,0},{8,4},{12,8},{5,1},{9,5},{13,9},{6,2},{10,6},{14,10},{7,3},{... | collective-permute-start | bytes 4616 | tf_op jit(solution)/shard_map/ppermute | solution.py:16
  15.3 26.6 %collective-permute-start.2 = (bf16[384,640]{1,0:T(8,128)(2,1)}, bf16[384,640]{1,0:T(8,128)(2,1)}, u32[]{:S(2)}, u32[]{:S(2)}) collective-permute-start(bf16[384,640]{1,0:T(8,128)(2,1)} %param.8), channel_id=1, source_target_pairs={{0,4},{4,8},{8,12},{1,5},{5,9},{9,13},{2,6},{6,10},{10,14},{3,7},{... | collective-permute-start | bytes 1474568 | tf_op jit(solution)/shard_map/ppermute | solution.py:16
  20.6 38.8 %collective-permute-start.3 = (bf16[384,640]{1,0:T(8,128)(2,1)}, bf16[384,640]{1,0:T(8,128)(2,1)}, u32[]{:S(2)}, u32[]{:S(2)}) collective-permute-start(bf16[384,640]{1,0:T(8,128)(2,1)} %param.8), channel_id=1, source_target_pairs={{4,0},{8,4},{12,8},{5,1},{9,5},{13,9},{6,2},{10,6},{14,10},{7,3},{... | collective-permute-start | bytes 1474568 | tf_op jit(solution)/shard_map/ppermute | solution.py:16
  21.9 42.0 %collective-permute-start.4 = (bf16[384,640]{1,0:T(8,128)(2,1)}, bf16[384,640]{1,0:T(8,128)(2,1)S(1)}, u32[]{:S(2)}, u32[]{:S(2)}) collective-permute-start(bf16[384,640]{1,0:T(8,128)(2,1)} %param.9), channel_id=1, source_target_pairs={{0,4},{4,8},{8,12},{1,5},{5,9},{9,13},{2,6},{6,10},{10,14},{3,7},{... | collective-permute-start | bytes 1474568 | tf_op jit(solution)/shard_map/ppermute | solution.py:16
  27.7 47.3 %collective-permute-start.5 = (bf16[384,640]{1,0:T(8,128)(2,1)S(1)}, bf16[384,640]{1,0:T(8,128)(2,1)}, u32[]{:S(2)}, u32[]{:S(2)}) collective-permute-start(bf16[384,640]{1,0:T(8,128)(2,1)S(1)} %copy-done.2), channel_id=1, source_target_pairs={{4,0},{8,4},{12,8},{5,1},{9,5},{13,9},{6,2},{10,6},{14,10},{7,3},{... | collective-permute-start | bytes 1474568 | tf_op jit(solution)/shard_map/ppermute | solution.py:16
  29.0 31.7 %copy-start.7 = (bf16[384,640]{1,0:T(8,128)(2,1)S(1)}, bf16[384,640]{1,0:T(8,128)(2,1)}, u32[]{:S(2)}) copy-start(bf16[384,640]{1,0:T(8,128)(2,1)} %param.7) | copy-start | bytes 1474564
  86.3 12.3 %collective-permute-start.6 = (bf16[384,640]{0,1:T(8,128)(2,1)}, bf16[384,640]{0,1:T(8,128)(2,1)S(1)}, u32[]{:S(2)}, u32[]{:S(2)}) collective-permute-start(bf16[384,640]{0,1:T(8,128)(2,1)} %get-tuple-element.28), channel_id=1, source_target_pairs={{0,3},{1,0},{2,1},{3,2},{4,7},{5,4},{6,5},{7,6},{8,11},{9,8},{10,9... | collective-permute-start | bytes 1474568 | tf_op jit(solution)/shard_map/ppermute | solution.py:114
  87.0 23.5 %collective-permute-start.7 = (bf16[384,640]{0,1:T(8,128)(2,1)}, bf16[384,640]{0,1:T(8,128)(2,1)S(1)}, u32[]{:S(2)}, u32[]{:S(2)}) collective-permute-start(bf16[384,640]{0,1:T(8,128)(2,1)} %get-tuple-element.28), channel_id=1, source_target_pairs={{0,2},{1,3},{2,0},{3,1},{4,6},{5,7},{6,4},{7,5},{8,10},{9,11},{10,... | collective-permute-start | bytes 1474568 | tf_op jit(solution)/shard_map/ppermute | solution.py:114
  87.8 23.6 %collective-permute-start.8 = (bf16[384,640]{0,1:T(8,128)(2,1)}, bf16[384,640]{0,1:T(8,128)(2,1)S(1)}, u32[]{:S(2)}, u32[]{:S(2)}) collective-permute-start(bf16[384,640]{0,1:T(8,128)(2,1)} %get-tuple-element.28), channel_id=1, source_target_pairs={{0,1},{1,2},{2,3},{3,0},{4,5},{5,6},{6,7},{7,4},{8,9},{9,10},{10,1... | collective-permute-start | bytes 1474568 | tf_op jit(solution)/shard_map/ppermute | solution.py:114
  88.0 45.9 %collective-permute-start.9 = (bf16[2560,384]{1,0:T(8,128)(2,1)}, bf16[2560,384]{1,0:T(8,128)(2,1)}, u32[]{:S(2)}, u32[]{:S(2)}) collective-permute-start(bf16[2560,384]{1,0:T(8,128)(2,1)} %all-gather.3.cloned.1.call-done), channel_id=1, source_target_pairs={{0,16},{16,0},{1,17},{17,1},{2,18},{18,2},{3,19},{19,3},{4,20},{20... | collective-permute-start | bytes 5898248 | tf_op jit(solution)/shard_map/ppermute | solution.py:66
  114.7 47.1 %collective-permute-start.10 = (bf16[2560,256]{1,0:T(8,128)(2,1)}, bf16[2560,256]{1,0:T(8,128)(2,1)S(1)}, u32[]{:S(2)}, u32[]{:S(2)}) collective-permute-start(bf16[2560,256]{1,0:T(8,128)(2,1)} %all-gather.5.cloned.1.call-done), channel_id=1, source_target_pairs={{0,16},{16,0},{1,17},{17,1},{2,18},{18,2},{3,19},{19,3},{4,20},{20... | collective-permute-start | bytes 3932168 | tf_op jit(solution)/shard_map/ppermute | solution.py:66
  117.8 5.1 %copy-start.3 = (bf16[384,128]{0,1:T(8,128)(2,1)S(1)}, bf16[384,128]{0,1:T(8,128)(2,1)}, u32[]{:S(2)}) copy-start(bf16[384,128]{0,1:T(8,128)(2,1)} %get-tuple-element.29) | copy-start | bytes 294916
  161.8 2.6 %copy-start.5 = (bf16[2560,384]{1,0:T(8,128)(2,1)S(1)}, bf16[2560,384]{1,0:T(8,128)(2,1)}, u32[]{:S(2)}) copy-start(bf16[2560,384]{1,0:T(8,128)(2,1)} %all-gather.3.cloned.1.call-done) | copy-start | bytes 5898244
  164.5 3.0 %copy-start.6 = (bf16[2560,256]{1,0:T(8,128)(2,1)S(1)}, bf16[2560,256]{1,0:T(8,128)(2,1)}, u32[]{:S(2)}) copy-start(bf16[2560,256]{1,0:T(8,128)(2,1)} %all-gather.5.cloned.1.call-done) | copy-start | bytes 3932164
Sparse Core Ops, SparseCore 0:
  9.1 63.2 all-gather.2
  73.9 35.6 all-gather.4

commit v3 on v0

--- a/solution.py
+++ b/solution.py
@@ -14,6 +14,18 @@
     peers = lax.axis_size(axis)
     pairs = [(i, i + by) for i in range(peers) if 0 <= i + by < peers]
     return lax.ppermute(value, axis, pairs)
+
+
+def chunk_bounds(size, unit=16, parts=2):
+    units = size // unit
+    bounds = []
+    first = 0
+    for index in range(parts):
+        last = size if index == parts - 1 else first + (units // parts) * unit
+        if last > first:
+            bounds.append((first, last))
+        first = last
+    return bounds
 
 
 def attend_head(query_head, key_head, value_head, allowed):
@@ -39,6 +51,14 @@
             for col_step in (-1, 0, 1):
                 every_offset.add(layer_step * layer_tiles + row_step * TGW + col_step)
     distances = [offset for offset in sorted(every_offset) if 0 < offset < seq_count]
+    rep_position = lax.axis_index("rep")
+    half_width = out_weight.shape[1] // 2
+    block_rows = out_weight.shape[0]
+    own_half = lax.dynamic_slice_in_dim(out_weight, rep_position * half_width, half_width, axis=1)
+    row_chunks = chunk_bounds(block_rows)
+    gathered = [
+        lax.all_gather(own_half[first:last], "seq", axis=0, tiled=True) for first, last in row_chunks
+    ]
     key_list = [keys]
     value_list = [values]
     clip_list = [clip_ids]
@@ -57,6 +77,10 @@
     key_stack = jnp.stack(key_list)
     value_stack = jnp.stack(value_list)
     clip_stack = jnp.stack(clip_list)
+    first_chunk, key_stack, value_stack, clip_stack = lax.optimization_barrier(
+        (gathered[0], key_stack, value_stack, clip_stack)
+    )
+    crossed = [lax.ppermute(first_chunk, "rep", [(0, 1), (1, 0)])]
     blocks = key_stack.shape[0]
     position = lax.axis_index("seq")
     window_row = lax.dynamic_index_in_dim(neighbours, position, 0, keepdims=False)
@@ -80,12 +104,27 @@
             )
         )
     attended = jnp.concatenate(head_outputs, axis=1)
-    all_features = lax.all_gather(attended, "head", axis=1, tiled=True)
-    empty = jnp.zeros((tile_rows, out_weight.shape[1]), jnp.float32)
-    weight_piece = lax.all_gather(out_weight, "seq", axis=0, tiled=True)
-    features = lax.slice_in_dim(all_features, 0, weight_piece.shape[0], axis=1)
-    projected = empty + jnp.dot(features, weight_piece, preferred_element_type=jnp.float32)
-    return projected.astype(jnp.bfloat16)
+    attended, crossed[0] = lax.optimization_barrier((attended, crossed[0]))
+    for chunk in gathered[1:]:
+        crossed.append(lax.ppermute(chunk, "rep", [(0, 1), (1, 0)]))
+    features = lax.all_gather(attended, "head", axis=1, tiled=True)
+    blocks = features.shape[1] // block_rows
+    own_sum = None
+    other_sum = None
+    for (first, last), chunk, twin_chunk in zip(row_chunks, gathered, crossed):
+        rows = features.reshape(tile_rows, blocks, block_rows)[:, :, first:last]
+        rows = rows.reshape(tile_rows, blocks * (last - first))
+        own_part = jnp.dot(rows, chunk, preferred_element_type=jnp.float32)
+        other_part = jnp.dot(rows, twin_chunk, preferred_element_type=jnp.float32)
+        own_sum = own_part if own_sum is None else own_sum + own_part
+        other_sum = other_part if other_sum is None else other_sum + other_part
+    own_out = own_sum.astype(jnp.bfloat16)
+    other_out = other_sum.astype(jnp.bfloat16)
+    return jnp.where(
+        rep_position == 0,
+        jnp.concatenate([own_out, other_out], axis=1),
+        jnp.concatenate([other_out, own_out], axis=1),
+    )
 
 
 def solution(mesh):

time: 208 us -> 160 us (0.77)
  waiting for transfers between devices: 154 us -> 94 us
  matrix products: 15.3 us -> 19.9 us
  starting transfers between devices: 18.1 us -> 21.9 us
  local copies, waits for them, and re-layouts: 2.27 us -> 4.43 us
    all_gather x2 -> x3, waiting for transfers between devices: 143 us -> 22.2 us  [the longest x1 22.1 us: on_device(): features = lax.all_gather(attended, 'head', axis=1, tiled=True)]
    ppermute x0 -> x2, waiting for transfers between devices: none -> 33.7 us  [the longest x1 24.1 us: on_device(): crossed = [lax.ppermute(first_chunk, 'rep', [(0, 1), (1, 0)])]]
    ppermute x6, waiting for transfers between devices: 10.1 us -> 38.1 us  [from_behind(): return lax.ppermute(value, axis, pairs)]
    slice x0 -> x2, local copies, waits for them, and re-layouts: none -> 3.86 us  [the longest x1 2.16 us: on_device(): own_half[first:last]]
    dot_general x5, matrix products: 3.14 us -> 6.67 us  [attend_head(): lax.dot_general(query_head, key_head, (((1,), (1,)), ((), ())), preferred...]
    ppermute x0 -> x2, starting transfers between devices: none -> 3.06 us  [the longest x1 1.54 us: on_device(): crossed.append(lax.ppermute(chunk, 'rep', [(0, 1), (1, 0)]))]
    dot_general x5, matrix products: 5.04 us -> 7.8 us  [attend_head(): jnp.dot(weights, value_head, preferred_element_type=jnp.float32)]
    dot_general x1 -> x4, matrix products: 7.1 us -> 5.41 us  [the longest x2 3.42 us: on_device(): other_part = jnp.dot(rows, twin_chunk, preferred_element_type=jnp.float32)]
  transfers between devices with their start and end apart: 8 -> 11, of which waited for: 6 -> 5; matrix products, arithmetic and copies ran while one was open for 4% -> 13% of each run, Pallas kernels for 0% -> 0%
where the time goes in v3:
time: 160 us; the launch traced here: 159 us
  waiting for transfers between devices  94 us (59%)
  starting transfers between devices  21.9 us (14%)
  matrix products  19.9 us (12%)
  between operations  13.4 us (8%)
  other arithmetic  5.85 us (4%)
  local copies, waits for them, and re-layouts  4.43 us (3%)
    ppermute x6, waiting for transfers between devices, from_behind(): return lax.ppermute(value, axis, pairs)  38.1 us
    ppermute x1, waiting for transfers between devices, on_device(): crossed = [lax.ppermute(first_chunk, 'rep', [(0, 1), (1, 0)])]  24.1 us
    all_gather x1, waiting for transfers between devices, on_device(): features = lax.all_gather(attended, 'head', axis=1, tiled=True)  22.1 us
    ppermute x6, starting transfers between devices, from_behind(): return lax.ppermute(value, axis, pairs)  18.7 us
    ppermute x1, waiting for transfers between devices, on_device(): crossed.append(lax.ppermute(chunk, 'rep', [(0, 1), (1, 0)]))  9.52 us
    dot_general x5, matrix products, attend_head(): jnp.dot(weights, value_head, preferred_element_type=jnp.float32)  7.8 us
    dot_general x5, matrix products, attend_head(): lax.dot_general(query_head, key_head, (((1,), (1,)), ((), ())), preferred...  6.67 us
    dot_general x2, matrix products, on_device(): other_part = jnp.dot(rows, twin_chunk, preferred_element_type=jnp.float32)  3.42 us
  transfers between devices with their start and end apart: 11, of which 5 were waited for; matrix products, arithmetic and copies ran while one was open for 13% of the time, Pallas kernels for 0%

profile of v3, /device:TPU:0, one launch (start us, length us, event | category | flops | bytes accessed | tf_op | source)
XLA Modules:
  0.0 159.5 jit_solution(5913191751845881678)
XLA Ops:
  6.5 0.0 all-gather.4.cloned.1.call-start
  6.6 2.2 %fusion.44 = (bf16[320,640]{1,0:T(8,128)(2,1)}, bf16[320,640]{1,0:T(8,128)(2,1)}) fusion(bf16[640,1280]{1,0:T(8,128)(2,1)} %param.10, s32[]{:T(128)S(6)} %add.20, s32[]{:T(128)S(6)} %select_n.48), kind=kLoop, calls=%fused_computation.76 | loop fusion | bytes 1638408 | tf_op jit(solution)/shard_map/slice | solution.py:60
  8.8 0.0 all-gather.4.cloned.1.call-update
  8.8 0.0 all-gather.8.cloned.1.call-start
  8.8 5.0 %collective-permute-start = (bf16[384,640]{1,0:T(8,128)(2,1)S(1)}, bf16[384,640]{1,0:T(8,128)(2,1)S(1)}, u32[]{:S(2)}, u32[]{:S(2)}) collective-permute-start(bf16[384,640]{1,0:T(8,128)(2,1)S(1)} %copy-done.2), channel_id=1, source_target_pairs={{0,4},{4,8},{8,12},{1,5},{5,9},{9,13},{2,6},{6,10},{10,14},{3,7},{... | collective-permute-start | bytes 1474568 | tf_op jit(solution)/shard_map/ppermute | solution.py:16
  13.8 1.3 collective-permute-start.1
  15.1 5.3 %collective-permute-start.2 = (bf16[384,640]{1,0:T(8,128)(2,1)S(1)}, bf16[384,640]{1,0:T(8,128)(2,1)}, u32[]{:S(2)}, u32[]{:S(2)}) collective-permute-start(bf16[384,640]{1,0:T(8,128)(2,1)S(1)} %copy-done.3), channel_id=1, source_target_pairs={{0,4},{4,8},{8,12},{1,5},{5,9},{9,13},{2,6},{6,10},{10,14},{3,7},{... | collective-permute-start | bytes 1474568 | tf_op jit(solution)/shard_map/ppermute | solution.py:16
  20.5 1.3 collective-permute-start.3
  21.8 4.5 %collective-permute-start.4 = (s32[384]{0:T(512)S(1)}, s32[384]{0:T(512)S(1)}, u32[]{:S(2)}, u32[]{:S(2)}) collective-permute-start(s32[384]{0:T(512)S(1)} %copy-done.4), channel_id=1, source_target_pairs={{0,4},{4,8},{8,12},{1,5},{5,9},{9,13},{2,6},{6,10},{10,14},{3,7},{... | collective-permute-start | bytes 4616 | tf_op jit(solution)/shard_map/ppermute | solution.py:16
  26.3 0.0 all-gather.8.cloned.1.call-update
  26.4 0.0 all-gather.6.cloned.1.call-start
  26.5 24.4 %collective-permute-done.4 = s32[384]{0:T(512)S(1)} collective-permute-done((s32[384]{0:T(512)S(1)}, s32[384]{0:T(512)S(1)}, u32[]{:S(2)}, u32[]{:S(2)}) %collective-permute-start.4) | collective-permute-done | bytes 1568 | tf_op jit(solution)/shard_map/ppermute | solution.py:16
  50.9 1.3 collective-permute-start.5
  52.1 0.2 and_reduce_fusion
  52.3 0.1 broadcast_in_dim.32
  52.4 13.8 %collective-permute-done.5 = s32[384]{0:T(512)S(1)} collective-permute-done((s32[384]{0:T(512)S(1)}, s32[384]{0:T(512)S(1)}, u32[]{:S(2)}, u32[]{:S(2)}) %collective-permute-start.5) | collective-permute-done | bytes 1568 | tf_op jit(solution)/shard_map/ppermute | solution.py:16
  66.2 0.0 collective-permute-done
  66.2 0.0 collective-permute-done.1
  66.2 0.2 pad_maximum_fusion
  66.4 0.0 collective-permute-done.2
  66.4 0.0 collective-permute-done.3
  66.5 2.0 %pad_maximum_fusion.1 = bf16[3,384,640]{2,1,0:T(8,128)(2,1)S(1)} fusion(bf16[1,384,640]{2,1,0:T(8,128)(2,1)} %bitcast.7, bf16[1,384,640]{2,1,0:T(8,128)(2,1)} %bitcast.6, bf16[1,384,640]{2,1,0:T(8,128)(2,1)} %bitcast.59), kind=kLoop, calls=%fused_computation.27 | loop fusion | flops 1474560 | bytes 2949120 | tf_op jit(solution)/shard_map/stack | solution.py:78
  68.5 0.0 all-gather.4.cloned.1.call-done
  68.5 1.5 fusion.48
  70.1 1.6 fusion.47
  71.7 0.6 fusion.46
  72.3 0.6 fusion.45
  72.9 2.3 %fusion.49 = (f32[384]{0:T(512)S(1)}, f32[384,1152]{0,1:T(8,128)S(1)}) fusion(bf16[384,640]{1,0:T(8,128)(2,1)S(1)} %copy-done.6, bf16[1152,640]{1,0:T(8,128)(2,1)} %bitcast.57, s32[1152]{0:T(1024)S(1)} %eq.39, s32[384]{0:T(512)S(1)} %copy-done.4, pred[1152]{0:T(1024)(128)(4,1)S(1)} %and.25), kind=kOutput, calls=%fused_computation.81 | convolution fusion | flops 115457664 | bytes 2176512 | tf_op jit(solution)/shard_map/dot_general | solution.py:32
  75.3 1.5 collective-permute-start.6
  76.8 2.2 %fusion.16 = (f32[384]{0:T(512)S(1)}, f32[384]{0:T(512)S(1)}, f32[384]{0:T(512)S(1)}, f32[384]{0:T(512)S(1)}, f32[384]{0:T(512)S(1)}) fusion(f32[384,1152]{0,1:T(8,128)S(1)} %get-tuple-element.27, f32[384]{0:T(512)S(1)} %get-tuple-element.26, s32[384]{0:T(512)S(1)} %copy-done.4, s32[1152]{0:T(1024)S(1)} %eq.39, pred[1152]{0:T(1024)(128)(4,1)S(1)} %and.25, ...), kind=kLoop, calls=%fused_computation.36 | loop fusion | flops 7518336 | bytes 8870016 | tf_op jit(solution)/shard_map/reduce_sum | solution.py:38
  79.0 1.6 fusion.17
  80.6 1.6 fusion.18
  82.1 1.6 fusion.19
  83.7 1.6 fusion.20
  85.3 1.6 fusion.21
  86.8 24.1 %collective-permute-done.6 = bf16[1280,640]{1,0:T(8,128)(2,1)} collective-permute-done((bf16[1280,640]{1,0:T(8,128)(2,1)S(1)}, bf16[1280,640]{1,0:T(8,128)(2,1)}, u32[]{:S(2)}, u32[]{:S(2)}) %collective-permute-start.6) | collective-permute-done | bytes 1638432 | tf_op jit(solution)/shard_map/ppermute | solution.py:83
  111.0 0.0 all-gather.6.cloned.1.call-update
  111.0 0.0 all-gather.8.cloned.1.call-done
  111.0 1.5 collective-permute-start.7
  112.6 22.1 %all-gather.6.cloned.1.call-done = bf16[384,2560]{0,1:T(8,128)(2,1)} async-done(((bf16[384,640]{0,1:T(8,128)(2,1)}), bf16[384,2560]{0,1:T(8,128)(2,1)}) %all-gather.6.cloned.1.call-update) | async-done | bytes 1966096 | tf_op jit(solution)/shard_map/all_gather | solution.py:110
  134.7 1.7 %fusion.43 = (bf16[384,4,320]{0,2,1:T(8,128)(2,1)S(1)}, bf16[384,4,320]{0,2,1:T(8,128)(2,1)S(1)}) fusion(bf16[384,4,640]{0,2,1:T(8,128)(2,1)} %bitcast.47), kind=kLoop, calls=%fused_computation.75 | loop fusion | bytes 3932160 | tf_op jit(solution)/shard_map/slice | solution.py:115
  136.4 9.5 %collective-permute-done.7 = bf16[1280,640]{1,0:T(8,128)(2,1)S(1)} collective-permute-done((bf16[1280,640]{1,0:T(8,128)(2,1)}, bf16[1280,640]{1,0:T(8,128)(2,1)S(1)}, u32[]{:S(2)}, u32[]{:S(2)}) %collective-permute-start.7) | collective-permute-done | bytes 1638432 | tf_op jit(solution)/shard_map/ppermute | solution.py:109
  145.9 1.0 fusion.51
  146.9 2.4 %fusion.11 = bf16[384,640]{1,0:T(8,128)(2,1)S(1)} fusion(f32[384,640]{1,0:T(8,128)S(1)} %fusion.51, bf16[384,1280]{0,1:T(8,128)(2,1)S(1)} %bitcast.45, bf16[1280,640]{1,0:T(8,128)(2,1)} %collective-permute-done.6), kind=kOutput, calls=%fused_computation.31 | convolution fusion | flops 629637120 | bytes 4096000 | tf_op jit(solution)/shard_map/dot_general | solution.py:118
  149.3 1.0 fusion.50
  150.3 0.4 copy-done.5
  150.8 1.0 fusion.10
  151.8 1.2 maximum_select_fusion
  (26 shorter events, 0.1 us)
Async XLA Ops:
  6.5 19.9 %copy-start.8 = (s32[3]{0:T(128)S(1)}, s32[3]{0:T(128)}, u32[]{:S(2)}) copy-start(s32[3]{0:T(128)} %constant.36) | copy-start | bytes 40
  6.5 2.3 %copy-start.2 = (bf16[384,640]{1,0:T(8,128)(2,1)S(1)}, bf16[384,640]{1,0:T(8,128)(2,1)}, u32[]{:S(2)}) copy-start(bf16[384,640]{1,0:T(8,128)(2,1)} %param.8) | copy-start | bytes 1474564
  6.5 8.6 %copy-start.3 = (bf16[384,640]{1,0:T(8,128)(2,1)S(1)}, bf16[384,640]{1,0:T(8,128)(2,1)}, u32[]{:S(2)}) copy-start(bf16[384,640]{1,0:T(8,128)(2,1)} %param.9) | copy-start | bytes 1474564
  6.5 15.2 %copy-start.4 = (s32[384]{0:T(512)S(1)}, s32[384]{0:T(512)}, u32[]{:S(2)}) copy-start(s32[384]{0:T(512)} %param.12) | copy-start | bytes 4612
  6.5 19.9 %copy-start.7 = (s32[4,27]{1,0:T(4,128)S(1)}, s32[4,27]{1,0:T(4,128)}, u32[]{:S(2)}) copy-start(s32[4,27]{1,0:T(4,128)} %param.11) | copy-start | bytes 1300
  6.5 62.0 %all-gather.4.cloned.1.call-start = ((), (), s32[]{:S(2)}) async-start(), calls=%async_computation | async-start | bytes 2048000 | tf_op jit(solution)/shard_map/all_gather | solution.py:60
  8.8 102.2 %all-gather.8.cloned.1.call-start = ((), (), s32[]{:S(2)}) async-start(), calls=%async_computation.2 | async-start | bytes 2048000 | tf_op jit(solution)/shard_map/all_gather | solution.py:60
  8.8 57.4 %collective-permute-start = (bf16[384,640]{1,0:T(8,128)(2,1)S(1)}, bf16[384,640]{1,0:T(8,128)(2,1)S(1)}, u32[]{:S(2)}, u32[]{:S(2)}) collective-permute-start(bf16[384,640]{1,0:T(8,128)(2,1)S(1)} %copy-done.2), channel_id=1, source_target_pairs={{0,4},{4,8},{8,12},{1,5},{5,9},{9,13},{2,6},{6,10},{10,14},{3,7},{... | collective-permute-start | bytes 1474568 | tf_op jit(solution)/shard_map/ppermute | solution.py:16
  13.8 52.4 %collective-permute-start.1 = (bf16[384,640]{1,0:T(8,128)(2,1)S(1)}, bf16[384,640]{1,0:T(8,128)(2,1)S(1)}, u32[]{:S(2)}, u32[]{:S(2)}) collective-permute-start(bf16[384,640]{1,0:T(8,128)(2,1)S(1)} %copy-done.2), channel_id=1, source_target_pairs={{4,0},{8,4},{12,8},{5,1},{9,5},{13,9},{6,2},{10,6},{14,10},{7,3},{... | collective-permute-start | bytes 1474568 | tf_op jit(solution)/shard_map/ppermute | solution.py:16
  15.1 51.3 %collective-permute-start.2 = (bf16[384,640]{1,0:T(8,128)(2,1)S(1)}, bf16[384,640]{1,0:T(8,128)(2,1)}, u32[]{:S(2)}, u32[]{:S(2)}) collective-permute-start(bf16[384,640]{1,0:T(8,128)(2,1)S(1)} %copy-done.3), channel_id=1, source_target_pairs={{0,4},{4,8},{8,12},{1,5},{5,9},{9,13},{2,6},{6,10},{10,14},{3,7},{... | collective-permute-start | bytes 1474568 | tf_op jit(solution)/shard_map/ppermute | solution.py:16
  20.5 46.0 %collective-permute-start.3 = (bf16[384,640]{1,0:T(8,128)(2,1)S(1)}, bf16[384,640]{1,0:T(8,128)(2,1)}, u32[]{:S(2)}, u32[]{:S(2)}) collective-permute-start(bf16[384,640]{1,0:T(8,128)(2,1)S(1)} %copy-done.3), channel_id=1, source_target_pairs={{4,0},{8,4},{12,8},{5,1},{9,5},{13,9},{6,2},{10,6},{14,10},{7,3},{... | collective-permute-start | bytes 1474568 | tf_op jit(solution)/shard_map/ppermute | solution.py:16
  21.8 29.1 %collective-permute-start.4 = (s32[384]{0:T(512)S(1)}, s32[384]{0:T(512)S(1)}, u32[]{:S(2)}, u32[]{:S(2)}) collective-permute-start(s32[384]{0:T(512)S(1)} %copy-done.4), channel_id=1, source_target_pairs={{0,4},{4,8},{8,12},{1,5},{5,9},{9,13},{2,6},{6,10},{10,14},{3,7},{... | collective-permute-start | bytes 4616 | tf_op jit(solution)/shard_map/ppermute | solution.py:16
  26.4 108.3 %all-gather.6.cloned.1.call-start = ((), (), s32[]{:S(2)}) async-start(), calls=%async_computation.1 | async-start | bytes 2457600 | tf_op jit(solution)/shard_map/all_gather | solution.py:110
  50.9 15.3 %collective-permute-start.5 = (s32[384]{0:T(512)S(1)}, s32[384]{0:T(512)S(1)}, u32[]{:S(2)}, u32[]{:S(2)}) collective-permute-start(s32[384]{0:T(512)S(1)} %copy-done.4), channel_id=1, source_target_pairs={{4,0},{8,4},{12,8},{5,1},{9,5},{13,9},{6,2},{10,6},{14,10},{7,3},{... | collective-permute-start | bytes 4616 | tf_op jit(solution)/shard_map/ppermute | solution.py:16
  66.4 5.9 %copy-start.1 = (bf16[3,384,640]{2,1,0:T(8,128)(2,1)}, bf16[3,384,640]{2,1,0:T(8,128)(2,1)S(1)}, u32[]{:S(2)}) copy-start(bf16[3,384,640]{2,1,0:T(8,128)(2,1)S(1)} %pad_maximum_fusion) | copy-start | bytes 4423684
  70.1 1.6 copy-start.6
  72.9 2.3 %copy-start = (bf16[1280,640]{1,0:T(8,128)(2,1)S(1)}, bf16[1280,640]{1,0:T(8,128)(2,1)}, u32[]{:S(2)}) copy-start(bf16[1280,640]{1,0:T(8,128)(2,1)} %all-gather.4.cloned.1.call-done) | copy-start | bytes 4915204
  75.3 35.7 %collective-permute-start.6 = (bf16[1280,640]{1,0:T(8,128)(2,1)S(1)}, bf16[1280,640]{1,0:T(8,128)(2,1)}, u32[]{:S(2)}, u32[]{:S(2)}) collective-permute-start(bf16[1280,640]{1,0:T(8,128)(2,1)S(1)} %copy-done), channel_id=1, source_target_pairs={{0,16},{16,0},{1,17},{17,1},{2,18},{18,2},{3,19},{19,3},{4,20},{20... | collective-permute-start | bytes 4915208 | tf_op jit(solution)/shard_map/ppermute | solution.py:83
  111.0 34.9 %collective-permute-start.7 = (bf16[1280,640]{1,0:T(8,128)(2,1)}, bf16[1280,640]{1,0:T(8,128)(2,1)S(1)}, u32[]{:S(2)}, u32[]{:S(2)}) collective-permute-start(bf16[1280,640]{1,0:T(8,128)(2,1)} %all-gather.8.cloned.1.call-done), channel_id=1, source_target_pairs={{0,16},{16,0},{1,17},{17,1},{2,18},{18,2},{3,19},{19,3},{4,20},{20... | collective-permute-start | bytes 4915208 | tf_op jit(solution)/shard_map/ppermute | solution.py:109
  149.3 1.4 copy-start.5
Sparse Core Ops, SparseCore 0:
  9.0 55.5 all-gather.3
  66.1 39.5 all-gather.7
  111.1 23.5 all-gather.5

commit v4 on v3

--- a/solution.py
+++ b/solution.py
@@ -16,7 +16,7 @@
     return lax.ppermute(value, axis, pairs)
 
 
-def chunk_bounds(size, unit=16, parts=2):
+def chunk_bounds(size, unit=16, parts=4):
     units = size // unit
     bounds = []
     first = 0
@@ -104,10 +104,22 @@
             )
         )
     attended = jnp.concatenate(head_outputs, axis=1)
-    attended, crossed[0] = lax.optimization_barrier((attended, crossed[0]))
-    for chunk in gathered[1:]:
-        crossed.append(lax.ppermute(chunk, "rep", [(0, 1), (1, 0)]))
-    features = lax.all_gather(attended, "head", axis=1, tiled=True)
+    for index in range(1, len(gathered)):
+        gathered[index], crossed[-1] = lax.optimization_barrier((gathered[index], crossed[-1]))
+        crossed.append(lax.ppermute(gathered[index], "rep", [(0, 1), (1, 0)]))
+    head_count = lax.axis_size("head")
+    head_position = lax.axis_index("head")
+    received = [attended]
+    for shift in range(1, head_count):
+        pairs = [(j, (j + shift) % head_count) for j in range(head_count)]
+        received.append(lax.ppermute(attended, "head", pairs))
+    ordered = []
+    for group in range(head_count):
+        block = received[0]
+        for shift in range(1, head_count):
+            block = jnp.where((head_position - shift) % head_count == group, received[shift], block)
+        ordered.append(block)
+    features = jnp.concatenate(ordered, axis=1)
     blocks = features.shape[1] // block_rows
     own_sum = None
     other_sum = None

time: 160 us -> 181 us (1.13)
  blocking collectives: 0 us -> 82.5 us
  waiting for transfers between devices: 94 us -> 49.9 us
  between operations: 13.4 us -> 0.41 us
  matrix products: 19.9 us -> 14.3 us
  other arithmetic: 5.85 us -> 8.06 us
  local copies, waits for them, and re-layouts: 4.43 us -> 2.52 us
    all_gather x0 -> x4, blocking collectives: none -> 82.5 us  [on_device(): lax.all_gather(own_half[first:last], 'seq', axis=0, tiled=True)]
    ppermute x1 -> x6, waiting for transfers between devices: 9.52 us -> 45.9 us  [the longest x3 45.9 us: on_device(): crossed.append(lax.ppermute(gathered[index], 'rep', [(0, 1), (1, 0)]))]
    ppermute x6, waiting for transfers between devices: 38.1 us -> 4.04 us  [from_behind(): return lax.ppermute(value, axis, pairs)]
    ppermute x1, waiting for transfers between devices: 24.1 us -> 0.01 us  [on_device(): crossed = [lax.ppermute(first_chunk, 'rep', [(0, 1), (1, 0)])]]
    all_gather x3 -> x0, waiting for transfers between devices: 22.2 us -> none  [the longest x1 22.1 us: on_device(): features = lax.all_gather(attended, 'head', axis=1, tiled=True)]
    dot_general x5, matrix products: 7.8 us -> 4.59 us  [attend_head(): jnp.dot(weights, value_head, preferred_element_type=jnp.float32)]
    another operation x1, other arithmetic: 0.19 us -> 2.35 us  [on_device(): key_stack = jnp.stack(key_list)]
    dot_general x5, matrix products: 6.67 us -> 4.69 us  [attend_head(): lax.dot_general(query_head, key_head, (((1,), (1,)), ((), ())), preferred...]
  transfers between devices with their start and end apart: 11 -> 13, of which waited for: 5 -> 4; matrix products, arithmetic and copies ran while one was open for 13% -> 9% of each run, Pallas kernels for 0% -> 0%
where the time goes in v4:
time: 181 us
  blocking collectives  82.5 us (46%)
  waiting for transfers between devices  49.9 us (28%)
  starting transfers between devices  22.8 us (13%)
  matrix products  14.3 us (8%)
  other arithmetic  8.06 us (4%)
  local copies, waits for them, and re-layouts  2.52 us (1%)
    all_gather x4, blocking collectives, on_device(): lax.all_gather(own_half[first:last], 'seq', axis=0, tiled=True)  82.5 us
    ppermute x3, waiting for transfers between devices, on_device(): crossed.append(lax.ppermute(gathered[index], 'rep', [(0, 1), (1, 0)]))  45.9 us
    ppermute x6, starting transfers between devices, from_behind(): return lax.ppermute(value, axis, pairs)  18 us
    dot_general x5, matrix products, attend_head(): lax.dot_general(query_head, key_head, (((1,), (1,)), ((), ())), preferred...  4.69 us
    dot_general x5, matrix products, attend_head(): jnp.dot(weights, value_head, preferred_element_type=jnp.float32)  4.59 us
    ppermute x6, waiting for transfers between devices, from_behind(): return lax.ppermute(value, axis, pairs)  4.04 us
  transfers between devices with their start and end apart: 13, of which 4 were waited for; matrix products, arithmetic and copies ran while one was open for 9% of the time, Pallas kernels for 0%

profile of v4, /device:TPU:0, one launch (start us, length us, event | category | flops | bytes accessed | tf_op | source)
XLA Modules:
  0.0 180.5 jit_solution(5776254294343076778)
XLA Ops:
  0.0 4.9 %collective-permute-start = (bf16[384,640]{1,0:T(8,128)(2,1)}, bf16[384,640]{1,0:T(8,128)(2,1)S(1)}, u32[]{:S(2)}, u32[]{:S(2)}) collective-permute-start(bf16[384,640]{1,0:T(8,128)(2,1)} %param.8), channel_id=1, source_target_pairs={{0,4},{4,8},{8,12},{1,5},{5,9},{9,13},{2,6},{6,10},{10,14},{3,7},{... | collective-permute-start | bytes 1474568 | tf_op jit(solution)/shard_map/ppermute | solution.py:16
  5.0 1.3 collective-permute-start.1
  6.3 4.6 %collective-permute-start.2 = (bf16[384,640]{1,0:T(8,128)(2,1)}, bf16[384,640]{1,0:T(8,128)(2,1)S(1)}, u32[]{:S(2)}, u32[]{:S(2)}) collective-permute-start(bf16[384,640]{1,0:T(8,128)(2,1)} %param.9), channel_id=1, source_target_pairs={{0,4},{4,8},{8,12},{1,5},{5,9},{9,13},{2,6},{6,10},{10,14},{3,7},{... | collective-permute-start | bytes 1474568 | tf_op jit(solution)/shard_map/ppermute | solution.py:16
  10.8 1.3 collective-permute-start.3
  12.1 4.5 %collective-permute-start.4 = (s32[384]{0:T(512)}, s32[384]{0:T(512)S(1)}, u32[]{:S(2)}, u32[]{:S(2)}) collective-permute-start(s32[384]{0:T(512)} %param.12), channel_id=1, source_target_pairs={{0,4},{4,8},{8,12},{1,5},{5,9},{9,13},{2,6},{6,10},{10,14},{3,7},{... | collective-permute-start | bytes 4616 | tf_op jit(solution)/shard_map/ppermute | solution.py:16
  16.8 1.4 fusion.47
  18.1 27.4 %all_gather.12 = bf16[640,640]{1,0:T(8,128)(2,1)S(1)} all-gather(bf16[160,640]{1,0:T(8,128)(2,1)S(1)} %get-tuple-element.40), channel_id=1, replica_groups=mesh['rep'=2,'seq'=4,'head'=4] {'seq'}, dimensions={0}, use_global_device_ids=true | all-gather | bytes 1024000 | tf_op jit(solution)/shard_map/all_gather | solution.py:60
  45.6 18.1 %all_gather.13 = bf16[640,640]{1,0:T(8,128)(2,1)S(1)} all-gather(bf16[160,640]{1,0:T(8,128)(2,1)S(1)} %get-tuple-element.38), channel_id=1, replica_groups=mesh['rep'=2,'seq'=4,'head'=4] {'seq'}, dimensions={0}, use_global_device_ids=true | all-gather | bytes 1024000 | tf_op jit(solution)/shard_map/all_gather | solution.py:60
  63.8 0.2 and_reduce_fusion
  64.0 1.3 collective-permute-start.5
  65.4 4.0 %collective-permute-done.5 = s32[384]{0:T(512)S(1)} collective-permute-done((s32[384]{0:T(512)S(1)}, s32[384]{0:T(512)S(1)}, u32[]{:S(2)}, u32[]{:S(2)}) %collective-permute-start.5) | collective-permute-done | bytes 1568 | tf_op jit(solution)/shard_map/ppermute | solution.py:16
  69.5 2.4 %pad_maximum_fusion.1 = bf16[3,384,640]{2,1,0:T(8,128)(2,1)} fusion(bf16[1,384,640]{2,1,0:T(8,128)(2,1)} %bitcast.4, bf16[1,384,640]{2,1,0:T(8,128)(2,1)S(1)} %bitcast.75, bf16[1,384,640]{2,1,0:T(8,128)(2,1)S(1)} %bitcast.72), kind=kLoop, calls=%fused_computation.27 | loop fusion | flops 1474560 | bytes 2949120 | tf_op jit(solution)/shard_map/stack | solution.py:77
  71.9 0.8 copy-done.2
  72.7 1.5 pad_maximum_fusion.2
  74.2 2.2 %fusion.51 = (f32[384]{0:T(512)S(1)}, f32[384,1152]{0,1:T(8,128)S(1)}) fusion(bf16[384,640]{1,0:T(8,128)(2,1)} %param.7, bf16[1152,640]{1,0:T(8,128)(2,1)} %bitcast.67, s32[1152]{0:T(1024)S(1)} %eq.89, s32[384]{0:T(512)S(1)} %copy-done.3, pred[1152]{0:T(1024)(128)(4,1)S(1)} %and.49), kind=kOutput, calls=%fused_computation.89 | convolution fusion | flops 115457664 | bytes 2171520 | tf_op jit(solution)/shard_map/dot_general | solution.py:32
  76.4 0.6 fusion.50
  77.0 0.6 fusion.49
  77.7 0.6 fusion.48
  78.3 0.6 fusion.52
  78.9 1.6 collective-permute-start.9
  80.5 2.2 %fusion.19 = (f32[384]{0:T(512)S(1)}, f32[384]{0:T(512)S(1)}, f32[384]{0:T(512)S(1)}, f32[384]{0:T(512)S(1)}, f32[384]{0:T(512)S(1)}) fusion(f32[384,1152]{0,1:T(8,128)S(1)} %get-tuple-element.43, f32[384]{0:T(512)S(1)} %get-tuple-element.42, s32[384]{0:T(512)S(1)} %copy-done.3, s32[1152]{0:T(1024)S(1)} %eq.89, pred[1152]{0:T(1024)(128)(4,1)S(1)} %and.49, ...), kind=kLoop, calls=%fused_computation.41 | loop fusion | flops 7518336 | bytes 8870016 | tf_op jit(solution)/shard_map/reduce_sum | solution.py:38
  82.8 0.9 fusion.20
  83.7 0.9 fusion.21
  84.6 0.9 fusion.22
  85.5 0.9 fusion.23
  86.5 0.9 fusion.24
  87.4 1.6 collective-permute-start.7
  89.0 0.2 collective-permute-start.8
  89.2 18.4 %all_gather.14 = bf16[640,640]{1,0:T(8,128)(2,1)S(1)} all-gather(bf16[160,640]{1,0:T(8,128)(2,1)S(1)} %get-tuple-element.39), channel_id=1, replica_groups=mesh['rep'=2,'seq'=4,'head'=4] {'seq'}, dimensions={0}, use_global_device_ids=true | all-gather | bytes 1024000 | tf_op jit(solution)/shard_map/all_gather | solution.py:60
  107.6 18.5 %all_gather.15 = bf16[640,640]{1,0:T(8,128)(2,1)S(1)} all-gather(bf16[160,640]{1,0:T(8,128)(2,1)S(1)} %get-tuple-element.41), channel_id=1, replica_groups=mesh['rep'=2,'seq'=4,'head'=4] {'seq'}, dimensions={0}, use_global_device_ids=true | all-gather | bytes 1024000 | tf_op jit(solution)/shard_map/all_gather | solution.py:60
  126.0 0.5 collective-permute-start.10
  126.6 0.3 select_select_fusion.3
  126.9 0.2 pad_maximum_fusion
  127.1 0.2 fusion.46
  127.4 17.1 %collective-permute-done.10 = bf16[640,640]{1,0:T(8,128)(2,1)S(1)} collective-permute-done((bf16[640,640]{1,0:T(8,128)(2,1)S(1)}, bf16[640,640]{1,0:T(8,128)(2,1)S(1)}, u32[]{:S(2)}, u32[]{:S(2)}) %collective-permute-start.10) | collective-permute-done | bytes 819232 | tf_op jit(solution)/shard_map/ppermute | solution.py:109
  144.5 0.5 collective-permute-start.11
  145.0 0.6 fusion.53
  145.6 0.6 convolution_add_fusion.2
  146.2 0.6 fusion.55
  146.9 16.0 %collective-permute-done.11 = bf16[640,640]{1,0:T(8,128)(2,1)S(1)} collective-permute-done((bf16[640,640]{1,0:T(8,128)(2,1)S(1)}, bf16[640,640]{1,0:T(8,128)(2,1)S(1)}, u32[]{:S(2)}, u32[]{:S(2)}) %collective-permute-start.11) | collective-permute-done | bytes 819232 | tf_op jit(solution)/shard_map/ppermute | solution.py:109
  162.9 0.5 collective-permute-start.12
  163.4 0.6 fusion.54
  164.0 0.6 fusion.56
  164.6 0.6 fusion.13
  165.3 12.8 %collective-permute-done.12 = bf16[640,640]{1,0:T(8,128)(2,1)S(1)} collective-permute-done((bf16[640,640]{1,0:T(8,128)(2,1)S(1)}, bf16[640,640]{1,0:T(8,128)(2,1)S(1)}, u32[]{:S(2)}, u32[]{:S(2)}) %collective-permute-start.12) | collective-permute-done | bytes 819232 | tf_op jit(solution)/shard_map/ppermute | solution.py:109
  178.0 0.6 fusion.57
  178.7 0.6 fusion.14
  179.3 1.2 maximum_select_fusion
  (33 shorter events, 0.3 us)
Async XLA Ops:
  0.0 69.5 %collective-permute-start = (bf16[384,640]{1,0:T(8,128)(2,1)}, bf16[384,640]{1,0:T(8,128)(2,1)S(1)}, u32[]{:S(2)}, u32[]{:S(2)}) collective-permute-start(bf16[384,640]{1,0:T(8,128)(2,1)} %param.8), channel_id=1, source_target_pairs={{0,4},{4,8},{8,12},{1,5},{5,9},{9,13},{2,6},{6,10},{10,14},{3,7},{... | collective-permute-start | bytes 1474568 | tf_op jit(solution)/shard_map/ppermute | solution.py:16
  5.0 64.5 %collective-permute-start.1 = (bf16[384,640]{1,0:T(8,128)(2,1)}, bf16[384,640]{1,0:T(8,128)(2,1)}, u32[]{:S(2)}, u32[]{:S(2)}) collective-permute-start(bf16[384,640]{1,0:T(8,128)(2,1)} %param.8), channel_id=1, source_target_pairs={{4,0},{8,4},{12,8},{5,1},{9,5},{13,9},{6,2},{10,6},{14,10},{7,3},{... | collective-permute-start | bytes 1474568 | tf_op jit(solution)/shard_map/ppermute | solution.py:16
  6.3 65.6 %collective-permute-start.2 = (bf16[384,640]{1,0:T(8,128)(2,1)}, bf16[384,640]{1,0:T(8,128)(2,1)S(1)}, u32[]{:S(2)}, u32[]{:S(2)}) collective-permute-start(bf16[384,640]{1,0:T(8,128)(2,1)} %param.9), channel_id=1, source_target_pairs={{0,4},{4,8},{8,12},{1,5},{5,9},{9,13},{2,6},{6,10},{10,14},{3,7},{... | collective-permute-start | bytes 1474568 | tf_op jit(solution)/shard_map/ppermute | solution.py:16
  10.8 61.0 %collective-permute-start.3 = (bf16[384,640]{1,0:T(8,128)(2,1)}, bf16[384,640]{1,0:T(8,128)(2,1)}, u32[]{:S(2)}, u32[]{:S(2)}) collective-permute-start(bf16[384,640]{1,0:T(8,128)(2,1)} %param.9), channel_id=1, source_target_pairs={{4,0},{8,4},{12,8},{5,1},{9,5},{13,9},{6,2},{10,6},{14,10},{7,3},{... | collective-permute-start | bytes 1474568 | tf_op jit(solution)/shard_map/ppermute | solution.py:16
  12.1 51.8 %collective-permute-start.4 = (s32[384]{0:T(512)}, s32[384]{0:T(512)S(1)}, u32[]{:S(2)}, u32[]{:S(2)}) collective-permute-start(s32[384]{0:T(512)} %param.12), channel_id=1, source_target_pairs={{0,4},{4,8},{8,12},{1,5},{5,9},{9,13},{2,6},{6,10},{10,14},{3,7},{... | collective-permute-start | bytes 4616 | tf_op jit(solution)/shard_map/ppermute | solution.py:16
  16.7 47.0 %copy-start.6 = (s32[3]{0:T(128)S(1)}, s32[3]{0:T(128)}, u32[]{:S(2)}) copy-start(s32[3]{0:T(128)} %constant.86) | copy-start | bytes 40
  16.7 47.0 %copy-start.5 = (s32[4,27]{1,0:T(4,128)S(1)}, s32[4,27]{1,0:T(4,128)}, u32[]{:S(2)}) copy-start(s32[4,27]{1,0:T(4,128)} %param.11) | copy-start | bytes 1300
  16.7 47.2 %copy-start.3 = (s32[384]{0:T(512)S(1)}, s32[384]{0:T(512)}, u32[]{:S(2)}) copy-start(s32[384]{0:T(512)} %param.12) | copy-start | bytes 4612
  16.7 52.8 %copy-start.1 = (bf16[384,640]{1,0:T(8,128)(2,1)S(1)}, bf16[384,640]{1,0:T(8,128)(2,1)}, u32[]{:S(2)}) copy-start(bf16[384,640]{1,0:T(8,128)(2,1)} %param.8) | copy-start | bytes 1474564
  64.0 5.5 %collective-permute-start.5 = (s32[384]{0:T(512)S(1)}, s32[384]{0:T(512)S(1)}, u32[]{:S(2)}, u32[]{:S(2)}) collective-permute-start(s32[384]{0:T(512)S(1)} %copy-done.3), channel_id=1, source_target_pairs={{4,0},{8,4},{12,8},{5,1},{9,5},{13,9},{6,2},{10,6},{14,10},{7,3},{... | collective-permute-start | bytes 4616 | tf_op jit(solution)/shard_map/ppermute | solution.py:16
  71.9 0.8 copy-start.2
  74.2 2.2 %copy-start = (bf16[3,384,640]{2,1,0:T(8,128)(2,1)S(1)}, bf16[3,384,640]{2,1,0:T(8,128)(2,1)}, u32[]{:S(2)}) copy-start(bf16[3,384,640]{2,1,0:T(8,128)(2,1)} %pad_maximum_fusion.1) | copy-start | bytes 4423684
  74.2 2.2 %copy-start.4 = (bf16[384,640]{1,0:T(8,128)(2,1)S(1)}, bf16[384,640]{1,0:T(8,128)(2,1)}, u32[]{:S(2)}) copy-start(bf16[384,640]{1,0:T(8,128)(2,1)} %param.7) | copy-start | bytes 1474564
  78.9 47.1 %collective-permute-start.9 = (bf16[640,640]{1,0:T(8,128)(2,1)S(1)}, bf16[640,640]{1,0:T(8,128)(2,1)S(1)}, u32[]{:S(2)}, u32[]{:S(2)}) collective-permute-start(bf16[640,640]{1,0:T(8,128)(2,1)S(1)} %all_gather.12), channel_id=1, source_target_pairs={{0,16},{16,0},{1,17},{17,1},{2,18},{18,2},{3,19},{19,3},{4,20},{20... | collective-permute-start | bytes 2457608 | tf_op jit(solution)/shard_map/ppermute | solution.py:83
  87.4 39.2 %collective-permute-start.6 = (bf16[384,640]{0,1:T(8,128)(2,1)S(1)}, bf16[384,640]{0,1:T(8,128)(2,1)S(1)}, u32[]{:S(2)}, u32[]{:S(2)}) collective-permute-start(bf16[384,640]{0,1:T(8,128)(2,1)S(1)} %fusion.24), channel_id=1, source_target_pairs={{0,3},{1,0},{2,1},{3,2},{4,7},{5,4},{6,5},{7,6},{8,11},{9,8},{10,9... | collective-permute-start | bytes 1474568 | tf_op jit(solution)/shard_map/ppermute | solution.py:115
  87.4 39.1 %collective-permute-start.7 = (bf16[384,640]{0,1:T(8,128)(2,1)S(1)}, bf16[384,640]{0,1:T(8,128)(2,1)S(1)}, u32[]{:S(2)}, u32[]{:S(2)}) collective-permute-start(bf16[384,640]{0,1:T(8,128)(2,1)S(1)} %fusion.24), channel_id=1, source_target_pairs={{0,2},{1,3},{2,0},{3,1},{4,6},{5,7},{6,4},{7,5},{8,10},{9,11},{10,... | collective-permute-start | bytes 1474568 | tf_op jit(solution)/shard_map/ppermute | solution.py:115
  89.0 37.6 %collective-permute-start.8 = (bf16[384,640]{0,1:T(8,128)(2,1)S(1)}, bf16[384,640]{0,1:T(8,128)(2,1)S(1)}, u32[]{:S(2)}, u32[]{:S(2)}) collective-permute-start(bf16[384,640]{0,1:T(8,128)(2,1)S(1)} %fusion.24), channel_id=1, source_target_pairs={{0,1},{1,2},{2,3},{3,0},{4,5},{5,6},{6,7},{7,4},{8,9},{9,10},{10,1... | collective-permute-start | bytes 1474568 | tf_op jit(solution)/shard_map/ppermute | solution.py:115
  126.0 18.4 %collective-permute-start.10 = (bf16[640,640]{1,0:T(8,128)(2,1)S(1)}, bf16[640,640]{1,0:T(8,128)(2,1)S(1)}, u32[]{:S(2)}, u32[]{:S(2)}) collective-permute-start(bf16[640,640]{1,0:T(8,128)(2,1)S(1)} %all_gather.13), channel_id=1, source_target_pairs={{0,16},{16,0},{1,17},{17,1},{2,18},{18,2},{3,19},{19,3},{4,20},{20... | collective-permute-start | bytes 2457608 | tf_op jit(solution)/shard_map/ppermute | solution.py:109
  144.5 18.4 %collective-permute-start.11 = (bf16[640,640]{1,0:T(8,128)(2,1)S(1)}, bf16[640,640]{1,0:T(8,128)(2,1)S(1)}, u32[]{:S(2)}, u32[]{:S(2)}) collective-permute-start(bf16[640,640]{1,0:T(8,128)(2,1)S(1)} %all_gather.14), channel_id=1, source_target_pairs={{0,16},{16,0},{1,17},{17,1},{2,18},{18,2},{3,19},{19,3},{4,20},{20... | collective-permute-start | bytes 2457608 | tf_op jit(solution)/shard_map/ppermute | solution.py:109
  162.9 15.2 %collective-permute-start.12 = (bf16[640,640]{1,0:T(8,128)(2,1)S(1)}, bf16[640,640]{1,0:T(8,128)(2,1)S(1)}, u32[]{:S(2)}, u32[]{:S(2)}) collective-permute-start(bf16[640,640]{1,0:T(8,128)(2,1)S(1)} %all_gather.15), channel_id=1, source_target_pairs={{0,16},{16,0},{1,17},{17,1},{2,18},{18,2},{3,19},{19,3},{4,20},{20... | collective-permute-start | bytes 2457608 | tf_op jit(solution)/shard_map/ppermute | solution.py:109

commit v5 on v4

--- a/solution.py
+++ b/solution.py
@@ -16,7 +16,7 @@
     return lax.ppermute(value, axis, pairs)
 
 
-def chunk_bounds(size, unit=16, parts=4):
+def chunk_bounds(size, unit=16, parts=3):
     units = size // unit
     bounds = []
     first = 0

time: 181 us -> 153 us (0.85)
  blocking collectives: 82.5 us -> 0 us
  waiting for transfers between devices: 49.9 us -> 87.8 us
  between operations: 0.41 us -> 13.5 us
  matrix products: 14.3 us -> 16.8 us
  starting transfers between devices: 22.8 us -> 25.2 us
  other arithmetic: 8.06 us -> 5.73 us
    all_gather x4 -> x0, blocking collectives: 82.5 us -> none  [on_device(): lax.all_gather(own_half[first:last], 'seq', axis=0, tiled=True)]
    all_gather x0 -> x3, waiting for transfers between devices: none -> 29.3 us  [on_device(): lax.all_gather(own_half[first:last], 'seq', axis=0, tiled=True)]
    ppermute x3 -> x2, waiting for transfers between devices: 45.9 us -> 19.8 us  [on_device(): crossed.append(lax.ppermute(gathered[index], 'rep', [(0, 1), (1, 0)]))]
    ppermute x6, waiting for transfers between devices: 4.04 us -> 28.2 us  [from_behind(): return lax.ppermute(value, axis, pairs)]
    ppermute x3, waiting for transfers between devices: 0.01 us -> 7.92 us  [on_device(): received.append(lax.ppermute(attended, 'head', pairs))]
    slice x1 -> x2, local copies, waits for them, and re-layouts: 1.36 us -> 3.66 us  [on_device(): own_half[first:last]]
    another operation x1, other arithmetic: 2.35 us -> 0.19 us  [on_device(): key_stack = jnp.stack(key_list)]
    ppermute x1, waiting for transfers between devices: 0.01 us -> 1.9 us  [on_device(): crossed = [lax.ppermute(first_chunk, 'rep', [(0, 1), (1, 0)])]]
  transfers between devices with their start and end apart: 13 -> 15, of which waited for: 4 -> 8; matrix products, arithmetic and copies ran while one was open for 9% -> 14% of each run, Pallas kernels for 0% -> 0%
where the time goes in v5:
time: 153 us
  waiting for transfers between devices  87.8 us (57%)
  starting transfers between devices  25.2 us (16%)
  matrix products  16.8 us (11%)
  between operations  13.5 us (9%)
  other arithmetic  5.73 us (4%)
  local copies, waits for them, and re-layouts  4.02 us (3%)
    all_gather x3, waiting for transfers between devices, on_device(): lax.all_gather(own_half[first:last], 'seq', axis=0, tiled=True)  29.3 us
    ppermute x6, waiting for transfers between devices, from_behind(): return lax.ppermute(value, axis, pairs)  28.2 us
    ppermute x2, waiting for transfers between devices, on_device(): crossed.append(lax.ppermute(gathered[index], 'rep', [(0, 1), (1, 0)]))  19.8 us
    ppermute x6, starting transfers between devices, from_behind(): return lax.ppermute(value, axis, pairs)  18.7 us
    ppermute x3, waiting for transfers between devices, on_device(): received.append(lax.ppermute(attended, 'head', pairs))  7.92 us
    dot_general x5, matrix products, attend_head(): lax.dot_general(query_head, key_head, (((1,), (1,)), ((), ())), preferred...  4.97 us
    dot_general x5, matrix products, attend_head(): jnp.dot(weights, value_head, preferred_element_type=jnp.float32)  4.62 us
    slice x2, local copies, waits for them, and re-layouts, on_device(): own_half[first:last]  3.66 us
  transfers between devices with their start and end apart: 15, of which 8 were waited for; matrix products, arithmetic and copies ran while one was open for 14% of the time, Pallas kernels for 0%

profile of v5, /device:TPU:0, one launch (start us, length us, event | category | flops | bytes accessed | tf_op | source)
XLA Modules:
  0.0 153.0 jit_solution(1318757133134919368)
XLA Ops:
  6.6 2.0 %fusion.45 = (bf16[208,640]{1,0:T(8,128)(2,1)}, bf16[208,640]{1,0:T(8,128)(2,1)}) fusion(bf16[640,1280]{1,0:T(8,128)(2,1)} %param.10, s32[]{:T(128)S(6)} %add.53, s32[]{:T(128)S(6)} %select_n.157), kind=kLoop, calls=%fused_computation.83 | loop fusion | bytes 1064968 | tf_op jit(solution)/shard_map/slice | solution.py:60
  8.6 0.7 all-gather.6.cloned.1.call-update
  9.4 5.0 %collective-permute-start = (bf16[384,640]{1,0:T(8,128)(2,1)}, bf16[384,640]{1,0:T(8,128)(2,1)S(1)}, u32[]{:S(2)}, u32[]{:S(2)}) collective-permute-start(bf16[384,640]{1,0:T(8,128)(2,1)} %param.8), channel_id=1, source_target_pairs={{0,4},{4,8},{8,12},{1,5},{5,9},{9,13},{2,6},{6,10},{10,14},{3,7},{... | collective-permute-start | bytes 1474568 | tf_op jit(solution)/shard_map/ppermute | solution.py:16
  14.3 1.3 collective-permute-start.1
  15.6 5.3 %collective-permute-start.2 = (bf16[384,640]{1,0:T(8,128)(2,1)}, bf16[384,640]{1,0:T(8,128)(2,1)}, u32[]{:S(2)}, u32[]{:S(2)}) collective-permute-start(bf16[384,640]{1,0:T(8,128)(2,1)} %param.9), channel_id=1, source_target_pairs={{0,4},{4,8},{8,12},{1,5},{5,9},{9,13},{2,6},{6,10},{10,14},{3,7},{... | collective-permute-start | bytes 1474568 | tf_op jit(solution)/shard_map/ppermute | solution.py:16
  21.0 1.3 collective-permute-start.3
  22.3 4.6 %collective-permute-start.4 = (s32[384]{0:T(512)}, s32[384]{0:T(512)S(1)}, u32[]{:S(2)}, u32[]{:S(2)}) collective-permute-start(s32[384]{0:T(512)} %param.12), channel_id=1, source_target_pairs={{0,4},{4,8},{8,12},{1,5},{5,9},{9,13},{2,6},{6,10},{10,14},{3,7},{... | collective-permute-start | bytes 4616 | tf_op jit(solution)/shard_map/ppermute | solution.py:16
  26.8 1.7 %dynamic-slice.2 = bf16[224,640]{1,0:T(8,128)(2,1)} dynamic-slice(bf16[640,1280]{1,0:T(8,128)(2,1)} %param.10, s32[]{:T(128)S(6)} %add.54, s32[]{:T(128)S(6)} %select_n.157), dynamic_slice_sizes={224,640} | dynamic-slice | bytes 573444 | tf_op jit(solution)/shard_map/slice | solution.py:60
  28.6 23.8 %collective-permute-done.4 = s32[384]{0:T(512)S(1)} collective-permute-done((s32[384]{0:T(512)}, s32[384]{0:T(512)S(1)}, u32[]{:S(2)}, u32[]{:S(2)}) %collective-permute-start.4) | collective-permute-done | bytes 1568 | tf_op jit(solution)/shard_map/ppermute | solution.py:16
  52.5 1.3 collective-permute-start.5
  53.8 0.2 and_reduce_fusion
  54.0 0.1 broadcast_in_dim.32
  54.1 4.4 %collective-permute-done.5 = s32[384]{0:T(512)S(1)} collective-permute-done((s32[384]{0:T(512)S(1)}, s32[384]{0:T(512)S(1)}, u32[]{:S(2)}, u32[]{:S(2)}) %collective-permute-start.5) | collective-permute-done | bytes 1568 | tf_op jit(solution)/shard_map/ppermute | solution.py:16
  58.5 0.2 pad_maximum_fusion.1
  58.7 1.4 pad_maximum_fusion.2
  60.1 1.5 fusion.49
  61.6 1.6 %fusion.48 = (f32[384]{0:T(512)S(1)}, f32[384,1152]{0,1:T(8,128)S(1)}) fusion(bf16[384,640]{1,0:T(8,128)(2,1)} %param.7, bf16[1152,640]{1,0:T(8,128)(2,1)S(1)} %bitcast.62, s32[1152]{0:T(1024)S(1)} %eq.89, s32[384]{0:T(512)S(1)} %copy-done.6, pred[1152]{0:T(1024)(128)(4,1)S(1)} %and.49), kind=kOutput, calls=%fused_computation.86 | convolution fusion | flops 115457664 | bytes 2176512 | tf_op jit(solution)/shard_map/dot_general | solution.py:32
  63.2 0.6 fusion.47
  63.8 0.6 fusion.46
  64.5 0.6 fusion.50
  65.1 1.4 collective-permute-start.9
  66.5 2.2 %fusion.17 = (f32[384]{0:T(512)S(1)}, f32[384]{0:T(512)S(1)}, f32[384]{0:T(512)S(1)}, f32[384]{0:T(512)S(1)}, f32[384]{0:T(512)S(1)}) fusion(f32[384,1152]{0,1:T(8,128)S(1)} %get-tuple-element.35, f32[384]{0:T(512)S(1)} %get-tuple-element.34, s32[384]{0:T(512)S(1)} %copy-done.6, s32[1152]{0:T(1024)S(1)} %eq.89, pred[1152]{0:T(1024)(128)(4,1)S(1)} %and.49, ...), kind=kLoop, calls=%fused_computation.39 | loop fusion | flops 7518336 | bytes 8870016 | tf_op jit(solution)/shard_map/reduce_sum | solution.py:38
  68.7 0.9 fusion.18
  69.7 0.9 fusion.19
  70.6 0.9 fusion.20
  71.5 0.9 fusion.21
  72.4 0.9 fusion.22
  73.4 1.6 %collective-permute-start.7 = (bf16[384,640]{0,1:T(8,128)(2,1)S(1)}, bf16[384,640]{0,1:T(8,128)(2,1)S(1)}, u32[]{:S(2)}, u32[]{:S(2)}) collective-permute-start(bf16[384,640]{0,1:T(8,128)(2,1)S(1)} %fusion.22), channel_id=1, source_target_pairs={{0,2},{1,3},{2,0},{3,1},{4,6},{5,7},{6,4},{7,5},{8,10},{9,11},{10,... | collective-permute-start | bytes 1474568 | tf_op jit(solution)/shard_map/ppermute | solution.py:115
  75.0 0.2 collective-permute-start.8
  75.2 10.9 %all-gather.6.cloned.1.call-done = bf16[832,640]{1,0:T(8,128)(2,1)} async-done(((bf16[208,640]{1,0:T(8,128)(2,1)}), bf16[832,640]{1,0:T(8,128)(2,1)}) %all-gather.6.cloned.1.call-update) | async-done | bytes 1064976 | tf_op jit(solution)/shard_map/all_gather | solution.py:60
  86.1 1.9 %collective-permute-done.9 = bf16[832,640]{1,0:T(8,128)(2,1)S(1)} collective-permute-done((bf16[832,640]{1,0:T(8,128)(2,1)}, bf16[832,640]{1,0:T(8,128)(2,1)S(1)}, u32[]{:S(2)}, u32[]{:S(2)}) %collective-permute-start.9) | collective-permute-done | bytes 1064992 | tf_op jit(solution)/shard_map/ppermute | solution.py:83
  88.0 1.7 %collective-permute-start.10 = (bf16[832,640]{1,0:T(8,128)(2,1)}, bf16[832,640]{1,0:T(8,128)(2,1)}, u32[]{:S(2)}, u32[]{:S(2)}) collective-permute-start(bf16[832,640]{1,0:T(8,128)(2,1)} %all-gather.6.cloned.1.call-done), channel_id=1, source_target_pairs={{0,16},{16,0},{1,17},{17,1},{2,18},{18,2},{3,19},{19,3},{4,20},{20... | collective-permute-start | bytes 3194888 | tf_op jit(solution)/shard_map/ppermute | solution.py:109
  89.6 7.9 %collective-permute-done.7 = bf16[384,640]{0,1:T(8,128)(2,1)S(1)} collective-permute-done((bf16[384,640]{0,1:T(8,128)(2,1)S(1)}, bf16[384,640]{0,1:T(8,128)(2,1)S(1)}, u32[]{:S(2)}, u32[]{:S(2)}) %collective-permute-start.7) | collective-permute-done | bytes 491552 | tf_op jit(solution)/shard_map/ppermute | solution.py:115
  97.5 0.1 collective-permute-done.8
  97.6 0.3 select_select_fusion.3
  97.9 0.2 pad_maximum_fusion
  98.1 0.1 slice.96
  98.2 0.1 fusion.44
  98.3 18.4 %all-gather.8.cloned.1.call-done = bf16[896,640]{1,0:T(8,128)(2,1)} async-done(((bf16[224,640]{1,0:T(8,128)(2,1)}), bf16[896,640]{1,0:T(8,128)(2,1)}) %all-gather.8.cloned.1.call-update) | async-done | bytes 1146896 | tf_op jit(solution)/shard_map/all_gather | solution.py:60
  116.7 1.5 collective-permute-start.11
  118.2 2.0 %fusion.51 = f32[384,640]{1,0:T(8,128)S(1)} fusion(bf16[384,832]{0,1:T(8,128)(2,1)S(1)} %bitcast.54, bf16[832,640]{1,0:T(8,128)(2,1)} %all-gather.4.cloned.1.call-done), kind=kOutput, calls=%fused_computation.89 | convolution fusion | flops 408944640 | bytes 2686976 | tf_op jit(solution)/shard_map/dot_general | solution.py:129
  120.2 0.8 convolution_add_fusion.2
  121.0 2.1 %fusion.52 = f32[384,640]{1,0:T(8,128)S(1)} fusion(bf16[384,832]{0,1:T(8,128)(2,1)S(1)} %bitcast.53, bf16[832,640]{1,0:T(8,128)(2,1)} %collective-permute-done.10), kind=kOutput, calls=%fused_computation.90 | convolution fusion | flops 408944640 | bytes 2686976 | tf_op jit(solution)/shard_map/dot_general | solution.py:130
  123.1 0.8 fusion.11
  123.9 19.8 %collective-permute-done.11 = bf16[896,640]{1,0:T(8,128)(2,1)S(1)} collective-permute-done((bf16[896,640]{1,0:T(8,128)(2,1)}, bf16[896,640]{1,0:T(8,128)(2,1)S(1)}, u32[]{:S(2)}, u32[]{:S(2)}) %collective-permute-start.11) | collective-permute-done | bytes 1146912 | tf_op jit(solution)/shard_map/ppermute | solution.py:109
  143.7 0.8 fusion.53
  144.5 0.8 fusion.12
  145.3 1.2 maximum_select_fusion
  (42 shorter events, 0.4 us)
Async XLA Ops:
  6.5 22.0 %copy-start.9 = (s32[3]{0:T(128)S(1)}, s32[3]{0:T(128)}, u32[]{:S(2)}) copy-start(s32[3]{0:T(128)} %constant.86) | copy-start | bytes 40
  6.5 51.9 %copy-start.4 = (bf16[384,640]{1,0:T(8,128)(2,1)S(1)}, bf16[384,640]{1,0:T(8,128)(2,1)}, u32[]{:S(2)}) copy-start(bf16[384,640]{1,0:T(8,128)(2,1)} %param.8) | copy-start | bytes 1474564
  6.5 45.9 %copy-start.6 = (s32[384]{0:T(512)S(1)}, s32[384]{0:T(512)}, u32[]{:S(2)}) copy-start(s32[384]{0:T(512)} %param.12) | copy-start | bytes 4612
  6.5 22.1 %copy-start.8 = (s32[4,27]{1,0:T(4,128)S(1)}, s32[4,27]{1,0:T(4,128)}, u32[]{:S(2)}) copy-start(s32[4,27]{1,0:T(4,128)} %param.11) | copy-start | bytes 1300
  6.5 53.5 %all-gather.4.cloned.1.call-start = ((), (), s32[]{:S(2)}) async-start(), calls=%async_computation | async-start | bytes 1331200 | tf_op jit(solution)/shard_map/all_gather | solution.py:60
  8.6 77.5 %all-gather.6.cloned.1.call-start = ((), (), s32[]{:S(2)}) async-start(), calls=%async_computation.1 | async-start | bytes 1331200 | tf_op jit(solution)/shard_map/all_gather | solution.py:60
  9.3 107.4 %all-gather.8.cloned.1.call-start = ((), (), s32[]{:S(2)}) async-start(), calls=%async_computation.2 | async-start | bytes 1433600 | tf_op jit(solution)/shard_map/all_gather | solution.py:60
  9.4 49.1 %collective-permute-start = (bf16[384,640]{1,0:T(8,128)(2,1)}, bf16[384,640]{1,0:T(8,128)(2,1)S(1)}, u32[]{:S(2)}, u32[]{:S(2)}) collective-permute-start(bf16[384,640]{1,0:T(8,128)(2,1)} %param.8), channel_id=1, source_target_pairs={{0,4},{4,8},{8,12},{1,5},{5,9},{9,13},{2,6},{6,10},{10,14},{3,7},{... | collective-permute-start | bytes 1474568 | tf_op jit(solution)/shard_map/ppermute | solution.py:16
  14.3 44.1 %collective-permute-start.1 = (bf16[384,640]{1,0:T(8,128)(2,1)}, bf16[384,640]{1,0:T(8,128)(2,1)S(1)}, u32[]{:S(2)}, u32[]{:S(2)}) collective-permute-start(bf16[384,640]{1,0:T(8,128)(2,1)} %param.8), channel_id=1, source_target_pairs={{4,0},{8,4},{12,8},{5,1},{9,5},{13,9},{6,2},{10,6},{14,10},{7,3},{... | collective-permute-start | bytes 1474568 | tf_op jit(solution)/shard_map/ppermute | solution.py:16
  15.6 43.0 %collective-permute-start.2 = (bf16[384,640]{1,0:T(8,128)(2,1)}, bf16[384,640]{1,0:T(8,128)(2,1)}, u32[]{:S(2)}, u32[]{:S(2)}) collective-permute-start(bf16[384,640]{1,0:T(8,128)(2,1)} %param.9), channel_id=1, source_target_pairs={{0,4},{4,8},{8,12},{1,5},{5,9},{9,13},{2,6},{6,10},{10,14},{3,7},{... | collective-permute-start | bytes 1474568 | tf_op jit(solution)/shard_map/ppermute | solution.py:16
  21.0 37.7 %collective-permute-start.3 = (bf16[384,640]{1,0:T(8,128)(2,1)}, bf16[384,640]{1,0:T(8,128)(2,1)}, u32[]{:S(2)}, u32[]{:S(2)}) collective-permute-start(bf16[384,640]{1,0:T(8,128)(2,1)} %param.9), channel_id=1, source_target_pairs={{4,0},{8,4},{12,8},{5,1},{9,5},{13,9},{6,2},{10,6},{14,10},{7,3},{... | collective-permute-start | bytes 1474568 | tf_op jit(solution)/shard_map/ppermute | solution.py:16
  22.3 30.2 %collective-permute-start.4 = (s32[384]{0:T(512)}, s32[384]{0:T(512)S(1)}, u32[]{:S(2)}, u32[]{:S(2)}) collective-permute-start(s32[384]{0:T(512)} %param.12), channel_id=1, source_target_pairs={{0,4},{4,8},{8,12},{1,5},{5,9},{9,13},{2,6},{6,10},{10,14},{3,7},{... | collective-permute-start | bytes 4616 | tf_op jit(solution)/shard_map/ppermute | solution.py:16
  28.5 30.1 %copy-start.5 = (bf16[384,640]{1,0:T(8,128)(2,1)S(1)}, bf16[384,640]{1,0:T(8,128)(2,1)}, u32[]{:S(2)}) copy-start(bf16[384,640]{1,0:T(8,128)(2,1)} %param.9) | copy-start | bytes 1474564
  52.5 5.9 %collective-permute-start.5 = (s32[384]{0:T(512)S(1)}, s32[384]{0:T(512)S(1)}, u32[]{:S(2)}, u32[]{:S(2)}) collective-permute-start(s32[384]{0:T(512)S(1)} %copy-done.6), channel_id=1, source_target_pairs={{4,0},{8,4},{12,8},{5,1},{9,5},{13,9},{6,2},{10,6},{14,10},{7,3},{... | collective-permute-start | bytes 4616 | tf_op jit(solution)/shard_map/ppermute | solution.py:16
  61.6 1.6 %copy-start.7 = (bf16[384,640]{1,0:T(8,128)(2,1)S(1)}, bf16[384,640]{1,0:T(8,128)(2,1)}, u32[]{:S(2)}) copy-start(bf16[384,640]{1,0:T(8,128)(2,1)} %param.7) | copy-start | bytes 1474564
  65.1 22.9 %collective-permute-start.9 = (bf16[832,640]{1,0:T(8,128)(2,1)}, bf16[832,640]{1,0:T(8,128)(2,1)S(1)}, u32[]{:S(2)}, u32[]{:S(2)}) collective-permute-start(bf16[832,640]{1,0:T(8,128)(2,1)} %all-gather.4.cloned.1.call-done), channel_id=1, source_target_pairs={{0,16},{16,0},{1,17},{17,1},{2,18},{18,2},{3,19},{19,3},{4,20},{20... | collective-permute-start | bytes 3194888 | tf_op jit(solution)/shard_map/ppermute | solution.py:83
  73.4 16.3 %collective-permute-start.6 = (bf16[384,640]{0,1:T(8,128)(2,1)S(1)}, bf16[384,640]{0,1:T(8,128)(2,1)S(1)}, u32[]{:S(2)}, u32[]{:S(2)}) collective-permute-start(bf16[384,640]{0,1:T(8,128)(2,1)S(1)} %fusion.22), channel_id=1, source_target_pairs={{0,3},{1,0},{2,1},{3,2},{4,7},{5,4},{6,5},{7,6},{8,11},{9,8},{10,9... | collective-permute-start | bytes 1474568 | tf_op jit(solution)/shard_map/ppermute | solution.py:115
  73.4 24.0 %collective-permute-start.7 = (bf16[384,640]{0,1:T(8,128)(2,1)S(1)}, bf16[384,640]{0,1:T(8,128)(2,1)S(1)}, u32[]{:S(2)}, u32[]{:S(2)}) collective-permute-start(bf16[384,640]{0,1:T(8,128)(2,1)S(1)} %fusion.22), channel_id=1, source_target_pairs={{0,2},{1,3},{2,0},{3,1},{4,6},{5,7},{6,4},{7,5},{8,10},{9,11},{10,... | collective-permute-start | bytes 1474568 | tf_op jit(solution)/shard_map/ppermute | solution.py:115
  75.0 22.5 %collective-permute-start.8 = (bf16[384,640]{0,1:T(8,128)(2,1)S(1)}, bf16[384,640]{0,1:T(8,128)(2,1)S(1)}, u32[]{:S(2)}, u32[]{:S(2)}) collective-permute-start(bf16[384,640]{0,1:T(8,128)(2,1)S(1)} %fusion.22), channel_id=1, source_target_pairs={{0,1},{1,2},{2,3},{3,0},{4,5},{5,6},{6,7},{7,4},{8,9},{9,10},{10,1... | collective-permute-start | bytes 1474568 | tf_op jit(solution)/shard_map/ppermute | solution.py:115
  88.0 9.9 %copy-start.2 = (bf16[832,640]{1,0:T(8,128)(2,1)}, bf16[832,640]{1,0:T(8,128)(2,1)S(1)}, u32[]{:S(2)}) copy-start(bf16[832,640]{1,0:T(8,128)(2,1)S(1)} %collective-permute-done.9) | copy-start | bytes 3194884
  88.0 28.8 %collective-permute-start.10 = (bf16[832,640]{1,0:T(8,128)(2,1)}, bf16[832,640]{1,0:T(8,128)(2,1)}, u32[]{:S(2)}, u32[]{:S(2)}) collective-permute-start(bf16[832,640]{1,0:T(8,128)(2,1)} %all-gather.6.cloned.1.call-done), channel_id=1, source_target_pairs={{0,16},{16,0},{1,17},{17,1},{2,18},{18,2},{3,19},{19,3},{4,20},{20... | collective-permute-start | bytes 3194888 | tf_op jit(solution)/shard_map/ppermute | solution.py:109
  98.3 21.9 %copy-start.1 = (bf16[832,640]{1,0:T(8,128)(2,1)S(1)}, bf16[832,640]{1,0:T(8,128)(2,1)}, u32[]{:S(2)}) copy-start(bf16[832,640]{1,0:T(8,128)(2,1)} %all-gather.6.cloned.1.call-done) | copy-start | bytes 3194884
  116.7 27.0 %collective-permute-start.11 = (bf16[896,640]{1,0:T(8,128)(2,1)}, bf16[896,640]{1,0:T(8,128)(2,1)S(1)}, u32[]{:S(2)}, u32[]{:S(2)}) collective-permute-start(bf16[896,640]{1,0:T(8,128)(2,1)} %all-gather.8.cloned.1.call-done), channel_id=1, source_target_pairs={{0,16},{16,0},{1,17},{17,1},{2,18},{18,2},{3,19},{19,3},{4,20},{20... | collective-permute-start | bytes 3440648 | tf_op jit(solution)/shard_map/ppermute | solution.py:109
  121.0 2.1 %copy-start = (bf16[896,640]{1,0:T(8,128)(2,1)S(1)}, bf16[896,640]{1,0:T(8,128)(2,1)}, u32[]{:S(2)}) copy-start(bf16[896,640]{1,0:T(8,128)(2,1)} %all-gather.8.cloned.1.call-done) | copy-start | bytes 3440644
  123.9 20.6 %copy-start.3 = (bf16[832,640]{1,0:T(8,128)(2,1)S(1)}, bf16[832,640]{1,0:T(8,128)(2,1)}, u32[]{:S(2)}) copy-start(bf16[832,640]{1,0:T(8,128)(2,1)} %copy-done.2) | copy-start | bytes 3194884
Sparse Core Ops, SparseCore 0:
  8.9 43.8 all-gather.3
  54.4 31.6 all-gather.5
  87.6 29.0 all-gather.7

commit v6 on v0

--- a/solution.py
+++ b/solution.py
@@ -8,12 +8,21 @@
 HD = 128
 TGH = 4
 TGW = 7
+LINE_LIMIT = 4
 
 
 def from_behind(value, axis, by):
     peers = lax.axis_size(axis)
     pairs = [(i, i + by) for i in range(peers) if 0 <= i + by < peers]
     return lax.ppermute(value, axis, pairs)
+
+
+def to_twin(value, seq_count, valid_positions):
+    pairs = []
+    for rep_index in (0, 1):
+        for seq_index in valid_positions:
+            pairs.append((rep_index * seq_count + seq_index, (1 - rep_index) * seq_count + seq_index))
+    return lax.ppermute(value, ("rep", "seq"), pairs)
 
 
 def attend_head(query_head, key_head, value_head, allowed):
@@ -28,10 +37,30 @@
     return jnp.dot(weights, value_head, preferred_element_type=jnp.float32).astype(jnp.bfloat16)
 
 
+def exchange_heads(attended):
+    head_count = lax.axis_size("head")
+    head_position = lax.axis_index("head")
+    received = [attended]
+    for shift in range(1, head_count):
+        pairs = [(j, (j + shift) % head_count) for j in range(head_count)]
+        received.append(lax.ppermute(attended, "head", pairs))
+    ordered = []
+    for group in range(head_count):
+        block = received[0]
+        for shift in range(1, head_count):
+            block = jnp.where((head_position - shift) % head_count == group, received[shift], block)
+        ordered.append(block)
+    return jnp.concatenate(ordered, axis=1)
+
+
 def on_device(queries, keys, values, out_weight, neighbours, clip_ids):
     tile_rows = queries.shape[0]
     feature_width = queries.shape[1]
     seq_count = lax.axis_size("seq")
+    position = lax.axis_index("seq")
+    rep_position = lax.axis_index("rep")
+    block_rows = out_weight.shape[0]
+    line_path = seq_count <= LINE_LIMIT and lax.axis_size("rep") == 2
     layer_tiles = TGH * TGW
     every_offset = set()
     for layer_step in (-1, 0, 1):
@@ -39,6 +68,18 @@
             for col_step in (-1, 0, 1):
                 every_offset.add(layer_step * layer_tiles + row_step * TGW + col_step)
     distances = [offset for offset in sorted(every_offset) if 0 < offset < seq_count]
+
+    if line_path:
+        half_width = out_weight.shape[1] // 2
+        own_half = lax.dynamic_slice_in_dim(out_weight, rep_position * half_width, half_width, axis=1)
+        other_half = lax.dynamic_slice_in_dim(
+            out_weight, (1 - rep_position) * half_width, half_width, axis=1
+        )
+        from_left = from_behind(own_half, "seq", 1)
+        from_right = from_behind(own_half, "seq", -1)
+    else:
+        weight_piece = lax.all_gather(out_weight, "seq", axis=0, tiled=True)
+
     key_list = [keys]
     value_list = [values]
     clip_list = [clip_ids]
@@ -57,8 +98,16 @@
     key_stack = jnp.stack(key_list)
     value_stack = jnp.stack(value_list)
     clip_stack = jnp.stack(clip_list)
+
+    arrivals = []
+    if line_path:
+        from_left, from_right, key_stack, value_stack, clip_stack = lax.optimization_barrier(
+            (from_left, from_right, key_stack, value_stack, clip_stack)
+        )
+        arrivals.append((-1, from_left, to_twin(from_left, seq_count, range(1, seq_count))))
+        arrivals.append((1, from_right, to_twin(from_right, seq_count, range(seq_count - 1))))
+
     blocks = key_stack.shape[0]
-    position = lax.axis_index("seq")
     window_row = lax.dynamic_index_in_dim(neighbours, position, 0, keepdims=False)
     sources = position - jnp.asarray(offsets, dtype=jnp.int32)
     present = jnp.any(
@@ -80,12 +129,50 @@
             )
         )
     attended = jnp.concatenate(head_outputs, axis=1)
-    all_features = lax.all_gather(attended, "head", axis=1, tiled=True)
-    empty = jnp.zeros((tile_rows, out_weight.shape[1]), jnp.float32)
-    weight_piece = lax.all_gather(out_weight, "seq", axis=0, tiled=True)
-    features = lax.slice_in_dim(all_features, 0, weight_piece.shape[0], axis=1)
-    projected = empty + jnp.dot(features, weight_piece, preferred_element_type=jnp.float32)
-    return projected.astype(jnp.bfloat16)
+
+    if not line_path:
+        features = exchange_heads(attended)
+        projected = jnp.dot(
+            lax.slice_in_dim(features, 0, weight_piece.shape[0], axis=1),
+            weight_piece,
+            preferred_element_type=jnp.float32,
+        )
+        return projected.astype(jnp.bfloat16)
+
+    for step in range(2, seq_count):
+        from_left = from_behind(from_left, "seq", 1)
+        from_right = from_behind(from_right, "seq", -1)
+        if step == seq_count - 1:
+            twins = [twin for _, _, twin in arrivals]
+            from_left, from_right, attended, twins = lax.optimization_barrier(
+                (from_left, from_right, attended, twins)
+            )
+            arrivals = [(a, b, twin) for (a, b, _), twin in zip(arrivals, twins)]
+        else:
+            from_left, from_right, attended = lax.optimization_barrier(
+                (from_left, from_right, attended)
+            )
+        arrivals.append((-step, from_left, to_twin(from_left, seq_count, range(step, seq_count))))
+        arrivals.append(
+            (step, from_right, to_twin(from_right, seq_count, range(seq_count - step)))
+        )
+
+    features = exchange_heads(attended)
+    own_rows = lax.dynamic_slice_in_dim(features, position * block_rows, block_rows, axis=1)
+    own_sum = jnp.dot(own_rows, own_half, preferred_element_type=jnp.float32)
+    other_sum = jnp.dot(own_rows, other_half, preferred_element_type=jnp.float32)
+    for step, own_block, twin_block in arrivals:
+        source = jnp.clip(position + step, 0, seq_count - 1)
+        rows = lax.dynamic_slice_in_dim(features, source * block_rows, block_rows, axis=1)
+        own_sum = own_sum + jnp.dot(rows, own_block, preferred_element_type=jnp.float32)
+        other_sum = other_sum + jnp.dot(rows, twin_block, preferred_element_type=jnp.float32)
+    own_out = own_sum.astype(jnp.bfloat16)
+    other_out = other_sum.astype(jnp.bfloat16)
+    return jnp.where(
+        rep_position == 0,
+        jnp.concatenate([own_out, other_out], axis=1),
+        jnp.concatenate([other_out, own_out], axis=1),
+    )
 
 
 def solution(mesh):

time: 208 us -> 163 us (0.78)
  the two profiles are of different devices: /device:TPU:0 before, /device:TPU:8 now
where the time goes in v6:
time: 163 us; the launch traced here: 162 us
  waiting for transfers between devices  75.4 us (46%)
  starting transfers between devices  45.8 us (28%)
  matrix products  24.2 us (15%)
  other arithmetic  12.2 us (7%)
  local copies, waits for them, and re-layouts  3.99 us (2%)
    ppermute x12, waiting for transfers between devices, from_behind(): return lax.ppermute(value, axis, pairs)  36 us
    ppermute x12, starting transfers between devices, from_behind(): return lax.ppermute(value, axis, pairs)  33.4 us
    ppermute x3, waiting for transfers between devices, exchange_heads(): received.append(lax.ppermute(attended, 'head', pairs))  21.1 us
    ppermute x6, waiting for transfers between devices, to_twin(): return lax.ppermute(value, ('rep', 'seq'), pairs)  18.4 us
    ppermute x6, starting transfers between devices, to_twin(): return lax.ppermute(value, ('rep', 'seq'), pairs)  10.6 us
    dot_general x5, matrix products, attend_head(): jnp.dot(weights, value_head, preferred_element_type=jnp.float32)  7.81 us
    dot_general x6, matrix products, on_device(): jnp.dot(rows, twin_block, preferred_element_type=jnp.float32)  5.03 us
    dot_general x6, matrix products, on_device(): jnp.dot(rows, own_block, preferred_element_type=jnp.float32)  5.02 us
  transfers between devices with their start and end apart: 21, of which 12 were waited for; matrix products, arithmetic and copies ran while one was open for 19% of the time, Pallas kernels for 0%

profile of v6, /device:TPU:8, one launch (start us, length us, event | category | flops | bytes accessed | tf_op | source)
XLA Modules:
  0.0 162.2 jit_solution(7152326705259527872)
XLA Ops:
  0.0 3.6 %collective-permute-start.2 = (bf16[384,640]{1,0:T(8,128)(2,1)}, bf16[384,640]{1,0:T(8,128)(2,1)}, u32[]{:S(2)}, u32[]{:S(2)}) collective-permute-start(bf16[384,640]{1,0:T(8,128)(2,1)} %param.8), channel_id=1, source_target_pairs={{0,4},{4,8},{8,12},{1,5},{5,9},{9,13},{2,6},{6,10},{10,14},{3,7},{... | collective-permute-start | bytes 1474568 | tf_op jit(solution)/shard_map/ppermute | solution.py:17
  3.6 3.5 %collective-permute-start.6 = (s32[384]{0:T(512)}, s32[384]{0:T(512)S(1)}, u32[]{:S(2)}, u32[]{:S(2)}) collective-permute-start(s32[384]{0:T(512)} %param.12), channel_id=1, source_target_pairs={{0,4},{4,8},{8,12},{1,5},{5,9},{9,13},{2,6},{6,10},{10,14},{3,7},{... | collective-permute-start | bytes 4616 | tf_op jit(solution)/shard_map/ppermute | solution.py:17
  7.2 1.9 %collective-permute-start = (bf16[640,640]{1,0:T(8,128)(2,1)S(1)}, bf16[640,640]{1,0:T(8,128)(2,1)S(1)}, u32[]{:S(2)}, u32[]{:S(2)}) collective-permute-start(bf16[640,640]{1,0:T(8,128)(2,1)S(1)} %constant_dynamic-slice_fusion.1), channel_id=1, source_target_pairs={{0,4},{4,8},{8,12},{1,5},{5,9},{9,13},{2,6},{6,10},{10,14},{3,7},{... | collective-permute-start | bytes 2457608 | tf_op jit(solution)/shard_map/ppermute | solution.py:17
  9.1 4.0 %collective-permute-start.1 = (bf16[640,640]{1,0:T(8,128)(2,1)S(1)}, bf16[640,640]{1,0:T(8,128)(2,1)}, u32[]{:S(2)}, u32[]{:S(2)}) collective-permute-start(bf16[640,640]{1,0:T(8,128)(2,1)S(1)} %constant_dynamic-slice_fusion.1), channel_id=1, source_target_pairs={{4,0},{8,4},{12,8},{5,1},{9,5},{13,9},{6,2},{10,6},{14,10},{7,3},{... | collective-permute-start | bytes 2457608 | tf_op jit(solution)/shard_map/ppermute | solution.py:17
  13.1 1.9 %collective-permute-start.3 = (bf16[384,640]{1,0:T(8,128)(2,1)}, bf16[384,640]{1,0:T(8,128)(2,1)}, u32[]{:S(2)}, u32[]{:S(2)}) collective-permute-start(bf16[384,640]{1,0:T(8,128)(2,1)} %param.8), channel_id=1, source_target_pairs={{4,0},{8,4},{12,8},{5,1},{9,5},{13,9},{6,2},{10,6},{14,10},{7,3},{... | collective-permute-start | bytes 1474568 | tf_op jit(solution)/shard_map/ppermute | solution.py:17
  15.1 1.4 collective-permute-done.6
  16.4 1.9 %collective-permute-start.7 = (s32[384]{0:T(512)}, s32[384]{0:T(512)S(1)}, u32[]{:S(2)}, u32[]{:S(2)}) collective-permute-start(s32[384]{0:T(512)} %param.12), channel_id=1, source_target_pairs={{4,0},{8,4},{12,8},{5,1},{9,5},{13,9},{6,2},{10,6},{14,10},{7,3},{... | collective-permute-start | bytes 4616 | tf_op jit(solution)/shard_map/ppermute | solution.py:17
  19.0 22.1 %collective-permute-done.7 = s32[384]{0:T(512)S(1)} collective-permute-done((s32[384]{0:T(512)}, s32[384]{0:T(512)S(1)}, u32[]{:S(2)}, u32[]{:S(2)}) %collective-permute-start.7) | collective-permute-done | bytes 1568 | tf_op jit(solution)/shard_map/ppermute | solution.py:17
  41.1 2.2 %collective-permute-start.4 = (bf16[384,640]{1,0:T(8,128)(2,1)}, bf16[384,640]{1,0:T(8,128)(2,1)}, u32[]{:S(2)}, u32[]{:S(2)}) collective-permute-start(bf16[384,640]{1,0:T(8,128)(2,1)} %param.9), channel_id=1, source_target_pairs={{0,4},{4,8},{8,12},{1,5},{5,9},{9,13},{2,6},{6,10},{10,14},{3,7},{... | collective-permute-start | bytes 1474568 | tf_op jit(solution)/shard_map/ppermute | solution.py:17
  43.3 4.4 %collective-permute-start.5 = (bf16[384,640]{1,0:T(8,128)(2,1)}, bf16[384,640]{1,0:T(8,128)(2,1)}, u32[]{:S(2)}, u32[]{:S(2)}) collective-permute-start(bf16[384,640]{1,0:T(8,128)(2,1)} %param.9), channel_id=1, source_target_pairs={{4,0},{8,4},{12,8},{5,1},{9,5},{13,9},{6,2},{10,6},{14,10},{7,3},{... | collective-permute-start | bytes 1474568 | tf_op jit(solution)/shard_map/ppermute | solution.py:17
  47.8 0.7 compare_bitcast_fusion
  49.1 0.7 fusion.88
  50.2 2.7 %pad_maximum_fusion.1 = bf16[3,384,640]{2,1,0:T(8,128)(2,1)} fusion(bf16[1,384,640]{2,1,0:T(8,128)(2,1)} %bitcast.2, bf16[1,384,640]{2,1,0:T(8,128)(2,1)} %bitcast.1, bf16[1,384,640]{2,1,0:T(8,128)(2,1)} %bitcast.55), kind=kLoop, calls=%fused_computation.27 | loop fusion | flops 1474560 | bytes 2949120 | tf_op jit(solution)/shard_map/stack | solution.py:98
  52.8 2.0 %collective-permute-done.4 = bf16[384,640]{1,0:T(8,128)(2,1)} collective-permute-done((bf16[384,640]{1,0:T(8,128)(2,1)}, bf16[384,640]{1,0:T(8,128)(2,1)}, u32[]{:S(2)}, u32[]{:S(2)}) %collective-permute-start.4) | collective-permute-done | bytes 491552 | tf_op jit(solution)/shard_map/ppermute | solution.py:17
  54.8 2.2 %collective-permute-done.5 = bf16[384,640]{1,0:T(8,128)(2,1)} collective-permute-done((bf16[384,640]{1,0:T(8,128)(2,1)}, bf16[384,640]{1,0:T(8,128)(2,1)}, u32[]{:S(2)}, u32[]{:S(2)}) %collective-permute-start.5) | collective-permute-done | bytes 491552 | tf_op jit(solution)/shard_map/ppermute | solution.py:17
  57.1 2.5 %pad_maximum_fusion.2 = bf16[3,384,640]{2,1,0:T(8,128)(2,1)} fusion(bf16[1,384,640]{2,1,0:T(8,128)(2,1)} %bitcast.5, bf16[1,384,640]{2,1,0:T(8,128)(2,1)} %bitcast.4, bf16[1,384,640]{2,1,0:T(8,128)(2,1)S(1)} %bitcast.56), kind=kLoop, calls=%fused_computation.28 | loop fusion | flops 1474560 | bytes 2949120 | tf_op jit(solution)/shard_map/stack | solution.py:99
  59.6 2.2 %fusion.97 = (f32[384]{0:T(512)S(1)}, f32[384,1152]{0,1:T(8,128)S(1)}) fusion(bf16[384,640]{1,0:T(8,128)(2,1)} %param.7, bf16[1152,640]{1,0:T(8,128)(2,1)} %bitcast.50, s32[1152]{0:T(1024)S(1)} %eq.89, s32[384]{0:T(512)S(1)} %copy-done.18, pred[1152]{0:T(1024)(128)(4,1)S(1)} %and.49), kind=kOutput, calls=%fused_computation.134 | convolution fusion | flops 115457664 | bytes 2171520 | tf_op jit(solution)/shard_map/dot_general | solution.py:29
  64.3 2.2 %collective-permute-start.8 = (bf16[640,640]{1,0:T(8,128)(2,1)S(1)}, bf16[640,640]{1,0:T(8,128)(2,1)S(1)}, u32[]{:S(2)}, u32[]{:S(2)}) collective-permute-start(bf16[640,640]{1,0:T(8,128)(2,1)S(1)} %collective-permute-done), channel_id=1, source_target_pairs={{0,4},{4,8},{8,12},{1,5},{5,9},{9,13},{2,6},{6,10},{10,14},{3,7},{... | collective-permute-start | bytes 2457608 | tf_op jit(solution)/shard_map/ppermute | solution.py:17
  66.5 3.4 %collective-permute-start.12 = (bf16[640,640]{1,0:T(8,128)(2,1)S(1)}, bf16[640,640]{1,0:T(8,128)(2,1)S(1)}, u32[]{:S(2)}, u32[]{:S(2)}) collective-permute-start(bf16[640,640]{1,0:T(8,128)(2,1)S(1)} %collective-permute-done), channel_id=1, source_target_pairs={{4,20},{8,24},{12,28},{20,4},{24,8},{28,12},{5,21},{9,25},{13,29},... | collective-permute-start | bytes 2457608 | tf_op jit(solution)/shard_map/ppermute | solution.py:25
  70.0 1.9 %collective-permute-start.9 = (bf16[640,640]{1,0:T(8,128)(2,1)}, bf16[640,640]{1,0:T(8,128)(2,1)S(1)}, u32[]{:S(2)}, u32[]{:S(2)}) collective-permute-start(bf16[640,640]{1,0:T(8,128)(2,1)} %collective-permute-done.1), channel_id=1, source_target_pairs={{4,0},{8,4},{12,8},{5,1},{9,5},{13,9},{6,2},{10,6},{14,10},{7,3},{... | collective-permute-start | bytes 2457608 | tf_op jit(solution)/shard_map/ppermute | solution.py:17
  71.9 2.5 %collective-permute-start.13 = (bf16[640,640]{1,0:T(8,128)(2,1)}, bf16[640,640]{1,0:T(8,128)(2,1)}, u32[]{:S(2)}, u32[]{:S(2)}) collective-permute-start(bf16[640,640]{1,0:T(8,128)(2,1)} %collective-permute-done.1), channel_id=1, source_target_pairs={{0,16},{4,20},{8,24},{16,0},{20,4},{24,8},{1,17},{5,21},{9,25},{17... | collective-permute-start | bytes 2457608 | tf_op jit(solution)/shard_map/ppermute | solution.py:25
  74.4 2.3 %fusion.26 = (f32[384]{0:T(512)S(1)}, f32[384]{0:T(512)S(1)}, f32[384]{0:T(512)S(1)}, f32[384]{0:T(512)S(1)}, f32[384]{0:T(512)S(1)}) fusion(f32[384,1152]{0,1:T(8,128)S(1)} %get-tuple-element.45, f32[384]{0:T(512)S(1)} %get-tuple-element.44, s32[384]{0:T(512)S(1)} %copy-done.18, s32[1152]{0:T(1024)S(1)} %eq.89, pred[1152]{0:T(1024)(128)(4,1)S(1)} %and.49, ...), kind=kLoop, calls=%fused_computation.47 | loop fusion | flops 7518336 | bytes 8870016 | tf_op jit(solution)/shard_map/reduce_sum | solution.py:35
  76.7 1.6 fusion.27
  78.3 1.6 fusion.28
  79.8 1.6 fusion.29
  81.4 1.6 fusion.30
  82.9 1.6 fusion.31
  84.5 4.9 %collective-permute-done.9 = bf16[640,640]{1,0:T(8,128)(2,1)S(1)} collective-permute-done((bf16[640,640]{1,0:T(8,128)(2,1)}, bf16[640,640]{1,0:T(8,128)(2,1)S(1)}, u32[]{:S(2)}, u32[]{:S(2)}) %collective-permute-start.9) | collective-permute-done | bytes 819232 | tf_op jit(solution)/shard_map/ppermute | solution.py:17
  89.4 2.2 %collective-permute-start.10 = (bf16[640,640]{1,0:T(8,128)(2,1)S(1)}, bf16[640,640]{1,0:T(8,128)(2,1)S(1)}, u32[]{:S(2)}, u32[]{:S(2)}) collective-permute-start(bf16[640,640]{1,0:T(8,128)(2,1)S(1)} %collective-permute-done.8), channel_id=1, source_target_pairs={{0,4},{4,8},{8,12},{1,5},{5,9},{9,13},{2,6},{6,10},{10,14},{3,7},{... | collective-permute-start | bytes 2457608 | tf_op jit(solution)/shard_map/ppermute | solution.py:17
  91.6 0.7 collective-permute-start.14
  92.3 3.7 %collective-permute-start.11 = (bf16[640,640]{1,0:T(8,128)(2,1)S(1)}, bf16[640,640]{1,0:T(8,128)(2,1)S(1)}, u32[]{:S(2)}, u32[]{:S(2)}) collective-permute-start(bf16[640,640]{1,0:T(8,128)(2,1)S(1)} %collective-permute-done.9), channel_id=1, source_target_pairs={{4,0},{8,4},{12,8},{5,1},{9,5},{13,9},{6,2},{10,6},{14,10},{7,3},{... | collective-permute-start | bytes 2457608 | tf_op jit(solution)/shard_map/ppermute | solution.py:17
  96.0 0.9 copy-done.3
  97.0 2.4 %collective-permute-start.15 = (bf16[640,640]{1,0:T(8,128)(2,1)S(1)}, bf16[640,640]{1,0:T(8,128)(2,1)S(1)}, u32[]{:S(2)}, u32[]{:S(2)}) collective-permute-start(bf16[640,640]{1,0:T(8,128)(2,1)S(1)} %collective-permute-done.9), channel_id=1, source_target_pairs={{0,16},{4,20},{16,0},{20,4},{1,17},{5,21},{17,1},{21,5},{2,18},{6,... | collective-permute-start | bytes 2457608 | tf_op jit(solution)/shard_map/ppermute | solution.py:25
  99.4 7.9 %collective-permute-done.13 = bf16[640,640]{1,0:T(8,128)(2,1)} collective-permute-done((bf16[640,640]{1,0:T(8,128)(2,1)}, bf16[640,640]{1,0:T(8,128)(2,1)}, u32[]{:S(2)}, u32[]{:S(2)}) %collective-permute-start.13) | collective-permute-done | bytes 819232 | tf_op jit(solution)/shard_map/ppermute | solution.py:25
  107.7 2.9 %collective-permute-done.11 = bf16[640,640]{1,0:T(8,128)(2,1)S(1)} collective-permute-done((bf16[640,640]{1,0:T(8,128)(2,1)S(1)}, bf16[640,640]{1,0:T(8,128)(2,1)S(1)}, u32[]{:S(2)}, u32[]{:S(2)}) %collective-permute-start.11) | collective-permute-done | bytes 819232 | tf_op jit(solution)/shard_map/ppermute | solution.py:17
  110.7 10.5 %collective-permute-done.15 = bf16[640,640]{1,0:T(8,128)(2,1)S(1)} collective-permute-done((bf16[640,640]{1,0:T(8,128)(2,1)S(1)}, bf16[640,640]{1,0:T(8,128)(2,1)S(1)}, u32[]{:S(2)}, u32[]{:S(2)}) %collective-permute-start.15) | collective-permute-done | bytes 819232 | tf_op jit(solution)/shard_map/ppermute | solution.py:25
  121.2 1.6 collective-permute-start.17
  122.9 0.7 collective-permute-start.19
  123.6 0.9 collective-permute-start.20
  124.5 7.5 %collective-permute-done.16 = bf16[384,640]{0,1:T(8,128)(2,1)} collective-permute-done((bf16[384,640]{0,1:T(8,128)(2,1)}, bf16[384,640]{0,1:T(8,128)(2,1)}, u32[]{:S(2)}, u32[]{:S(2)}) %collective-permute-start.16) | collective-permute-done | bytes 491552 | tf_op jit(solution)/shard_map/ppermute | solution.py:46
  132.0 13.4 %collective-permute-done.17 = bf16[384,640]{0,1:T(8,128)(2,1)} collective-permute-done((bf16[384,640]{0,1:T(8,128)(2,1)}, bf16[384,640]{0,1:T(8,128)(2,1)}, u32[]{:S(2)}, u32[]{:S(2)}) %collective-permute-start.17) | collective-permute-done | bytes 491552 | tf_op jit(solution)/shard_map/ppermute | solution.py:46
  145.6 1.8 %select_select_fusion.3 = (bf16[384,640]{0,1:T(8,128)(2,1)S(1)}, bf16[384,640]{0,1:T(8,128)(2,1)S(1)}, bf16[384,640]{0,1:T(8,128)(2,1)S(1)}, bf16[384,640]{0,1:T(8,128)(2,1)S(1)}) fusion(bf16[384,640]{0,1:T(8,128)(2,1)} %collective-permute-done.16, bf16[384,640]{0,1:T(8,128)(2,1)} %collective-permute-done.17, bf16[384,640]{0,1:T(8,128)(2,1)} %collective-permute-done.18, ...), kind=kLoop, calls=%fused_computation.63 | loop fusion | flops 2949120 | bytes 3932172 | tf_op jit(solution)/shard_map/jit(_where)/select_n | solution.py:51
  147.6 0.9 copy-done.6
  151.0 1.8 %fusion.51 = f32[384,640]{1,0:T(8,128)S(1)} fusion(bf16[640,640]{1,0:T(8,128)(2,1)} %collective-permute-done.1, bf16[384,2560]{0,1:T(8,128)(2,1)S(1)} %pad_maximum_fusion, s32[]{:T(128)S(6)} %select_n.219), kind=kOutput, calls=%fused_computation.82 | convolution fusion | flops 314572800 | bytes 2293764 | tf_op jit(solution)/shard_map/dot_general | solution.py:167
  154.8 1.9 %fusion.49 = f32[384,640]{1,0:T(8,128)S(1)} fusion(bf16[640,640]{1,0:T(8,128)(2,1)} %collective-permute-done.13, bf16[384,2560]{0,1:T(8,128)(2,1)S(1)} %pad_maximum_fusion, s32[]{:T(128)S(6)} %select_n.219), kind=kOutput, calls=%fused_computation.80 | convolution fusion | flops 314572800 | bytes 2293764 | tf_op jit(solution)/shard_map/dot_general | solution.py:168
  158.0 0.9 fusion.20
  160.2 0.8 fusion.21
  161.0 1.2 maximum_select_fusion
  (76 shorter events, 12.1 us)
Async XLA Ops:
  0.0 7.1 %copy-start = (bf16[640,1280]{1,0:T(8,128)(2,1)S(1)}, bf16[640,1280]{1,0:T(8,128)(2,1)}, u32[]{:S(2)}) copy-start(bf16[640,1280]{1,0:T(8,128)(2,1)} %param.10) | copy-start | bytes 4915204
  0.0 43.3 %collective-permute-start.2 = (bf16[384,640]{1,0:T(8,128)(2,1)}, bf16[384,640]{1,0:T(8,128)(2,1)}, u32[]{:S(2)}, u32[]{:S(2)}) collective-permute-start(bf16[384,640]{1,0:T(8,128)(2,1)} %param.8), channel_id=1, source_target_pairs={{0,4},{4,8},{8,12},{1,5},{5,9},{9,13},{2,6},{6,10},{10,14},{3,7},{... | collective-permute-start | bytes 1474568 | tf_op jit(solution)/shard_map/ppermute | solution.py:17
  3.6 12.8 %collective-permute-start.6 = (s32[384]{0:T(512)}, s32[384]{0:T(512)S(1)}, u32[]{:S(2)}, u32[]{:S(2)}) collective-permute-start(s32[384]{0:T(512)} %param.12), channel_id=1, source_target_pairs={{0,4},{4,8},{8,12},{1,5},{5,9},{9,13},{2,6},{6,10},{10,14},{3,7},{... | collective-permute-start | bytes 4616 | tf_op jit(solution)/shard_map/ppermute | solution.py:17
  7.2 52.3 %collective-permute-start = (bf16[640,640]{1,0:T(8,128)(2,1)S(1)}, bf16[640,640]{1,0:T(8,128)(2,1)S(1)}, u32[]{:S(2)}, u32[]{:S(2)}) collective-permute-start(bf16[640,640]{1,0:T(8,128)(2,1)S(1)} %constant_dynamic-slice_fusion.1), channel_id=1, source_target_pairs={{0,4},{4,8},{8,12},{1,5},{5,9},{9,13},{2,6},{6,10},{10,14},{3,7},{... | collective-permute-start | bytes 2457608 | tf_op jit(solution)/shard_map/ppermute | solution.py:17
  9.1 50.4 %collective-permute-start.1 = (bf16[640,640]{1,0:T(8,128)(2,1)S(1)}, bf16[640,640]{1,0:T(8,128)(2,1)}, u32[]{:S(2)}, u32[]{:S(2)}) collective-permute-start(bf16[640,640]{1,0:T(8,128)(2,1)S(1)} %constant_dynamic-slice_fusion.1), channel_id=1, source_target_pairs={{4,0},{8,4},{12,8},{5,1},{9,5},{13,9},{6,2},{10,6},{14,10},{7,3},{... | collective-permute-start | bytes 2457608 | tf_op jit(solution)/shard_map/ppermute | solution.py:17
  13.1 37.0 %collective-permute-start.3 = (bf16[384,640]{1,0:T(8,128)(2,1)}, bf16[384,640]{1,0:T(8,128)(2,1)}, u32[]{:S(2)}, u32[]{:S(2)}) collective-permute-start(bf16[384,640]{1,0:T(8,128)(2,1)} %param.8), channel_id=1, source_target_pairs={{4,0},{8,4},{12,8},{5,1},{9,5},{13,9},{6,2},{10,6},{14,10},{7,3},{... | collective-permute-start | bytes 1474568 | tf_op jit(solution)/shard_map/ppermute | solution.py:17
  16.4 24.7 %collective-permute-start.7 = (s32[384]{0:T(512)}, s32[384]{0:T(512)S(1)}, u32[]{:S(2)}, u32[]{:S(2)}) collective-permute-start(s32[384]{0:T(512)} %param.12), channel_id=1, source_target_pairs={{4,0},{8,4},{12,8},{5,1},{9,5},{13,9},{6,2},{10,6},{14,10},{7,3},{... | collective-permute-start | bytes 4616 | tf_op jit(solution)/shard_map/ppermute | solution.py:17
  41.1 13.7 %collective-permute-start.4 = (bf16[384,640]{1,0:T(8,128)(2,1)}, bf16[384,640]{1,0:T(8,128)(2,1)}, u32[]{:S(2)}, u32[]{:S(2)}) collective-permute-start(bf16[384,640]{1,0:T(8,128)(2,1)} %param.9), channel_id=1, source_target_pairs={{0,4},{4,8},{8,12},{1,5},{5,9},{9,13},{2,6},{6,10},{10,14},{3,7},{... | collective-permute-start | bytes 1474568 | tf_op jit(solution)/shard_map/ppermute | solution.py:17
  43.3 13.7 %collective-permute-start.5 = (bf16[384,640]{1,0:T(8,128)(2,1)}, bf16[384,640]{1,0:T(8,128)(2,1)}, u32[]{:S(2)}, u32[]{:S(2)}) collective-permute-start(bf16[384,640]{1,0:T(8,128)(2,1)} %param.9), channel_id=1, source_target_pairs={{4,0},{8,4},{12,8},{5,1},{9,5},{13,9},{6,2},{10,6},{14,10},{7,3},{... | collective-permute-start | bytes 1474568 | tf_op jit(solution)/shard_map/ppermute | solution.py:17
  50.1 7.0 %copy-start.17 = (bf16[384,640]{1,0:T(8,128)(2,1)S(1)}, bf16[384,640]{1,0:T(8,128)(2,1)}, u32[]{:S(2)}) copy-start(bf16[384,640]{1,0:T(8,128)(2,1)} %param.9) | copy-start | bytes 1474564
  52.8 6.8 %copy-start.18 = (s32[384]{0:T(512)S(1)}, s32[384]{0:T(512)}, u32[]{:S(2)}) copy-start(s32[384]{0:T(512)} %param.12) | copy-start | bytes 4612
  59.6 2.2 %copy-start.2 = (bf16[3,384,640]{2,1,0:T(8,128)(2,1)S(1)}, bf16[3,384,640]{2,1,0:T(8,128)(2,1)}, u32[]{:S(2)}) copy-start(bf16[3,384,640]{2,1,0:T(8,128)(2,1)} %pad_maximum_fusion.1) | copy-start | bytes 4423684
  59.6 2.2 %copy-start.19 = (bf16[384,640]{1,0:T(8,128)(2,1)S(1)}, bf16[384,640]{1,0:T(8,128)(2,1)}, u32[]{:S(2)}) copy-start(bf16[384,640]{1,0:T(8,128)(2,1)} %param.7) | copy-start | bytes 1474564
  64.3 20.2 %collective-permute-start.8 = (bf16[640,640]{1,0:T(8,128)(2,1)S(1)}, bf16[640,640]{1,0:T(8,128)(2,1)S(1)}, u32[]{:S(2)}, u32[]{:S(2)}) collective-permute-start(bf16[640,640]{1,0:T(8,128)(2,1)S(1)} %collective-permute-done), channel_id=1, source_target_pairs={{0,4},{4,8},{8,12},{1,5},{5,9},{9,13},{2,6},{6,10},{10,14},{3,7},{... | collective-permute-start | bytes 2457608 | tf_op jit(solution)/shard_map/ppermute | solution.py:17
  66.5 29.5 %collective-permute-start.12 = (bf16[640,640]{1,0:T(8,128)(2,1)S(1)}, bf16[640,640]{1,0:T(8,128)(2,1)S(1)}, u32[]{:S(2)}, u32[]{:S(2)}) collective-permute-start(bf16[640,640]{1,0:T(8,128)(2,1)S(1)} %collective-permute-done), channel_id=1, source_target_pairs={{4,20},{8,24},{12,28},{20,4},{24,8},{28,12},{5,21},{9,25},{13,29},... | collective-permute-start | bytes 2457608 | tf_op jit(solution)/shard_map/ppermute | solution.py:25
  70.0 19.4 %collective-permute-start.9 = (bf16[640,640]{1,0:T(8,128)(2,1)}, bf16[640,640]{1,0:T(8,128)(2,1)S(1)}, u32[]{:S(2)}, u32[]{:S(2)}) collective-permute-start(bf16[640,640]{1,0:T(8,128)(2,1)} %collective-permute-done.1), channel_id=1, source_target_pairs={{4,0},{8,4},{12,8},{5,1},{9,5},{13,9},{6,2},{10,6},{14,10},{7,3},{... | collective-permute-start | bytes 2457608 | tf_op jit(solution)/shard_map/ppermute | solution.py:17
  71.9 35.4 %collective-permute-start.13 = (bf16[640,640]{1,0:T(8,128)(2,1)}, bf16[640,640]{1,0:T(8,128)(2,1)}, u32[]{:S(2)}, u32[]{:S(2)}) collective-permute-start(bf16[640,640]{1,0:T(8,128)(2,1)} %collective-permute-done.1), channel_id=1, source_target_pairs={{0,16},{4,20},{8,24},{16,0},{20,4},{24,8},{1,17},{5,21},{9,25},{17... | collective-permute-start | bytes 2457608 | tf_op jit(solution)/shard_map/ppermute | solution.py:25
  74.4 2.3 %copy-start.1 = (bf16[3,384,640]{2,1,0:T(8,128)(2,1)S(1)}, bf16[3,384,640]{2,1,0:T(8,128)(2,1)}, u32[]{:S(2)}) copy-start(bf16[3,384,640]{2,1,0:T(8,128)(2,1)} %pad_maximum_fusion.2) | copy-start | bytes 4423684
  84.5 14.9 %copy-start.5 = (bf16[640,640]{1,0:T(8,128)(2,1)}, bf16[640,640]{1,0:T(8,128)(2,1)S(1)}, u32[]{:S(2)}) copy-start(bf16[640,640]{1,0:T(8,128)(2,1)S(1)} %collective-permute-done.8) | copy-start | bytes 2457604
  89.4 21.2 %copy-start.7 = (bf16[640,640]{1,0:T(8,128)(2,1)}, bf16[640,640]{1,0:T(8,128)(2,1)S(1)}, u32[]{:S(2)}) copy-start(bf16[640,640]{1,0:T(8,128)(2,1)S(1)} %collective-permute-done.9) | copy-start | bytes 2457604
  89.4 18.3 %collective-permute-start.10 = (bf16[640,640]{1,0:T(8,128)(2,1)S(1)}, bf16[640,640]{1,0:T(8,128)(2,1)S(1)}, u32[]{:S(2)}, u32[]{:S(2)}) collective-permute-start(bf16[640,640]{1,0:T(8,128)(2,1)S(1)} %collective-permute-done.8), channel_id=1, source_target_pairs={{0,4},{4,8},{8,12},{1,5},{5,9},{9,13},{2,6},{6,10},{10,14},{3,7},{... | collective-permute-start | bytes 2457608 | tf_op jit(solution)/shard_map/ppermute | solution.py:17
  91.6 19.0 %collective-permute-start.14 = (bf16[640,640]{1,0:T(8,128)(2,1)S(1)}, bf16[640,640]{1,0:T(8,128)(2,1)S(1)}, u32[]{:S(2)}, u32[]{:S(2)}) collective-permute-start(bf16[640,640]{1,0:T(8,128)(2,1)S(1)} %collective-permute-done.8), channel_id=1, source_target_pairs={{8,24},{12,28},{24,8},{28,12},{9,25},{13,29},{25,9},{29,13},{10,26... | collective-permute-start | bytes 2457608 | tf_op jit(solution)/shard_map/ppermute | solution.py:25
  92.3 18.3 %collective-permute-start.11 = (bf16[640,640]{1,0:T(8,128)(2,1)S(1)}, bf16[640,640]{1,0:T(8,128)(2,1)S(1)}, u32[]{:S(2)}, u32[]{:S(2)}) collective-permute-start(bf16[640,640]{1,0:T(8,128)(2,1)S(1)} %collective-permute-done.9), channel_id=1, source_target_pairs={{4,0},{8,4},{12,8},{5,1},{9,5},{13,9},{6,2},{10,6},{14,10},{7,3},{... | collective-permute-start | bytes 2457608 | tf_op jit(solution)/shard_map/ppermute | solution.py:17
  96.0 0.9 copy-start.3
  97.0 24.2 %collective-permute-start.15 = (bf16[640,640]{1,0:T(8,128)(2,1)S(1)}, bf16[640,640]{1,0:T(8,128)(2,1)S(1)}, u32[]{:S(2)}, u32[]{:S(2)}) collective-permute-start(bf16[640,640]{1,0:T(8,128)(2,1)S(1)} %collective-permute-done.9), channel_id=1, source_target_pairs={{0,16},{4,20},{16,0},{20,4},{1,17},{5,21},{17,1},{21,5},{2,18},{6,... | collective-permute-start | bytes 2457608 | tf_op jit(solution)/shard_map/ppermute | solution.py:25
  107.7 13.5 %copy-start.9 = (bf16[640,640]{1,0:T(8,128)(2,1)}, bf16[640,640]{1,0:T(8,128)(2,1)S(1)}, u32[]{:S(2)}) copy-start(bf16[640,640]{1,0:T(8,128)(2,1)S(1)} %collective-permute-done.10) | copy-start | bytes 2457604
  110.6 10.5 %copy-start.11 = (bf16[640,640]{1,0:T(8,128)(2,1)}, bf16[640,640]{1,0:T(8,128)(2,1)S(1)}, u32[]{:S(2)}) copy-start(bf16[640,640]{1,0:T(8,128)(2,1)S(1)} %collective-permute-done.11) | copy-start | bytes 2457604
  110.6 12.1 %copy-start.13 = (bf16[640,640]{1,0:T(8,128)(2,1)}, bf16[640,640]{1,0:T(8,128)(2,1)S(1)}, u32[]{:S(2)}) copy-start(bf16[640,640]{1,0:T(8,128)(2,1)S(1)} %collective-permute-done.14) | copy-start | bytes 2457604
  121.2 1.6 copy-start.15
  121.2 10.9 %collective-permute-start.16 = (bf16[384,640]{0,1:T(8,128)(2,1)}, bf16[384,640]{0,1:T(8,128)(2,1)}, u32[]{:S(2)}, u32[]{:S(2)}) collective-permute-start(bf16[384,640]{0,1:T(8,128)(2,1)} %fusion.31), channel_id=1, source_target_pairs={{0,3},{1,0},{2,1},{3,2},{4,7},{5,4},{6,5},{7,6},{8,11},{9,8},{10,9... | collective-permute-start | bytes 1474568 | tf_op jit(solution)/shard_map/ppermute | solution.py:46
  121.2 24.3 %collective-permute-start.17 = (bf16[384,640]{0,1:T(8,128)(2,1)}, bf16[384,640]{0,1:T(8,128)(2,1)}, u32[]{:S(2)}, u32[]{:S(2)}) collective-permute-start(bf16[384,640]{0,1:T(8,128)(2,1)} %fusion.31), channel_id=1, source_target_pairs={{0,2},{1,3},{2,0},{3,1},{4,6},{5,7},{6,4},{7,5},{8,10},{9,11},{10,... | collective-permute-start | bytes 1474568 | tf_op jit(solution)/shard_map/ppermute | solution.py:46
  122.7 22.8 %collective-permute-start.18 = (bf16[384,640]{0,1:T(8,128)(2,1)}, bf16[384,640]{0,1:T(8,128)(2,1)}, u32[]{:S(2)}, u32[]{:S(2)}) collective-permute-start(bf16[384,640]{0,1:T(8,128)(2,1)} %fusion.31), channel_id=1, source_target_pairs={{0,1},{1,2},{2,3},{3,0},{4,5},{5,6},{6,7},{7,4},{8,9},{9,10},{10,1... | collective-permute-start | bytes 1474568 | tf_op jit(solution)/shard_map/ppermute | solution.py:46
  122.9 36.0 %collective-permute-start.19 = (bf16[640,640]{1,0:T(8,128)(2,1)}, bf16[640,640]{1,0:T(8,128)(2,1)S(1)}, u32[]{:S(2)}, u32[]{:S(2)}) collective-permute-start(bf16[640,640]{1,0:T(8,128)(2,1)} %copy-done.9), channel_id=1, source_target_pairs={{12,28},{28,12},{13,29},{29,13},{14,30},{30,14},{15,31},{31,15}} | collective-permute-start | bytes 2457608 | tf_op jit(solution)/shard_map/ppermute | solution.py:25
  123.6 35.9 %collective-permute-start.20 = (bf16[640,640]{1,0:T(8,128)(2,1)}, bf16[640,640]{1,0:T(8,128)(2,1)S(1)}, u32[]{:S(2)}, u32[]{:S(2)}) collective-permute-start(bf16[640,640]{1,0:T(8,128)(2,1)} %copy-done.11), channel_id=1, source_target_pairs={{0,16},{16,0},{1,17},{17,1},{2,18},{18,2},{3,19},{19,3}} | collective-permute-start | bytes 2457608 | tf_op jit(solution)/shard_map/ppermute | solution.py:25
  147.4 1.1 copy-start.6
  148.5 1.1 copy-start.8
  148.5 1.8 %copy-start.10 = (bf16[640,640]{1,0:T(8,128)(2,1)S(1)}, bf16[640,640]{1,0:T(8,128)(2,1)}, u32[]{:S(2)}) copy-start(bf16[640,640]{1,0:T(8,128)(2,1)} %copy-done.9) | copy-start | bytes 2457604
  151.0 2.5 %copy-start.12 = (bf16[640,640]{1,0:T(8,128)(2,1)S(1)}, bf16[640,640]{1,0:T(8,128)(2,1)}, u32[]{:S(2)}) copy-start(bf16[640,640]{1,0:T(8,128)(2,1)} %copy-done.11) | copy-start | bytes 2457604
  152.8 1.3 copy-start.4
  154.2 2.5 %copy-start.14 = (bf16[640,640]{1,0:T(8,128)(2,1)S(1)}, bf16[640,640]{1,0:T(8,128)(2,1)}, u32[]{:S(2)}) copy-start(bf16[640,640]{1,0:T(8,128)(2,1)} %copy-done.13) | copy-start | bytes 2457604
  154.8 2.5 %copy-start.16 = (bf16[640,640]{1,0:T(8,128)(2,1)S(1)}, bf16[640,640]{1,0:T(8,128)(2,1)}, u32[]{:S(2)}) copy-start(bf16[640,640]{1,0:T(8,128)(2,1)} %copy-done.15) | copy-start | bytes 2457604

commit v7 on v0

--- a/solution.py
+++ b/solution.py
@@ -28,10 +28,28 @@
     return jnp.dot(weights, value_head, preferred_element_type=jnp.float32).astype(jnp.bfloat16)
 
 
+def exchange_heads(attended):
+    head_count = lax.axis_size("head")
+    head_position = lax.axis_index("head")
+    received = [attended]
+    for shift in range(1, head_count):
+        pairs = [(j, (j + shift) % head_count) for j in range(head_count)]
+        received.append(lax.ppermute(attended, "head", pairs))
+    ordered = []
+    for group in range(head_count):
+        block = received[0]
+        for shift in range(1, head_count):
+            block = jnp.where((head_position - shift) % head_count == group, received[shift], block)
+        ordered.append(block)
+    return jnp.concatenate(ordered, axis=1)
+
+
 def on_device(queries, keys, values, out_weight, neighbours, clip_ids):
     tile_rows = queries.shape[0]
     feature_width = queries.shape[1]
     seq_count = lax.axis_size("seq")
+    position = lax.axis_index("seq")
+    rep_position = lax.axis_index("rep")
     layer_tiles = TGH * TGW
     every_offset = set()
     for layer_step in (-1, 0, 1):
@@ -39,6 +57,11 @@
             for col_step in (-1, 0, 1):
                 every_offset.add(layer_step * layer_tiles + row_step * TGW + col_step)
     distances = [offset for offset in sorted(every_offset) if 0 < offset < seq_count]
+
+    half_width = out_weight.shape[1] // lax.axis_size("rep")
+    own_half = lax.dynamic_slice_in_dim(out_weight, rep_position * half_width, half_width, axis=1)
+    both_halves = lax.all_gather(own_half, ("rep", "seq"), axis=0, tiled=True)
+
     key_list = [keys]
     value_list = [values]
     clip_list = [clip_ids]
@@ -57,8 +80,8 @@
     key_stack = jnp.stack(key_list)
     value_stack = jnp.stack(value_list)
     clip_stack = jnp.stack(clip_list)
+
     blocks = key_stack.shape[0]
-    position = lax.axis_index("seq")
     window_row = lax.dynamic_index_in_dim(neighbours, position, 0, keepdims=False)
     sources = position - jnp.asarray(offsets, dtype=jnp.int32)
     present = jnp.any(
@@ -80,12 +103,16 @@
             )
         )
     attended = jnp.concatenate(head_outputs, axis=1)
-    all_features = lax.all_gather(attended, "head", axis=1, tiled=True)
-    empty = jnp.zeros((tile_rows, out_weight.shape[1]), jnp.float32)
-    weight_piece = lax.all_gather(out_weight, "seq", axis=0, tiled=True)
-    features = lax.slice_in_dim(all_features, 0, weight_piece.shape[0], axis=1)
-    projected = empty + jnp.dot(features, weight_piece, preferred_element_type=jnp.float32)
-    return projected.astype(jnp.bfloat16)
+
+    features = exchange_heads(attended)
+    rows = features.shape[1]
+    pieces = []
+    for rep_index in range(lax.axis_size("rep")):
+        weight_half = lax.slice_in_dim(both_halves, rep_index * rows, (rep_index + 1) * rows, axis=0)
+        pieces.append(
+            jnp.dot(features, weight_half, preferred_element_type=jnp.float32).astype(jnp.bfloat16)
+        )
+    return jnp.concatenate(pieces, axis=1)
 
 
 def solution(mesh):

time: 208 us -> 146 us (0.70)
  waiting for transfers between devices: 154 us -> 82.1 us
  other arithmetic: 5.25 us -> 8.64 us
  starting transfers between devices: 18.1 us -> 20.5 us
    all_gather x2 -> x1, waiting for transfers between devices: 143 us -> 21.3 us  [on_device(): both_halves = lax.all_gather(own_half, ('rep', 'seq'), axis=0, tiled=True)]
    ppermute x6, waiting for transfers between devices: 10.1 us -> 38.2 us  [from_behind(): return lax.ppermute(value, axis, pairs)]
    ppermute x0 -> x3, waiting for transfers between devices: none -> 22.6 us  [exchange_heads(): received.append(lax.ppermute(attended, 'head', pairs))]
    dot_general x5, matrix products: 5.04 us -> 7.76 us  [attend_head(): jnp.dot(weights, value_head, preferred_element_type=jnp.float32)]
    select_n x0 -> x1, other arithmetic: none -> 2.51 us  [exchange_heads(): jnp.where((head_position - shift) % head_count == group, received[shift],...]
    dot_general x1 -> x2, matrix products: 7.1 us -> 6.15 us  [on_device(): jnp.dot(features, weight_half, preferred_element_type=jnp.float32)]
  transfers between devices with their start and end apart: 8 -> 10, of which waited for: 6 -> 6; matrix products, arithmetic and copies ran while one was open for 4% -> 13% of each run, Pallas kernels for 0% -> 0%
where the time goes in v7:
time: 146 us; the launch traced here: 145 us
  waiting for transfers between devices  82.1 us (56%)
  starting transfers between devices  20.5 us (14%)
  matrix products  17.1 us (12%)
  between operations  13.6 us (9%)
  other arithmetic  8.64 us (6%)
  local copies, waits for them, and re-layouts  3.37 us (2%)
    ppermute x6, waiting for transfers between devices, from_behind(): return lax.ppermute(value, axis, pairs)  38.2 us
    ppermute x3, waiting for transfers between devices, exchange_heads(): received.append(lax.ppermute(attended, 'head', pairs))  22.6 us
    all_gather x1, waiting for transfers between devices, on_device(): both_halves = lax.all_gather(own_half, ('rep', 'seq'), axis=0, tiled=True)  21.3 us
    ppermute x6, starting transfers between devices, from_behind(): return lax.ppermute(value, axis, pairs)  18.7 us
    dot_general x5, matrix products, attend_head(): jnp.dot(weights, value_head, preferred_element_type=jnp.float32)  7.76 us
    dot_general x2, matrix products, on_device(): jnp.dot(features, weight_half, preferred_element_type=jnp.float32)  6.15 us
    dot_general x5, matrix products, attend_head(): lax.dot_general(query_head, key_head, (((1,), (1,)), ((), ())), preferred...  3.16 us
  transfers between devices with their start and end apart: 10, of which 6 were waited for; matrix products, arithmetic and copies ran while one was open for 13% of the time, Pallas kernels for 0%

profile of v7, /device:TPU:0, one launch (start us, length us, event | category | flops | bytes accessed | tf_op | source)
XLA Modules:
  0.0 145.3 jit_solution(1023972841355006737)
XLA Ops:
  6.5 0.0 copy-start.10
  6.6 0.0 all-gather.2.cloned.1.call-start
  6.6 1.7 %copy-done = bf16[640,1280]{1,0:T(8,128)(2,1)S(1)} copy-done((bf16[640,1280]{1,0:T(8,128)(2,1)S(1)}, bf16[640,1280]{1,0:T(8,128)(2,1)}, u32[]{:S(2)}) %copy-start) | copy-done | bytes 1638424
  8.3 1.0 constant_dynamic-slice_fusion
  9.2 0.0 all-gather.2.cloned.1.call-update
  9.3 0.0 copy-done.1
  9.3 5.7 %collective-permute-start.2 = (bf16[384,640]{1,0:T(8,128)(2,1)S(1)}, bf16[384,640]{1,0:T(8,128)(2,1)}, u32[]{:S(2)}, u32[]{:S(2)}) collective-permute-start(bf16[384,640]{1,0:T(8,128)(2,1)S(1)} %copy-done.1), channel_id=1, source_target_pairs={{0,4},{4,8},{8,12},{1,5},{5,9},{9,13},{2,6},{6,10},{10,14},{3,7},{... | collective-permute-start | bytes 1474568 | tf_op jit(solution)/shard_map/ppermute | solution.py:16
  15.0 1.3 collective-permute-start.3
  16.3 4.6 %collective-permute-start.4 = (bf16[384,640]{1,0:T(8,128)(2,1)S(1)}, bf16[384,640]{1,0:T(8,128)(2,1)S(1)}, u32[]{:S(2)}, u32[]{:S(2)}) collective-permute-start(bf16[384,640]{1,0:T(8,128)(2,1)S(1)} %copy-done.2), channel_id=1, source_target_pairs={{0,4},{4,8},{8,12},{1,5},{5,9},{9,13},{2,6},{6,10},{10,14},{3,7},{... | collective-permute-start | bytes 1474568 | tf_op jit(solution)/shard_map/ppermute | solution.py:16
  20.9 1.3 collective-permute-start.5
  22.2 0.0 copy-done.7
  22.2 4.5 %collective-permute-start = (s32[384]{0:T(512)S(1)}, s32[384]{0:T(512)S(1)}, u32[]{:S(2)}, u32[]{:S(2)}) collective-permute-start(s32[384]{0:T(512)S(1)} %copy-done.7), channel_id=1, source_target_pairs={{0,4},{4,8},{8,12},{1,5},{5,9},{9,13},{2,6},{6,10},{10,14},{3,7},{... | collective-permute-start | bytes 4616 | tf_op jit(solution)/shard_map/ppermute | solution.py:16
  26.7 0.0 copy-done.11
  26.8 23.3 %collective-permute-done = s32[384]{0:T(512)S(1)} collective-permute-done((s32[384]{0:T(512)S(1)}, s32[384]{0:T(512)S(1)}, u32[]{:S(2)}, u32[]{:S(2)}) %collective-permute-start) | collective-permute-done | bytes 1568 | tf_op jit(solution)/shard_map/ppermute | solution.py:16
  50.1 1.3 collective-permute-start.1
  51.4 0.2 and_reduce_fusion
  51.6 0.1 broadcast_in_dim.32
  51.7 14.9 %collective-permute-done.1 = s32[384]{0:T(512)S(1)} collective-permute-done((s32[384]{0:T(512)S(1)}, s32[384]{0:T(512)S(1)}, u32[]{:S(2)}, u32[]{:S(2)}) %collective-permute-start.1) | collective-permute-done | bytes 1568 | tf_op jit(solution)/shard_map/ppermute | solution.py:16
  66.6 0.0 collective-permute-done.2
  66.7 0.0 collective-permute-done.3
  66.7 1.4 pad_maximum_fusion.1
  68.0 0.0 copy-start.9
  68.0 0.0 collective-permute-done.4
  68.1 0.0 collective-permute-done.5
  68.1 1.3 pad_maximum_fusion.2
  69.4 0.6 fusion.53
  70.0 0.6 fusion.54
  70.6 0.6 fusion.55
  71.3 0.6 fusion.56
  71.9 0.6 fusion.57
  72.5 2.3 %fusion.24 = (f32[384]{0:T(512)S(1)}, f32[384]{0:T(512)S(1)}, f32[384]{0:T(512)S(1)}, f32[384]{0:T(512)S(1)}, f32[384]{0:T(512)S(1)}) fusion(f32[384,1152]{0,1:T(8,128)S(1)} %get-tuple-element.15, f32[384]{0:T(512)S(1)} %get-tuple-element.14, s32[384]{0:T(512)S(1)} %copy-done.7, s32[1152]{0:T(1024)S(1)} %eq.85, pred[1152]{0:T(1024)(128)(4,1)S(1)} %and.49, ...), kind=kLoop, calls=%fused_computation.39 | loop fusion | flops 7518336 | bytes 8870016 | tf_op jit(solution)/shard_map/reduce_sum | solution.py:26
  74.8 1.5 %fusion.25 = bf16[384,640]{0,1:T(8,128)(2,1)} fusion(f32[384,1152]{0,1:T(8,128)S(1)} %get-tuple-element.23, f32[384]{0:T(512)S(1)} %get-tuple-element.9, f32[384]{0:T(512)S(1)} %get-tuple-element.22, s32[384]{0:T(512)S(1)} %copy-done.7, s32[1152]{0:T(1024)S(1)} %eq.85, pred[1152]{0:T(1024)(128)(4,1)S(1)} %and.49, bf16[1152,640]{1,0:T(8,128)(2,1)S(1)} %bitcast.32), kind=kOutput, calls=%fused_computation.45 | convolution fusion | flops 115949568 | bytes 2179072 | tf_op jit(solution)/shard_map/dot_general | solution.py:28
  76.3 1.6 %fusion.26 = bf16[384,640]{0,1:T(8,128)(2,1)} fusion(bf16[384,640]{0,1:T(8,128)(2,1)} %fusion.25, f32[384,1152]{0,1:T(8,128)S(1)} %get-tuple-element.21, f32[384]{0:T(512)S(1)} %get-tuple-element.8, f32[384]{0:T(512)S(1)} %get-tuple-element.20, s32[384]{0:T(512)S(1)} %copy-done.7, s32[1152]{0:T(1024)S(1)} %eq.85, pred[1152]{0:T(1024)(128)(4,1)S(1)} %and.49, ...), kind=kOutput, calls=%fused_computation.46 | convolution fusion | flops 115949568 | bytes 2179072 | tf_op jit(solution)/shard_map/dot_general | solution.py:28
  77.9 1.5 %fusion.27 = bf16[384,640]{0,1:T(8,128)(2,1)} fusion(bf16[384,640]{0,1:T(8,128)(2,1)} %fusion.26, f32[384,1152]{0,1:T(8,128)S(1)} %get-tuple-element.19, f32[384]{0:T(512)S(1)} %get-tuple-element.7, f32[384]{0:T(512)S(1)} %get-tuple-element.18, s32[384]{0:T(512)S(1)} %copy-done.7, s32[1152]{0:T(1024)S(1)} %eq.85, pred[1152]{0:T(1024)(128)(4,1)S(1)} %and.49, ...), kind=kOutput, calls=%fused_computation.47 | convolution fusion | flops 115949568 | bytes 2179072 | tf_op jit(solution)/shard_map/dot_general | solution.py:28
  79.4 1.6 %fusion.28 = bf16[384,640]{0,1:T(8,128)(2,1)} fusion(bf16[384,640]{0,1:T(8,128)(2,1)} %fusion.27, f32[384,1152]{0,1:T(8,128)S(1)} %get-tuple-element.17, f32[384]{0:T(512)S(1)} %get-tuple-element.6, f32[384]{0:T(512)S(1)} %get-tuple-element.16, s32[384]{0:T(512)S(1)} %copy-done.7, s32[1152]{0:T(1024)S(1)} %eq.85, pred[1152]{0:T(1024)(128)(4,1)S(1)} %and.49, ...), kind=kOutput, calls=%fused_computation.48 | convolution fusion | flops 115949568 | bytes 2179072 | tf_op jit(solution)/shard_map/dot_general | solution.py:28
  81.0 1.6 %fusion.29 = bf16[384,640]{0,1:T(8,128)(2,1)} fusion(bf16[384,640]{0,1:T(8,128)(2,1)} %fusion.28, f32[384,1152]{0,1:T(8,128)S(1)} %get-tuple-element.15, f32[384]{0:T(512)S(1)} %get-tuple-element.5, f32[384]{0:T(512)S(1)} %get-tuple-element.14, s32[384]{0:T(512)S(1)} %copy-done.7, s32[1152]{0:T(1024)S(1)} %eq.85, pred[1152]{0:T(1024)(128)(4,1)S(1)} %and.49, ...), kind=kOutput, calls=%fused_computation.49 | convolution fusion | flops 115949568 | bytes 2179072 | tf_op jit(solution)/shard_map/dot_general | solution.py:28
  82.5 0.0 collective-permute-start.6
  82.5 1.5 %collective-permute-start.7 = (bf16[384,640]{0,1:T(8,128)(2,1)}, bf16[384,640]{0,1:T(8,128)(2,1)S(1)}, u32[]{:S(2)}, u32[]{:S(2)}) collective-permute-start(bf16[384,640]{0,1:T(8,128)(2,1)} %fusion.29), channel_id=1, source_target_pairs={{0,2},{1,3},{2,0},{3,1},{4,6},{5,7},{6,4},{7,5},{8,10},{9,11},{10,... | collective-permute-start | bytes 1474568 | tf_op jit(solution)/shard_map/ppermute | solution.py:37
  84.1 0.2 collective-permute-start.8
  84.3 9.1 %collective-permute-done.6 = bf16[384,640]{0,1:T(8,128)(2,1)S(1)} collective-permute-done((bf16[384,640]{0,1:T(8,128)(2,1)}, bf16[384,640]{0,1:T(8,128)(2,1)S(1)}, u32[]{:S(2)}, u32[]{:S(2)}) %collective-permute-start.6) | collective-permute-done | bytes 491552 | tf_op jit(solution)/shard_map/ppermute | solution.py:37
  93.4 13.4 %collective-permute-done.7 = bf16[384,640]{0,1:T(8,128)(2,1)S(1)} collective-permute-done((bf16[384,640]{0,1:T(8,128)(2,1)}, bf16[384,640]{0,1:T(8,128)(2,1)S(1)}, u32[]{:S(2)}, u32[]{:S(2)}) %collective-permute-start.7) | collective-permute-done | bytes 491552 | tf_op jit(solution)/shard_map/ppermute | solution.py:37
  106.8 0.1 collective-permute-done.8
  106.9 2.5 %select_select_fusion.3 = (bf16[384,640]{0,1:T(8,128)(2,1)}, bf16[384,640]{0,1:T(8,128)(2,1)}, bf16[384,640]{0,1:T(8,128)(2,1)}, bf16[384,640]{0,1:T(8,128)(2,1)}) fusion(bf16[384,640]{0,1:T(8,128)(2,1)S(1)} %collective-permute-done.6, bf16[384,640]{0,1:T(8,128)(2,1)S(1)} %collective-permute-done.7, bf16[384,640]{0,1:T(8,128)(2,1)S(1)} %collective-permute-done.8, ...), kind=kLoop, calls=%fused_computation.54 | loop fusion | flops 2949120 | bytes 3932172 | tf_op jit(solution)/shard_map/jit(_where)/select_n | solution.py:42
  109.4 21.3 %all-gather.2.cloned.1.call-done = bf16[5120,640]{1,0:T(8,128)(2,1)} async-done(((bf16[640,640]{1,0:T(8,128)(2,1)}), bf16[5120,640]{1,0:T(8,128)(2,1)}) %all-gather.2.cloned.1.call-update) | async-done | bytes 6553616 | tf_op jit(solution)/shard_map/all_gather | solution.py:63
  130.7 4.4 %fusion.14 = bf16[384,640]{1,0:T(8,128)(2,1)S(1)} fusion(bf16[5120,640]{1,0:T(8,128)(2,1)} %all-gather.2.cloned.1.call-done, bf16[384,640]{0,1:T(8,128)(2,1)} %get-tuple-element.11, bf16[384,640]{0,1:T(8,128)(2,1)} %get-tuple-element.12, bf16[384,640]{0,1:T(8,128)(2,1)} %get-tuple-element.13, bf16[384,640]{0,1:T(8,128)(2,1)} %get-tuple-element.10), kind=kOutput, calls=%fused_computation.33 | convolution fusion | flops 1266401280 | bytes 5734400 | tf_op jit(solution)/shard_map/dot_general | solution.py:113
  135.1 0.6 copy-done.8
  135.7 1.8 %fusion.17 = bf16[384,640]{1,0:T(8,128)(2,1)S(1)} fusion(bf16[5120,640]{1,0:T(8,128)(2,1)S(1)} %copy-done.8, bf16[384,640]{0,1:T(8,128)(2,1)S(1)} %copy-done.4, bf16[384,640]{0,1:T(8,128)(2,1)S(1)} %copy-done.5, bf16[384,640]{0,1:T(8,128)(2,1)S(1)} %copy-done.6, bf16[384,640]{0,1:T(8,128)(2,1)S(1)} %copy-done.3), kind=kOutput, calls=%fused_computation.34 | convolution fusion | flops 1266401280 | bytes 5734400 | tf_op jit(solution)/shard_map/dot_general | solution.py:113
  137.4 1.0 pad_maximum_fusion.3
  (26 shorter events, 0.1 us)
Async XLA Ops:
  6.5 1.7 %copy-start = (bf16[640,1280]{1,0:T(8,128)(2,1)S(1)}, bf16[640,1280]{1,0:T(8,128)(2,1)}, u32[]{:S(2)}) copy-start(bf16[640,1280]{1,0:T(8,128)(2,1)} %param.10) | copy-start | bytes 4915204
  6.5 20.2 %copy-start.11 = (s32[3]{0:T(128)S(1)}, s32[3]{0:T(128)}, u32[]{:S(2)}) copy-start(s32[3]{0:T(128)} %constant.86) | copy-start | bytes 40
  6.5 2.7 %copy-start.1 = (bf16[384,640]{1,0:T(8,128)(2,1)S(1)}, bf16[384,640]{1,0:T(8,128)(2,1)}, u32[]{:S(2)}) copy-start(bf16[384,640]{1,0:T(8,128)(2,1)} %param.8) | copy-start | bytes 1474564
  6.5 9.7 %copy-start.2 = (bf16[384,640]{1,0:T(8,128)(2,1)S(1)}, bf16[384,640]{1,0:T(8,128)(2,1)}, u32[]{:S(2)}) copy-start(bf16[384,640]{1,0:T(8,128)(2,1)} %param.9) | copy-start | bytes 1474564
  6.5 15.6 %copy-start.7 = (s32[384]{0:T(512)S(1)}, s32[384]{0:T(512)}, u32[]{:S(2)}) copy-start(s32[384]{0:T(512)} %param.12) | copy-start | bytes 4612
  6.5 20.2 %copy-start.10 = (s32[4,27]{1,0:T(4,128)S(1)}, s32[4,27]{1,0:T(4,128)}, u32[]{:S(2)}) copy-start(s32[4,27]{1,0:T(4,128)} %param.11) | copy-start | bytes 1300
  6.6 124.1 %all-gather.2.cloned.1.call-start = ((), (), s32[]{:S(2)}) async-start(), calls=%async_computation | async-start | bytes 7372800 | tf_op jit(solution)/shard_map/all_gather | solution.py:63
  9.3 57.4 %collective-permute-start.2 = (bf16[384,640]{1,0:T(8,128)(2,1)S(1)}, bf16[384,640]{1,0:T(8,128)(2,1)}, u32[]{:S(2)}, u32[]{:S(2)}) collective-permute-start(bf16[384,640]{1,0:T(8,128)(2,1)S(1)} %copy-done.1), channel_id=1, source_target_pairs={{0,4},{4,8},{8,12},{1,5},{5,9},{9,13},{2,6},{6,10},{10,14},{3,7},{... | collective-permute-start | bytes 1474568 | tf_op jit(solution)/shard_map/ppermute | solution.py:16
  15.0 51.7 %collective-permute-start.3 = (bf16[384,640]{1,0:T(8,128)(2,1)S(1)}, bf16[384,640]{1,0:T(8,128)(2,1)}, u32[]{:S(2)}, u32[]{:S(2)}) collective-permute-start(bf16[384,640]{1,0:T(8,128)(2,1)S(1)} %copy-done.1), channel_id=1, source_target_pairs={{4,0},{8,4},{12,8},{5,1},{9,5},{13,9},{6,2},{10,6},{14,10},{7,3},{... | collective-permute-start | bytes 1474568 | tf_op jit(solution)/shard_map/ppermute | solution.py:16
  16.3 51.8 %collective-permute-start.4 = (bf16[384,640]{1,0:T(8,128)(2,1)S(1)}, bf16[384,640]{1,0:T(8,128)(2,1)S(1)}, u32[]{:S(2)}, u32[]{:S(2)}) collective-permute-start(bf16[384,640]{1,0:T(8,128)(2,1)S(1)} %copy-done.2), channel_id=1, source_target_pairs={{0,4},{4,8},{8,12},{1,5},{5,9},{9,13},{2,6},{6,10},{10,14},{3,7},{... | collective-permute-start | bytes 1474568 | tf_op jit(solution)/shard_map/ppermute | solution.py:16
  20.9 47.2 %collective-permute-start.5 = (bf16[384,640]{1,0:T(8,128)(2,1)S(1)}, bf16[384,640]{1,0:T(8,128)(2,1)}, u32[]{:S(2)}, u32[]{:S(2)}) collective-permute-start(bf16[384,640]{1,0:T(8,128)(2,1)S(1)} %copy-done.2), channel_id=1, source_target_pairs={{4,0},{8,4},{12,8},{5,1},{9,5},{13,9},{6,2},{10,6},{14,10},{7,3},{... | collective-permute-start | bytes 1474568 | tf_op jit(solution)/shard_map/ppermute | solution.py:16
  22.2 27.9 %collective-permute-start = (s32[384]{0:T(512)S(1)}, s32[384]{0:T(512)S(1)}, u32[]{:S(2)}, u32[]{:S(2)}) collective-permute-start(s32[384]{0:T(512)S(1)} %copy-done.7), channel_id=1, source_target_pairs={{0,4},{4,8},{8,12},{1,5},{5,9},{9,13},{2,6},{6,10},{10,14},{3,7},{... | collective-permute-start | bytes 4616 | tf_op jit(solution)/shard_map/ppermute | solution.py:16
  50.1 16.5 %collective-permute-start.1 = (s32[384]{0:T(512)S(1)}, s32[384]{0:T(512)S(1)}, u32[]{:S(2)}, u32[]{:S(2)}) collective-permute-start(s32[384]{0:T(512)S(1)} %copy-done.7), channel_id=1, source_target_pairs={{4,0},{8,4},{12,8},{5,1},{9,5},{13,9},{6,2},{10,6},{14,10},{7,3},{... | collective-permute-start | bytes 4616 | tf_op jit(solution)/shard_map/ppermute | solution.py:16
  68.0 1.3 copy-start.9
  82.5 10.9 %collective-permute-start.6 = (bf16[384,640]{0,1:T(8,128)(2,1)}, bf16[384,640]{0,1:T(8,128)(2,1)S(1)}, u32[]{:S(2)}, u32[]{:S(2)}) collective-permute-start(bf16[384,640]{0,1:T(8,128)(2,1)} %fusion.29), channel_id=1, source_target_pairs={{0,3},{1,0},{2,1},{3,2},{4,7},{5,4},{6,5},{7,6},{8,11},{9,8},{10,9... | collective-permute-start | bytes 1474568 | tf_op jit(solution)/shard_map/ppermute | solution.py:37
  82.5 24.3 %collective-permute-start.7 = (bf16[384,640]{0,1:T(8,128)(2,1)}, bf16[384,640]{0,1:T(8,128)(2,1)S(1)}, u32[]{:S(2)}, u32[]{:S(2)}) collective-permute-start(bf16[384,640]{0,1:T(8,128)(2,1)} %fusion.29), channel_id=1, source_target_pairs={{0,2},{1,3},{2,0},{3,1},{4,6},{5,7},{6,4},{7,5},{8,10},{9,11},{10,... | collective-permute-start | bytes 1474568 | tf_op jit(solution)/shard_map/ppermute | solution.py:37
  84.1 22.8 %collective-permute-start.8 = (bf16[384,640]{0,1:T(8,128)(2,1)}, bf16[384,640]{0,1:T(8,128)(2,1)S(1)}, u32[]{:S(2)}, u32[]{:S(2)}) collective-permute-start(bf16[384,640]{0,1:T(8,128)(2,1)} %fusion.29), channel_id=1, source_target_pairs={{0,1},{1,2},{2,3},{3,0},{4,5},{5,6},{6,7},{7,4},{8,9},{9,10},{10,1... | collective-permute-start | bytes 1474568 | tf_op jit(solution)/shard_map/ppermute | solution.py:37
  130.6 4.4 %copy-start.3 = (bf16[384,640]{0,1:T(8,128)(2,1)S(1)}, bf16[384,640]{0,1:T(8,128)(2,1)}, u32[]{:S(2)}) copy-start(bf16[384,640]{0,1:T(8,128)(2,1)} %get-tuple-element.10) | copy-start | bytes 1474564
  130.6 4.4 %copy-start.4 = (bf16[384,640]{0,1:T(8,128)(2,1)S(1)}, bf16[384,640]{0,1:T(8,128)(2,1)}, u32[]{:S(2)}) copy-start(bf16[384,640]{0,1:T(8,128)(2,1)} %get-tuple-element.11) | copy-start | bytes 1474564
  130.6 4.4 %copy-start.5 = (bf16[384,640]{0,1:T(8,128)(2,1)S(1)}, bf16[384,640]{0,1:T(8,128)(2,1)}, u32[]{:S(2)}) copy-start(bf16[384,640]{0,1:T(8,128)(2,1)} %get-tuple-element.12) | copy-start | bytes 1474564
  130.6 4.4 %copy-start.6 = (bf16[384,640]{0,1:T(8,128)(2,1)S(1)}, bf16[384,640]{0,1:T(8,128)(2,1)}, u32[]{:S(2)}) copy-start(bf16[384,640]{0,1:T(8,128)(2,1)} %get-tuple-element.13) | copy-start | bytes 1474564
  130.7 5.0 %copy-start.8 = (bf16[5120,640]{1,0:T(8,128)(2,1)S(1)}, bf16[5120,640]{1,0:T(8,128)(2,1)}, u32[]{:S(2)}) copy-start(bf16[5120,640]{1,0:T(8,128)(2,1)} %all-gather.2.cloned.1.call-done) | copy-start | bytes 19660804
Sparse Core Ops, SparseCore 0:
  9.5 121.1 all-gather.1

commit v8 on v6

--- a/solution.py
+++ b/solution.py
@@ -9,6 +9,7 @@
 TGH = 4
 TGW = 7
 LINE_LIMIT = 4
+SC_LANES = 2
 
 
 def from_behind(value, axis, by):
@@ -71,10 +72,14 @@
 
     if line_path:
         half_width = out_weight.shape[1] // 2
-        own_half = lax.dynamic_slice_in_dim(out_weight, rep_position * half_width, half_width, axis=1)
-        other_half = lax.dynamic_slice_in_dim(
+        sc_width = SC_LANES * 128
+        own_full = lax.dynamic_slice_in_dim(out_weight, rep_position * half_width, half_width, axis=1)
+        other_full = lax.dynamic_slice_in_dim(
             out_weight, (1 - rep_position) * half_width, half_width, axis=1
         )
+        both_sc = lax.all_gather(own_full[:, :sc_width], ("rep", "seq"), axis=0, tiled=True)
+        own_half = own_full[:, sc_width:]
+        other_half = other_full[:, sc_width:]
         from_left = from_behind(own_half, "seq", 1)
         from_right = from_behind(own_half, "seq", -1)
     else:
@@ -168,11 +173,18 @@
         other_sum = other_sum + jnp.dot(rows, twin_block, preferred_element_type=jnp.float32)
     own_out = own_sum.astype(jnp.bfloat16)
     other_out = other_sum.astype(jnp.bfloat16)
-    return jnp.where(
-        rep_position == 0,
-        jnp.concatenate([own_out, other_out], axis=1),
-        jnp.concatenate([other_out, own_out], axis=1),
-    )
+    rows = features.shape[1]
+    sc_parts = [
+        jnp.dot(
+            features,
+            lax.slice_in_dim(both_sc, index * rows, (index + 1) * rows, axis=0),
+            preferred_element_type=jnp.float32,
+        ).astype(jnp.bfloat16)
+        for index in range(2)
+    ]
+    first_line = jnp.where(rep_position == 0, own_out, other_out)
+    second_line = jnp.where(rep_position == 0, other_out, own_out)
+    return jnp.concatenate([sc_parts[0], first_line, sc_parts[1], second_line], axis=1)
 
 
 def solution(mesh):

time: 163 us -> 172 us (1.055)
  the two profiles are of different devices: /device:TPU:8 before, /device:TPU:0 now
where the time goes in v8:
time: 172 us; the launch traced here: 171 us
  waiting for transfers between devices  60.4 us (35%)
  starting transfers between devices  50.7 us (29%)
  matrix products  28.3 us (16%)
  between operations  14.1 us (8%)
  other arithmetic  11.1 us (6%)
  local copies, waits for them, and re-layouts  6.15 us (4%)
    ppermute x12, starting transfers between devices, from_behind(): return lax.ppermute(value, axis, pairs)  36.4 us
    ppermute x12, waiting for transfers between devices, from_behind(): return lax.ppermute(value, axis, pairs)  21.5 us
    all_gather x1, waiting for transfers between devices, on_device(): lax.all_gather(own_full[:, :sc_width], ('rep', 'seq'), axis=0, tiled=True)  19.6 us
    ppermute x3, waiting for transfers between devices, exchange_heads(): received.append(lax.ppermute(attended, 'head', pairs))  17.3 us
    ppermute x6, starting transfers between devices, to_twin(): return lax.ppermute(value, ('rep', 'seq'), pairs)  12.5 us
    dot_general x5, matrix products, attend_head(): jnp.dot(weights, value_head, preferred_element_type=jnp.float32)  7.81 us
    dot_general x6, matrix products, on_device(): jnp.dot(rows, own_block, preferred_element_type=jnp.float32)  6.29 us
    dot_general x5, matrix products, attend_head(): lax.dot_general(query_head, key_head, (((1,), (1,)), ((), ())), preferred...  5.61 us
  transfers between devices with their start and end apart: 22, of which 9 were waited for; matrix products, arithmetic and copies ran while one was open for 19% of the time, Pallas kernels for 0%

profile of v8, /device:TPU:0, one launch (start us, length us, event | category | flops | bytes accessed | tf_op | source)
XLA Modules:
  0.0 170.8 jit_solution(18302112608736288358)
XLA Ops:
  6.5 5.9 %collective-permute-start.2 = (bf16[384,640]{1,0:T(8,128)(2,1)}, bf16[384,640]{1,0:T(8,128)(2,1)}, u32[]{:S(2)}, u32[]{:S(2)}) collective-permute-start(bf16[384,640]{1,0:T(8,128)(2,1)} %param.8), channel_id=1, source_target_pairs={{0,4},{4,8},{8,12},{1,5},{5,9},{9,13},{2,6},{6,10},{10,14},{3,7},{... | collective-permute-start | bytes 1474568 | tf_op jit(solution)/shard_map/ppermute | solution.py:18
  12.4 1.3 collective-permute-start.3
  13.7 5.4 %collective-permute-start.4 = (bf16[384,640]{1,0:T(8,128)(2,1)}, bf16[384,640]{1,0:T(8,128)(2,1)}, u32[]{:S(2)}, u32[]{:S(2)}) collective-permute-start(bf16[384,640]{1,0:T(8,128)(2,1)} %param.9), channel_id=1, source_target_pairs={{0,4},{4,8},{8,12},{1,5},{5,9},{9,13},{2,6},{6,10},{10,14},{3,7},{... | collective-permute-start | bytes 1474568 | tf_op jit(solution)/shard_map/ppermute | solution.py:18
  19.1 1.3 collective-permute-start.5
  20.3 4.6 %collective-permute-start.6 = (s32[384]{0:T(512)}, s32[384]{0:T(512)S(1)}, u32[]{:S(2)}, u32[]{:S(2)}) collective-permute-start(s32[384]{0:T(512)} %param.12), channel_id=1, source_target_pairs={{0,4},{4,8},{8,12},{1,5},{5,9},{9,13},{2,6},{6,10},{10,14},{3,7},{... | collective-permute-start | bytes 4616 | tf_op jit(solution)/shard_map/ppermute | solution.py:18
  25.6 0.7 compare_bitcast_fusion
  26.4 6.6 %collective-permute-done.6 = s32[384]{0:T(512)S(1)} collective-permute-done((s32[384]{0:T(512)}, s32[384]{0:T(512)S(1)}, u32[]{:S(2)}, u32[]{:S(2)}) %collective-permute-start.6) | collective-permute-done | bytes 1568 | tf_op jit(solution)/shard_map/ppermute | solution.py:18
  32.9 1.3 collective-permute-start.7
  34.2 0.7 fusion.98
  35.6 3.5 %collective-permute-done.7 = s32[384]{0:T(512)S(1)} collective-permute-done((s32[384]{0:T(512)}, s32[384]{0:T(512)S(1)}, u32[]{:S(2)}, u32[]{:S(2)}) %collective-permute-start.7) | collective-permute-done | bytes 1568 | tf_op jit(solution)/shard_map/ppermute | solution.py:18
  39.1 3.9 %collective-permute-start = (bf16[640,384]{1,0:T(8,128)(2,1)S(1)}, bf16[640,384]{1,0:T(8,128)(2,1)S(1)}, u32[]{:S(2)}, u32[]{:S(2)}) collective-permute-start(bf16[640,384]{1,0:T(8,128)(2,1)S(1)} %constant_dynamic-slice_fusion), channel_id=1, source_target_pairs={{0,4},{4,8},{8,12},{1,5},{5,9},{9,13},{2,6},{6,10},{10,14},{3,7},{... | collective-permute-start | bytes 1474568 | tf_op jit(solution)/shard_map/ppermute | solution.py:18
  43.0 1.3 collective-permute-start.1
  44.7 2.7 %pad_maximum_fusion.1 = bf16[3,384,640]{2,1,0:T(8,128)(2,1)} fusion(bf16[1,384,640]{2,1,0:T(8,128)(2,1)} %bitcast.2, bf16[1,384,640]{2,1,0:T(8,128)(2,1)} %bitcast.1, bf16[1,384,640]{2,1,0:T(8,128)(2,1)} %bitcast.55), kind=kLoop, calls=%fused_computation.27 | loop fusion | flops 1474560 | bytes 2949120 | tf_op jit(solution)/shard_map/stack | solution.py:103
  47.3 2.5 %pad_maximum_fusion.2 = bf16[3,384,640]{2,1,0:T(8,128)(2,1)} fusion(bf16[1,384,640]{2,1,0:T(8,128)(2,1)} %bitcast.5, bf16[1,384,640]{2,1,0:T(8,128)(2,1)} %bitcast.4, bf16[1,384,640]{2,1,0:T(8,128)(2,1)S(1)} %bitcast.56), kind=kLoop, calls=%fused_computation.28 | loop fusion | flops 1474560 | bytes 2949120 | tf_op jit(solution)/shard_map/stack | solution.py:104
  49.8 1.6 collective-permute-done
  51.5 4.3 %collective-permute-done.1 = bf16[640,384]{1,0:T(8,128)(2,1)} collective-permute-done((bf16[640,384]{1,0:T(8,128)(2,1)S(1)}, bf16[640,384]{1,0:T(8,128)(2,1)}, u32[]{:S(2)}, u32[]{:S(2)}) %collective-permute-start.1) | collective-permute-done | bytes 491552 | tf_op jit(solution)/shard_map/ppermute | solution.py:18
  55.7 2.2 %fusion.107 = (f32[384]{0:T(512)S(1)}, f32[384,1152]{0,1:T(8,128)S(1)}) fusion(bf16[384,640]{1,0:T(8,128)(2,1)} %param.7, bf16[1152,640]{1,0:T(8,128)(2,1)} %bitcast.50, s32[1152]{0:T(1024)S(1)} %eq.89, s32[384]{0:T(512)S(1)} %copy-done.24, pred[1152]{0:T(1024)(128)(4,1)S(1)} %and.49), kind=kOutput, calls=%fused_computation.143 | convolution fusion | flops 115457664 | bytes 2171520 | tf_op jit(solution)/shard_map/dot_general | solution.py:30
  57.9 1.6 fusion.106
  61.4 3.5 %collective-permute-start.8 = (bf16[640,384]{1,0:T(8,128)(2,1)S(1)}, bf16[640,384]{1,0:T(8,128)(2,1)S(1)}, u32[]{:S(2)}, u32[]{:S(2)}) collective-permute-start(bf16[640,384]{1,0:T(8,128)(2,1)S(1)} %collective-permute-done), channel_id=1, source_target_pairs={{0,4},{4,8},{8,12},{1,5},{5,9},{9,13},{2,6},{6,10},{10,14},{3,7},{... | collective-permute-start | bytes 1474568 | tf_op jit(solution)/shard_map/ppermute | solution.py:18
  65.6 1.3 collective-permute-start.9
  66.9 3.4 %collective-permute-start.13 = (bf16[640,384]{1,0:T(8,128)(2,1)}, bf16[640,384]{1,0:T(8,128)(2,1)S(1)}, u32[]{:S(2)}, u32[]{:S(2)}) collective-permute-start(bf16[640,384]{1,0:T(8,128)(2,1)} %collective-permute-done.1), channel_id=1, source_target_pairs={{0,16},{4,20},{8,24},{16,0},{20,4},{24,8},{1,17},{5,21},{9,25},{17... | collective-permute-start | bytes 1474568 | tf_op jit(solution)/shard_map/ppermute | solution.py:26
  70.3 2.3 %fusion.28 = (f32[384]{0:T(512)S(1)}, f32[384]{0:T(512)S(1)}, f32[384]{0:T(512)S(1)}, f32[384]{0:T(512)S(1)}, f32[384]{0:T(512)S(1)}) fusion(f32[384,1152]{0,1:T(8,128)S(1)} %get-tuple-element.47, f32[384]{0:T(512)S(1)} %get-tuple-element.46, s32[384]{0:T(512)S(1)} %copy-done.24, s32[1152]{0:T(1024)S(1)} %eq.89, pred[1152]{0:T(1024)(128)(4,1)S(1)} %and.49, ...), kind=kLoop, calls=%fused_computation.49 | loop fusion | flops 7518336 | bytes 8870016 | tf_op jit(solution)/shard_map/reduce_sum | solution.py:36
  72.6 1.6 fusion.37
  74.2 1.6 fusion.38
  75.8 1.6 fusion.39
  77.3 1.6 fusion.40
  78.9 1.6 fusion.41
  80.5 5.5 %collective-permute-start.10 = (bf16[640,384]{1,0:T(8,128)(2,1)S(1)}, bf16[640,384]{1,0:T(8,128)(2,1)}, u32[]{:S(2)}, u32[]{:S(2)}) collective-permute-start(bf16[640,384]{1,0:T(8,128)(2,1)S(1)} %collective-permute-done.8), channel_id=1, source_target_pairs={{0,4},{4,8},{8,12},{1,5},{5,9},{9,13},{2,6},{6,10},{10,14},{3,7},{... | collective-permute-start | bytes 1474568 | tf_op jit(solution)/shard_map/ppermute | solution.py:18
  86.7 1.3 collective-permute-start.11
  88.0 0.8 copy-done.11
  88.8 3.4 %collective-permute-start.15 = (bf16[640,384]{1,0:T(8,128)(2,1)S(1)}, bf16[640,384]{1,0:T(8,128)(2,1)S(1)}, u32[]{:S(2)}, u32[]{:S(2)}) collective-permute-start(bf16[640,384]{1,0:T(8,128)(2,1)S(1)} %collective-permute-done.9), channel_id=1, source_target_pairs={{0,16},{4,20},{16,0},{20,4},{1,17},{5,21},{17,1},{21,5},{2,18},{6,... | collective-permute-start | bytes 1474568 | tf_op jit(solution)/shard_map/ppermute | solution.py:26
  92.3 5.6 %collective-permute-done.11 = bf16[640,384]{1,0:T(8,128)(2,1)} collective-permute-done((bf16[640,384]{1,0:T(8,128)(2,1)S(1)}, bf16[640,384]{1,0:T(8,128)(2,1)}, u32[]{:S(2)}, u32[]{:S(2)}) %collective-permute-start.11) | collective-permute-done | bytes 491552 | tf_op jit(solution)/shard_map/ppermute | solution.py:18
  97.8 2.0 %collective-permute-done.15 = bf16[640,384]{1,0:T(8,128)(2,1)S(1)} collective-permute-done((bf16[640,384]{1,0:T(8,128)(2,1)S(1)}, bf16[640,384]{1,0:T(8,128)(2,1)S(1)}, u32[]{:S(2)}, u32[]{:S(2)}) %collective-permute-start.15) | collective-permute-done | bytes 491552 | tf_op jit(solution)/shard_map/ppermute | solution.py:26
  99.8 1.6 collective-permute-start.17
  101.6 0.8 constant_dynamic-slice_fusion.2
  103.1 3.6 %collective-permute-start.20 = (bf16[640,384]{1,0:T(8,128)(2,1)}, bf16[640,384]{1,0:T(8,128)(2,1)S(1)}, u32[]{:S(2)}, u32[]{:S(2)}) collective-permute-start(bf16[640,384]{1,0:T(8,128)(2,1)} %collective-permute-done.11), channel_id=1, source_target_pairs={{0,16},{16,0},{1,17},{17,1},{2,18},{18,2},{3,19},{19,3}} | collective-permute-start | bytes 1474568 | tf_op jit(solution)/shard_map/ppermute | solution.py:26
  106.8 3.9 %collective-permute-done.16 = bf16[384,640]{0,1:T(8,128)(2,1)} collective-permute-done((bf16[384,640]{0,1:T(8,128)(2,1)}, bf16[384,640]{0,1:T(8,128)(2,1)}, u32[]{:S(2)}, u32[]{:S(2)}) %collective-permute-start.16) | collective-permute-done | bytes 491552 | tf_op jit(solution)/shard_map/ppermute | solution.py:47
  110.7 13.3 %collective-permute-done.17 = bf16[384,640]{0,1:T(8,128)(2,1)S(1)} collective-permute-done((bf16[384,640]{0,1:T(8,128)(2,1)}, bf16[384,640]{0,1:T(8,128)(2,1)S(1)}, u32[]{:S(2)}, u32[]{:S(2)}) %collective-permute-start.17) | collective-permute-done | bytes 491552 | tf_op jit(solution)/shard_map/ppermute | solution.py:47
  124.0 0.8 copy-done.23
  124.8 1.8 %select_select_fusion.3 = (bf16[384,640]{0,1:T(8,128)(2,1)S(1)}, bf16[384,640]{0,1:T(8,128)(2,1)S(1)}, bf16[384,640]{0,1:T(8,128)(2,1)S(1)}, bf16[384,640]{0,1:T(8,128)(2,1)S(1)}) fusion(bf16[384,640]{0,1:T(8,128)(2,1)} %collective-permute-done.16, bf16[384,640]{0,1:T(8,128)(2,1)} %copy-done.23, bf16[384,640]{0,1:T(8,128)(2,1)} %collective-permute-done.18, ...), kind=kLoop, calls=%fused_computation.69 | loop fusion | flops 2949120 | bytes 3932172 | tf_op jit(solution)/shard_map/jit(_where)/select_n | solution.py:52
  127.6 1.6 fusion.61
  130.8 1.6 fusion.49
  132.4 1.6 fusion.45
  137.8 1.4 broadcast_select_fusion.1
  139.2 19.6 %all-gather.2.cloned.1.call-done = bf16[5120,256]{1,0:T(8,128)(2,1)} async-done(((bf16[640,256]{1,0:T(8,128)(2,1)}), bf16[5120,256]{1,0:T(8,128)(2,1)}) %all-gather.2.cloned.1.call-update) | async-done | bytes 2621456 | tf_op jit(solution)/shard_map/all_gather | solution.py:80
  158.8 2.7 %fusion.31 = bf16[384,256]{0,1:T(8,128)(2,1)S(1)} fusion(bf16[5120,256]{1,0:T(8,128)(2,1)} %all-gather.2.cloned.1.call-done, bf16[384,640]{0,1:T(8,128)(2,1)S(1)} %get-tuple-element.41, bf16[384,640]{0,1:T(8,128)(2,1)} %copy-done.1, bf16[384,640]{0,1:T(8,128)(2,1)} %copy-done.3, bf16[384,640]{0,1:T(8,128)(2,1)S(1)} %get-tuple-element.40), kind=kOutput, calls=%fused_computation.52 | convolution fusion | flops 511279104 | bytes 3473408 | tf_op jit(solution)/shard_map/dot_general | solution.py:178
  161.5 0.9 fusion.34
  162.6 1.3 copy.9
  (97 shorter events, 12.3 us)
Async XLA Ops:
  6.5 19.0 %copy-start = (bf16[640,1280]{1,0:T(8,128)(2,1)S(1)}, bf16[640,1280]{1,0:T(8,128)(2,1)}, u32[]{:S(2)}) copy-start(bf16[640,1280]{1,0:T(8,128)(2,1)} %param.10) | copy-start | bytes 4915204
  6.5 152.3 %all-gather.2.cloned.1.call-start = ((), (), s32[]{:S(2)}) async-start(), calls=%async_computation | async-start | bytes 2949120 | tf_op jit(solution)/shard_map/all_gather | solution.py:80
  6.5 36.5 %collective-permute-start.2 = (bf16[384,640]{1,0:T(8,128)(2,1)}, bf16[384,640]{1,0:T(8,128)(2,1)}, u32[]{:S(2)}, u32[]{:S(2)}) collective-permute-start(bf16[384,640]{1,0:T(8,128)(2,1)} %param.8), channel_id=1, source_target_pairs={{0,4},{4,8},{8,12},{1,5},{5,9},{9,13},{2,6},{6,10},{10,14},{3,7},{... | collective-permute-start | bytes 1474568 | tf_op jit(solution)/shard_map/ppermute | solution.py:18
  12.4 32.3 %collective-permute-start.3 = (bf16[384,640]{1,0:T(8,128)(2,1)}, bf16[384,640]{1,0:T(8,128)(2,1)}, u32[]{:S(2)}, u32[]{:S(2)}) collective-permute-start(bf16[384,640]{1,0:T(8,128)(2,1)} %param.8), channel_id=1, source_target_pairs={{4,0},{8,4},{12,8},{5,1},{9,5},{13,9},{6,2},{10,6},{14,10},{7,3},{... | collective-permute-start | bytes 1474568 | tf_op jit(solution)/shard_map/ppermute | solution.py:18
  13.7 33.6 %collective-permute-start.4 = (bf16[384,640]{1,0:T(8,128)(2,1)}, bf16[384,640]{1,0:T(8,128)(2,1)}, u32[]{:S(2)}, u32[]{:S(2)}) collective-permute-start(bf16[384,640]{1,0:T(8,128)(2,1)} %param.9), channel_id=1, source_target_pairs={{0,4},{4,8},{8,12},{1,5},{5,9},{9,13},{2,6},{6,10},{10,14},{3,7},{... | collective-permute-start | bytes 1474568 | tf_op jit(solution)/shard_map/ppermute | solution.py:18
  19.1 28.3 %collective-permute-start.5 = (bf16[384,640]{1,0:T(8,128)(2,1)}, bf16[384,640]{1,0:T(8,128)(2,1)}, u32[]{:S(2)}, u32[]{:S(2)}) collective-permute-start(bf16[384,640]{1,0:T(8,128)(2,1)} %param.9), channel_id=1, source_target_pairs={{4,0},{8,4},{12,8},{5,1},{9,5},{13,9},{6,2},{10,6},{14,10},{7,3},{... | collective-permute-start | bytes 1474568 | tf_op jit(solution)/shard_map/ppermute | solution.py:18
  20.3 12.6 %collective-permute-start.6 = (s32[384]{0:T(512)}, s32[384]{0:T(512)S(1)}, u32[]{:S(2)}, u32[]{:S(2)}) collective-permute-start(s32[384]{0:T(512)} %param.12), channel_id=1, source_target_pairs={{0,4},{4,8},{8,12},{1,5},{5,9},{9,13},{2,6},{6,10},{10,14},{3,7},{... | collective-permute-start | bytes 4616 | tf_op jit(solution)/shard_map/ppermute | solution.py:18
  25.6 21.8 %copy-start.8 = (bf16[384,640]{1,0:T(8,128)(2,1)S(1)}, bf16[384,640]{1,0:T(8,128)(2,1)}, u32[]{:S(2)}) copy-start(bf16[384,640]{1,0:T(8,128)(2,1)} %param.9) | copy-start | bytes 1474564
  32.9 6.1 %collective-permute-start.7 = (s32[384]{0:T(512)}, s32[384]{0:T(512)S(1)}, u32[]{:S(2)}, u32[]{:S(2)}) collective-permute-start(s32[384]{0:T(512)} %param.12), channel_id=1, source_target_pairs={{4,0},{8,4},{12,8},{5,1},{9,5},{13,9},{6,2},{10,6},{14,10},{7,3},{... | collective-permute-start | bytes 4616 | tf_op jit(solution)/shard_map/ppermute | solution.py:18
  39.1 12.4 %collective-permute-start = (bf16[640,384]{1,0:T(8,128)(2,1)S(1)}, bf16[640,384]{1,0:T(8,128)(2,1)S(1)}, u32[]{:S(2)}, u32[]{:S(2)}) collective-permute-start(bf16[640,384]{1,0:T(8,128)(2,1)S(1)} %constant_dynamic-slice_fusion), channel_id=1, source_target_pairs={{0,4},{4,8},{8,12},{1,5},{5,9},{9,13},{2,6},{6,10},{10,14},{3,7},{... | collective-permute-start | bytes 1474568 | tf_op jit(solution)/shard_map/ppermute | solution.py:18
  43.0 12.7 %collective-permute-start.1 = (bf16[640,384]{1,0:T(8,128)(2,1)S(1)}, bf16[640,384]{1,0:T(8,128)(2,1)}, u32[]{:S(2)}, u32[]{:S(2)}) collective-permute-start(bf16[640,384]{1,0:T(8,128)(2,1)S(1)} %constant_dynamic-slice_fusion), channel_id=1, source_target_pairs={{4,0},{8,4},{12,8},{5,1},{9,5},{13,9},{6,2},{10,6},{14,10},{7,3},{... | collective-permute-start | bytes 1474568 | tf_op jit(solution)/shard_map/ppermute | solution.py:18
  47.3 8.4 %copy-start.24 = (s32[384]{0:T(512)S(1)}, s32[384]{0:T(512)}, u32[]{:S(2)}) copy-start(s32[384]{0:T(512)} %param.12) | copy-start | bytes 4612
  51.5 13.4 %copy-start.9 = (bf16[640,384]{1,0:T(8,128)(2,1)}, bf16[640,384]{1,0:T(8,128)(2,1)S(1)}, u32[]{:S(2)}) copy-start(bf16[640,384]{1,0:T(8,128)(2,1)S(1)} %collective-permute-done) | copy-start | bytes 1474564
  55.7 2.2 %copy-start.6 = (bf16[3,384,640]{2,1,0:T(8,128)(2,1)S(1)}, bf16[3,384,640]{2,1,0:T(8,128)(2,1)}, u32[]{:S(2)}) copy-start(bf16[3,384,640]{2,1,0:T(8,128)(2,1)} %pad_maximum_fusion.1) | copy-start | bytes 4423684
  57.9 1.6 copy-start.26
  61.4 19.1 %collective-permute-start.8 = (bf16[640,384]{1,0:T(8,128)(2,1)S(1)}, bf16[640,384]{1,0:T(8,128)(2,1)S(1)}, u32[]{:S(2)}, u32[]{:S(2)}) collective-permute-start(bf16[640,384]{1,0:T(8,128)(2,1)S(1)} %collective-permute-done), channel_id=1, source_target_pairs={{0,4},{4,8},{8,12},{1,5},{5,9},{9,13},{2,6},{6,10},{10,14},{3,7},{... | collective-permute-start | bytes 1474568 | tf_op jit(solution)/shard_map/ppermute | solution.py:18
  64.9 23.1 %collective-permute-start.12 = (bf16[640,384]{1,0:T(8,128)(2,1)S(1)}, bf16[640,384]{1,0:T(8,128)(2,1)S(1)}, u32[]{:S(2)}, u32[]{:S(2)}) collective-permute-start(bf16[640,384]{1,0:T(8,128)(2,1)S(1)} %collective-permute-done), channel_id=1, source_target_pairs={{4,20},{8,24},{12,28},{20,4},{24,8},{28,12},{5,21},{9,25},{13,29},... | collective-permute-start | bytes 1474568 | tf_op jit(solution)/shard_map/ppermute | solution.py:26
  65.6 14.9 %collective-permute-start.9 = (bf16[640,384]{1,0:T(8,128)(2,1)}, bf16[640,384]{1,0:T(8,128)(2,1)S(1)}, u32[]{:S(2)}, u32[]{:S(2)}) collective-permute-start(bf16[640,384]{1,0:T(8,128)(2,1)} %collective-permute-done.1), channel_id=1, source_target_pairs={{4,0},{8,4},{12,8},{5,1},{9,5},{13,9},{6,2},{10,6},{14,10},{7,3},{... | collective-permute-start | bytes 1474568 | tf_op jit(solution)/shard_map/ppermute | solution.py:18
  66.9 25.3 %collective-permute-start.13 = (bf16[640,384]{1,0:T(8,128)(2,1)}, bf16[640,384]{1,0:T(8,128)(2,1)S(1)}, u32[]{:S(2)}, u32[]{:S(2)}) collective-permute-start(bf16[640,384]{1,0:T(8,128)(2,1)} %collective-permute-done.1), channel_id=1, source_target_pairs={{0,16},{4,20},{8,24},{16,0},{20,4},{24,8},{1,17},{5,21},{9,25},{17... | collective-permute-start | bytes 1474568 | tf_op jit(solution)/shard_map/ppermute | solution.py:26
  70.3 2.3 %copy-start.5 = (bf16[3,384,640]{2,1,0:T(8,128)(2,1)S(1)}, bf16[3,384,640]{2,1,0:T(8,128)(2,1)}, u32[]{:S(2)}) copy-start(bf16[3,384,640]{2,1,0:T(8,128)(2,1)} %pad_maximum_fusion.2) | copy-start | bytes 4423684
  80.4 11.8 %copy-start.13 = (bf16[640,384]{1,0:T(8,128)(2,1)}, bf16[640,384]{1,0:T(8,128)(2,1)S(1)}, u32[]{:S(2)}) copy-start(bf16[640,384]{1,0:T(8,128)(2,1)S(1)} %collective-permute-done.8) | copy-start | bytes 1474564
  80.5 19.4 %copy-start.17 = (bf16[640,384]{1,0:T(8,128)(2,1)}, bf16[640,384]{1,0:T(8,128)(2,1)S(1)}, u32[]{:S(2)}) copy-start(bf16[640,384]{1,0:T(8,128)(2,1)S(1)} %collective-permute-done.9) | copy-start | bytes 1474564
  80.5 11.8 %collective-permute-start.10 = (bf16[640,384]{1,0:T(8,128)(2,1)S(1)}, bf16[640,384]{1,0:T(8,128)(2,1)}, u32[]{:S(2)}, u32[]{:S(2)}) collective-permute-start(bf16[640,384]{1,0:T(8,128)(2,1)S(1)} %collective-permute-done.8), channel_id=1, source_target_pairs={{0,4},{4,8},{8,12},{1,5},{5,9},{9,13},{2,6},{6,10},{10,14},{3,7},{... | collective-permute-start | bytes 1474568 | tf_op jit(solution)/shard_map/ppermute | solution.py:18
  86.0 11.8 %collective-permute-start.14 = (bf16[640,384]{1,0:T(8,128)(2,1)S(1)}, bf16[640,384]{1,0:T(8,128)(2,1)S(1)}, u32[]{:S(2)}, u32[]{:S(2)}) collective-permute-start(bf16[640,384]{1,0:T(8,128)(2,1)S(1)} %collective-permute-done.8), channel_id=1, source_target_pairs={{8,24},{12,28},{24,8},{28,12},{9,25},{13,29},{25,9},{29,13},{10,26... | collective-permute-start | bytes 1474568 | tf_op jit(solution)/shard_map/ppermute | solution.py:26
  86.7 11.1 %collective-permute-start.11 = (bf16[640,384]{1,0:T(8,128)(2,1)S(1)}, bf16[640,384]{1,0:T(8,128)(2,1)}, u32[]{:S(2)}, u32[]{:S(2)}) collective-permute-start(bf16[640,384]{1,0:T(8,128)(2,1)S(1)} %collective-permute-done.9), channel_id=1, source_target_pairs={{4,0},{8,4},{12,8},{5,1},{9,5},{13,9},{6,2},{10,6},{14,10},{7,3},{... | collective-permute-start | bytes 1474568 | tf_op jit(solution)/shard_map/ppermute | solution.py:18
  88.0 0.8 copy-start.11
  88.8 11.0 %collective-permute-start.15 = (bf16[640,384]{1,0:T(8,128)(2,1)S(1)}, bf16[640,384]{1,0:T(8,128)(2,1)S(1)}, u32[]{:S(2)}, u32[]{:S(2)}) collective-permute-start(bf16[640,384]{1,0:T(8,128)(2,1)S(1)} %collective-permute-done.9), channel_id=1, source_target_pairs={{0,16},{4,20},{16,0},{20,4},{1,17},{5,21},{17,1},{21,5},{2,18},{6,... | collective-permute-start | bytes 1474568 | tf_op jit(solution)/shard_map/ppermute | solution.py:26
  92.2 5.6 %copy-start.15 = (bf16[640,384]{1,0:T(8,128)(2,1)}, bf16[640,384]{1,0:T(8,128)(2,1)S(1)}, u32[]{:S(2)}) copy-start(bf16[640,384]{1,0:T(8,128)(2,1)S(1)} %collective-permute-done.13) | copy-start | bytes 1474564
  97.8 2.0 %copy-start.19 = (bf16[640,384]{1,0:T(8,128)(2,1)}, bf16[640,384]{1,0:T(8,128)(2,1)S(1)}, u32[]{:S(2)}) copy-start(bf16[640,384]{1,0:T(8,128)(2,1)S(1)} %collective-permute-done.14) | copy-start | bytes 1474564
  99.8 1.6 copy-start.21
  99.8 10.9 %collective-permute-start.16 = (bf16[384,640]{0,1:T(8,128)(2,1)}, bf16[384,640]{0,1:T(8,128)(2,1)}, u32[]{:S(2)}, u32[]{:S(2)}) collective-permute-start(bf16[384,640]{0,1:T(8,128)(2,1)} %fusion.41), channel_id=1, source_target_pairs={{0,3},{1,0},{2,1},{3,2},{4,7},{5,4},{6,5},{7,6},{8,11},{9,8},{10,9... | collective-permute-start | bytes 1474568 | tf_op jit(solution)/shard_map/ppermute | solution.py:47
  99.8 24.2 %collective-permute-start.17 = (bf16[384,640]{0,1:T(8,128)(2,1)}, bf16[384,640]{0,1:T(8,128)(2,1)S(1)}, u32[]{:S(2)}, u32[]{:S(2)}) collective-permute-start(bf16[384,640]{0,1:T(8,128)(2,1)} %fusion.41), channel_id=1, source_target_pairs={{0,2},{1,3},{2,0},{3,1},{4,6},{5,7},{6,4},{7,5},{8,10},{9,11},{10,... | collective-permute-start | bytes 1474568 | tf_op jit(solution)/shard_map/ppermute | solution.py:47
  101.4 23.4 %collective-permute-start.18 = (bf16[384,640]{0,1:T(8,128)(2,1)}, bf16[384,640]{0,1:T(8,128)(2,1)}, u32[]{:S(2)}, u32[]{:S(2)}) collective-permute-start(bf16[384,640]{0,1:T(8,128)(2,1)} %fusion.41), channel_id=1, source_target_pairs={{0,1},{1,2},{2,3},{3,0},{4,5},{5,6},{6,7},{7,4},{8,9},{9,10},{10,1... | collective-permute-start | bytes 1474568 | tf_op jit(solution)/shard_map/ppermute | solution.py:47
  102.4 33.7 %collective-permute-start.19 = (bf16[640,384]{1,0:T(8,128)(2,1)}, bf16[640,384]{1,0:T(8,128)(2,1)S(1)}, u32[]{:S(2)}, u32[]{:S(2)}) collective-permute-start(bf16[640,384]{1,0:T(8,128)(2,1)} %collective-permute-done.10), channel_id=1, source_target_pairs={{12,28},{28,12},{13,29},{29,13},{14,30},{30,14},{15,31},{31,15}} | collective-permute-start | bytes 1474568 | tf_op jit(solution)/shard_map/ppermute | solution.py:26
  103.1 33.5 %collective-permute-start.20 = (bf16[640,384]{1,0:T(8,128)(2,1)}, bf16[640,384]{1,0:T(8,128)(2,1)S(1)}, u32[]{:S(2)}, u32[]{:S(2)}) collective-permute-start(bf16[640,384]{1,0:T(8,128)(2,1)} %collective-permute-done.11), channel_id=1, source_target_pairs={{0,16},{16,0},{1,17},{17,1},{2,18},{18,2},{3,19},{19,3}} | collective-permute-start | bytes 1474568 | tf_op jit(solution)/shard_map/ppermute | solution.py:26
  124.0 0.8 copy-start.23
  126.7 1.0 copy-start.3
  127.6 1.6 copy-start.10
  127.6 2.2 %copy-start.14 = (bf16[640,384]{1,0:T(8,128)(2,1)S(1)}, bf16[640,384]{1,0:T(8,128)(2,1)}, u32[]{:S(2)}) copy-start(bf16[640,384]{1,0:T(8,128)(2,1)} %copy-done.13) | copy-start | bytes 1474564
  129.3 1.0 copy-start.18
  130.8 3.2 %copy-start.12 = (bf16[640,384]{1,0:T(8,128)(2,1)S(1)}, bf16[640,384]{1,0:T(8,128)(2,1)}, u32[]{:S(2)}) copy-start(bf16[640,384]{1,0:T(8,128)(2,1)} %copy-done.11) | copy-start | bytes 1474564
  132.4 2.1 %copy-start.16 = (bf16[640,384]{1,0:T(8,128)(2,1)S(1)}, bf16[640,384]{1,0:T(8,128)(2,1)}, u32[]{:S(2)}) copy-start(bf16[640,384]{1,0:T(8,128)(2,1)} %copy-done.15) | copy-start | bytes 1474564
  134.0 1.1 copy-start.20
  134.6 1.1 copy-start.22
  139.2 22.3 %copy-start.2 = (bf16[384,640]{0,1:T(8,128)(2,1)S(1)}, bf16[384,640]{0,1:T(8,128)(2,1)}, u32[]{:S(2)}) copy-start(bf16[384,640]{0,1:T(8,128)(2,1)} %copy-done.1) | copy-start | bytes 1474564
  158.8 2.7 %copy-start.4 = (bf16[384,640]{0,1:T(8,128)(2,1)S(1)}, bf16[384,640]{0,1:T(8,128)(2,1)}, u32[]{:S(2)}) copy-start(bf16[384,640]{0,1:T(8,128)(2,1)} %copy-done.3) | copy-start | bytes 1474564
  158.8 2.7 %copy-start.25 = (bf16[5120,256]{1,0:T(8,128)(2,1)S(1)}, bf16[5120,256]{1,0:T(8,128)(2,1)}, u32[]{:S(2)}) copy-start(bf16[5120,256]{1,0:T(8,128)(2,1)} %all-gather.2.cloned.1.call-done) | copy-start | bytes 7864324
  161.5 1.0 copy-start.7
  (1 other events, 0.8 us)
Sparse Core Ops, SparseCore 0:
  102.5 56.3 all-gather.1

commit v9 on v8

--- a/solution.py
+++ b/solution.py
@@ -106,8 +106,8 @@
 
     arrivals = []
     if line_path:
-        from_left, from_right, key_stack, value_stack, clip_stack = lax.optimization_barrier(
-            (from_left, from_right, key_stack, value_stack, clip_stack)
+        from_left, from_right, key_stack, value_stack, clip_stack, both_sc = lax.optimization_barrier(
+            (from_left, from_right, key_stack, value_stack, clip_stack, both_sc)
         )
         arrivals.append((-1, from_left, to_twin(from_left, seq_count, range(1, seq_count))))
         arrivals.append((1, from_right, to_twin(from_right, seq_count, range(seq_count - 1))))

time: 172 us -> 180 us (1.047)
  waiting for transfers between devices: 60.4 us -> 74 us
  matrix products: 28.3 us -> 25.7 us
    ppermute x12, waiting for transfers between devices: 21.5 us -> 54.4 us  [from_behind(): return lax.ppermute(value, axis, pairs)]
    all_gather x1, waiting for transfers between devices: 19.6 us -> 0.01 us  [on_device(): lax.all_gather(own_full[:, :sc_width], ('rep', 'seq'), axis=0, tiled=True)]
  transfers between devices with their start and end apart: 22 -> 22, of which waited for: 9 -> 11; matrix products, arithmetic and copies ran while one was open for 19% -> 17% of each run, Pallas kernels for 0% -> 0%
where the time goes in v9:
time: 180 us; the launch traced here: 179 us
  waiting for transfers between devices  74 us (41%)
  starting transfers between devices  50.6 us (28%)
  matrix products  25.7 us (14%)
  between operations  13.9 us (8%)
  other arithmetic  10.3 us (6%)
  local copies, waits for them, and re-layouts  4.47 us (2%)
    ppermute x12, waiting for transfers between devices, from_behind(): return lax.ppermute(value, axis, pairs)  54.4 us
    ppermute x12, starting transfers between devices, from_behind(): return lax.ppermute(value, axis, pairs)  36.6 us
    ppermute x3, waiting for transfers between devices, exchange_heads(): received.append(lax.ppermute(attended, 'head', pairs))  18.4 us
    ppermute x6, starting transfers between devices, to_twin(): return lax.ppermute(value, ('rep', 'seq'), pairs)  12.3 us
    dot_general x5, matrix products, attend_head(): jnp.dot(weights, value_head, preferred_element_type=jnp.float32)  7.8 us
    dot_general x6, matrix products, on_device(): jnp.dot(rows, own_block, preferred_element_type=jnp.float32)  7.23 us
    dot_general x5, matrix products, attend_head(): lax.dot_general(query_head, key_head, (((1,), (1,)), ((), ())), preferred...  4.58 us
  transfers between devices with their start and end apart: 22, of which 11 were waited for; matrix products, arithmetic and copies ran while one was open for 17% of the time, Pallas kernels for 0%

profile of v9, /device:TPU:0, one launch (start us, length us, event | category | flops | bytes accessed | tf_op | source)
XLA Modules:
  0.0 179.1 jit_solution(16357979287771978817)
XLA Ops:
  6.6 1.4 copy-done
  8.0 0.7 constant_dynamic-slice_fusion.2
  8.8 5.7 %collective-permute-start.2 = (bf16[384,640]{1,0:T(8,128)(2,1)}, bf16[384,640]{1,0:T(8,128)(2,1)}, u32[]{:S(2)}, u32[]{:S(2)}) collective-permute-start(bf16[384,640]{1,0:T(8,128)(2,1)} %param.8), channel_id=1, source_target_pairs={{0,4},{4,8},{8,12},{1,5},{5,9},{9,13},{2,6},{6,10},{10,14},{3,7},{... | collective-permute-start | bytes 1474568 | tf_op jit(solution)/shard_map/ppermute | solution.py:18
  14.5 1.3 collective-permute-start.3
  15.8 5.4 %collective-permute-start.4 = (bf16[384,640]{1,0:T(8,128)(2,1)}, bf16[384,640]{1,0:T(8,128)(2,1)}, u32[]{:S(2)}, u32[]{:S(2)}) collective-permute-start(bf16[384,640]{1,0:T(8,128)(2,1)} %param.9), channel_id=1, source_target_pairs={{0,4},{4,8},{8,12},{1,5},{5,9},{9,13},{2,6},{6,10},{10,14},{3,7},{... | collective-permute-start | bytes 1474568 | tf_op jit(solution)/shard_map/ppermute | solution.py:18
  21.1 1.3 collective-permute-start.5
  22.4 4.6 %collective-permute-start.6 = (s32[384]{0:T(512)}, s32[384]{0:T(512)S(1)}, u32[]{:S(2)}, u32[]{:S(2)}) collective-permute-start(s32[384]{0:T(512)} %param.12), channel_id=1, source_target_pairs={{0,4},{4,8},{8,12},{1,5},{5,9},{9,13},{2,6},{6,10},{10,14},{3,7},{... | collective-permute-start | bytes 4616 | tf_op jit(solution)/shard_map/ppermute | solution.py:18
  27.8 17.8 %collective-permute-done.6 = s32[384]{0:T(512)S(1)} collective-permute-done((s32[384]{0:T(512)}, s32[384]{0:T(512)S(1)}, u32[]{:S(2)}, u32[]{:S(2)}) %collective-permute-start.6) | collective-permute-done | bytes 1568 | tf_op jit(solution)/shard_map/ppermute | solution.py:18
  45.6 1.3 collective-permute-start.7
  46.9 4.6 %collective-permute-done.7 = s32[384]{0:T(512)S(1)} collective-permute-done((s32[384]{0:T(512)S(1)}, s32[384]{0:T(512)S(1)}, u32[]{:S(2)}, u32[]{:S(2)}) %collective-permute-start.7) | collective-permute-done | bytes 1568 | tf_op jit(solution)/shard_map/ppermute | solution.py:18
  51.5 4.7 %collective-permute-start = (bf16[640,384]{1,0:T(8,128)(2,1)S(1)}, bf16[640,384]{1,0:T(8,128)(2,1)}, u32[]{:S(2)}, u32[]{:S(2)}) collective-permute-start(bf16[640,384]{1,0:T(8,128)(2,1)S(1)} %constant_dynamic-slice_fusion), channel_id=1, source_target_pairs={{0,4},{4,8},{8,12},{1,5},{5,9},{9,13},{2,6},{6,10},{10,14},{3,7},{... | collective-permute-start | bytes 1474568 | tf_op jit(solution)/shard_map/ppermute | solution.py:18
  56.2 1.3 collective-permute-start.1
  57.8 2.5 %pad_maximum_fusion.1 = bf16[3,384,640]{2,1,0:T(8,128)(2,1)} fusion(bf16[1,384,640]{2,1,0:T(8,128)(2,1)} %bitcast.2, bf16[1,384,640]{2,1,0:T(8,128)(2,1)} %bitcast.1, bf16[1,384,640]{2,1,0:T(8,128)(2,1)S(1)} %bitcast.55), kind=kLoop, calls=%fused_computation.27 | loop fusion | flops 1474560 | bytes 2949120 | tf_op jit(solution)/shard_map/stack | solution.py:103
  60.4 2.6 %pad_maximum_fusion.2 = bf16[3,384,640]{2,1,0:T(8,128)(2,1)} fusion(bf16[1,384,640]{2,1,0:T(8,128)(2,1)} %bitcast.5, bf16[1,384,640]{2,1,0:T(8,128)(2,1)} %bitcast.4, bf16[1,384,640]{2,1,0:T(8,128)(2,1)S(1)} %bitcast.56), kind=kLoop, calls=%fused_computation.28 | loop fusion | flops 1474560 | bytes 2949120 | tf_op jit(solution)/shard_map/stack | solution.py:104
  62.9 13.5 %collective-permute-done = bf16[640,384]{1,0:T(8,128)(2,1)} collective-permute-done((bf16[640,384]{1,0:T(8,128)(2,1)S(1)}, bf16[640,384]{1,0:T(8,128)(2,1)}, u32[]{:S(2)}, u32[]{:S(2)}) %collective-permute-start) | collective-permute-done | bytes 491552 | tf_op jit(solution)/shard_map/ppermute | solution.py:18
  76.5 7.3 %collective-permute-done.1 = bf16[640,384]{1,0:T(8,128)(2,1)} collective-permute-done((bf16[640,384]{1,0:T(8,128)(2,1)S(1)}, bf16[640,384]{1,0:T(8,128)(2,1)}, u32[]{:S(2)}, u32[]{:S(2)}) %collective-permute-start.1) | collective-permute-done | bytes 491552 | tf_op jit(solution)/shard_map/ppermute | solution.py:18
  83.8 2.1 %fusion.107 = (f32[384]{0:T(512)S(1)}, f32[384,1152]{0,1:T(8,128)S(1)}) fusion(bf16[384,640]{1,0:T(8,128)(2,1)S(1)} %copy-done.15, bf16[1152,640]{1,0:T(8,128)(2,1)} %bitcast.50, s32[1152]{0:T(1024)S(1)} %eq.89, s32[384]{0:T(512)S(1)} %copy-done.13, pred[1152]{0:T(1024)(128)(4,1)S(1)} %and.49), kind=kOutput, calls=%fused_computation.143 | convolution fusion | flops 115457664 | bytes 2176512 | tf_op jit(solution)/shard_map/dot_general | solution.py:30
  88.4 4.1 %collective-permute-start.8 = (bf16[640,384]{1,0:T(8,128)(2,1)}, bf16[640,384]{1,0:T(8,128)(2,1)S(1)}, u32[]{:S(2)}, u32[]{:S(2)}) collective-permute-start(bf16[640,384]{1,0:T(8,128)(2,1)} %collective-permute-done), channel_id=1, source_target_pairs={{0,4},{4,8},{8,12},{1,5},{5,9},{9,13},{2,6},{6,10},{10,14},{3,7},{... | collective-permute-start | bytes 1474568 | tf_op jit(solution)/shard_map/ppermute | solution.py:18
  92.5 0.7 collective-permute-start.12
  93.2 1.3 collective-permute-start.9
  94.5 3.3 %collective-permute-start.13 = (bf16[640,384]{1,0:T(8,128)(2,1)}, bf16[640,384]{1,0:T(8,128)(2,1)S(1)}, u32[]{:S(2)}, u32[]{:S(2)}) collective-permute-start(bf16[640,384]{1,0:T(8,128)(2,1)} %collective-permute-done.1), channel_id=1, source_target_pairs={{0,16},{4,20},{8,24},{16,0},{20,4},{24,8},{1,17},{5,21},{9,25},{17... | collective-permute-start | bytes 1474568 | tf_op jit(solution)/shard_map/ppermute | solution.py:26
  97.9 2.3 %fusion.28 = (f32[384]{0:T(512)S(1)}, f32[384]{0:T(512)S(1)}, f32[384]{0:T(512)S(1)}, f32[384]{0:T(512)S(1)}, f32[384]{0:T(512)S(1)}) fusion(f32[384,1152]{0,1:T(8,128)S(1)} %get-tuple-element.49, f32[384]{0:T(512)S(1)} %get-tuple-element.48, s32[384]{0:T(512)S(1)} %copy-done.13, s32[1152]{0:T(1024)S(1)} %eq.89, pred[1152]{0:T(1024)(128)(4,1)S(1)} %and.49, ...), kind=kLoop, calls=%fused_computation.49 | loop fusion | flops 7518336 | bytes 8870016 | tf_op jit(solution)/shard_map/reduce_sum | solution.py:36
  100.2 1.6 fusion.37
  101.7 1.6 fusion.38
  103.3 1.6 fusion.39
  104.8 1.6 fusion.40
  106.4 1.6 fusion.41
  108.0 1.9 %collective-permute-done.9 = bf16[640,384]{1,0:T(8,128)(2,1)S(1)} collective-permute-done((bf16[640,384]{1,0:T(8,128)(2,1)}, bf16[640,384]{1,0:T(8,128)(2,1)S(1)}, u32[]{:S(2)}, u32[]{:S(2)}) %collective-permute-start.9) | collective-permute-done | bytes 491552 | tf_op jit(solution)/shard_map/ppermute | solution.py:18
  109.9 4.4 %collective-permute-start.10 = (bf16[640,384]{1,0:T(8,128)(2,1)S(1)}, bf16[640,384]{1,0:T(8,128)(2,1)}, u32[]{:S(2)}, u32[]{:S(2)}) collective-permute-start(bf16[640,384]{1,0:T(8,128)(2,1)S(1)} %collective-permute-done.8), channel_id=1, source_target_pairs={{0,4},{4,8},{8,12},{1,5},{5,9},{9,13},{2,6},{6,10},{10,14},{3,7},{... | collective-permute-start | bytes 1474568 | tf_op jit(solution)/shard_map/ppermute | solution.py:18
  115.0 1.3 collective-permute-start.11
  116.4 3.4 %collective-permute-start.15 = (bf16[640,384]{1,0:T(8,128)(2,1)S(1)}, bf16[640,384]{1,0:T(8,128)(2,1)S(1)}, u32[]{:S(2)}, u32[]{:S(2)}) collective-permute-start(bf16[640,384]{1,0:T(8,128)(2,1)S(1)} %collective-permute-done.9), channel_id=1, source_target_pairs={{0,16},{4,20},{16,0},{20,4},{1,17},{5,21},{17,1},{21,5},{2,18},{6,... | collective-permute-start | bytes 1474568 | tf_op jit(solution)/shard_map/ppermute | solution.py:26
  119.7 3.4 %collective-permute-done.10 = bf16[640,384]{1,0:T(8,128)(2,1)} collective-permute-done((bf16[640,384]{1,0:T(8,128)(2,1)S(1)}, bf16[640,384]{1,0:T(8,128)(2,1)}, u32[]{:S(2)}, u32[]{:S(2)}) %collective-permute-start.10) | collective-permute-done | bytes 491552 | tf_op jit(solution)/shard_map/ppermute | solution.py:18
  123.2 5.7 %collective-permute-done.11 = bf16[640,384]{1,0:T(8,128)(2,1)} collective-permute-done((bf16[640,384]{1,0:T(8,128)(2,1)S(1)}, bf16[640,384]{1,0:T(8,128)(2,1)}, u32[]{:S(2)}, u32[]{:S(2)}) %collective-permute-start.11) | collective-permute-done | bytes 491552 | tf_op jit(solution)/shard_map/ppermute | solution.py:18
  128.9 1.2 collective-permute-done.15
  130.1 1.5 collective-permute-start.17
  132.5 3.6 %collective-permute-start.20 = (bf16[640,384]{1,0:T(8,128)(2,1)}, bf16[640,384]{1,0:T(8,128)(2,1)S(1)}, u32[]{:S(2)}, u32[]{:S(2)}) collective-permute-start(bf16[640,384]{1,0:T(8,128)(2,1)} %collective-permute-done.11), channel_id=1, source_target_pairs={{0,16},{16,0},{1,17},{17,1},{2,18},{18,2},{3,19},{19,3}} | collective-permute-start | bytes 1474568 | tf_op jit(solution)/shard_map/ppermute | solution.py:26
  136.1 4.9 %collective-permute-done.16 = bf16[384,640]{0,1:T(8,128)(2,1)} collective-permute-done((bf16[384,640]{0,1:T(8,128)(2,1)}, bf16[384,640]{0,1:T(8,128)(2,1)}, u32[]{:S(2)}, u32[]{:S(2)}) %collective-permute-start.16) | collective-permute-done | bytes 491552 | tf_op jit(solution)/shard_map/ppermute | solution.py:47
  141.0 13.4 %collective-permute-done.17 = bf16[384,640]{0,1:T(8,128)(2,1)} collective-permute-done((bf16[384,640]{0,1:T(8,128)(2,1)}, bf16[384,640]{0,1:T(8,128)(2,1)}, u32[]{:S(2)}, u32[]{:S(2)}) %collective-permute-start.17) | collective-permute-done | bytes 491552 | tf_op jit(solution)/shard_map/ppermute | solution.py:47
  154.5 1.8 %select_select_fusion.3 = (bf16[384,640]{0,1:T(8,128)(2,1)S(1)}, bf16[384,640]{0,1:T(8,128)(2,1)S(1)}, bf16[384,640]{0,1:T(8,128)(2,1)S(1)}, bf16[384,640]{0,1:T(8,128)(2,1)S(1)}) fusion(bf16[384,640]{0,1:T(8,128)(2,1)} %collective-permute-done.16, bf16[384,640]{0,1:T(8,128)(2,1)} %collective-permute-done.17, bf16[384,640]{0,1:T(8,128)(2,1)} %collective-permute-done.18, ...), kind=kLoop, calls=%fused_computation.69 | loop fusion | flops 2949120 | bytes 3932172 | tf_op jit(solution)/shard_map/jit(_where)/select_n | solution.py:52
  156.5 1.5 fusion.65
  158.1 1.6 fusion.61
  160.7 1.5 fusion.49
  162.2 1.6 fusion.45
  165.9 0.7 copy-done.14
  166.6 0.9 fusion.31
  168.1 0.9 fusion.34
  170.2 0.7 broadcast_select_fusion.1
  171.0 1.3 copy.9
  (77 shorter events, 10.3 us)
Async XLA Ops:
  6.5 1.5 copy-start
  6.5 51.3 %copy-start.3 = (bf16[384,640]{1,0:T(8,128)(2,1)S(1)}, bf16[384,640]{1,0:T(8,128)(2,1)}, u32[]{:S(2)}) copy-start(bf16[384,640]{1,0:T(8,128)(2,1)} %param.8) | copy-start | bytes 1474564
  6.5 39.0 %copy-start.13 = (s32[384]{0:T(512)S(1)}, s32[384]{0:T(512)}, u32[]{:S(2)}) copy-start(s32[384]{0:T(512)} %param.12) | copy-start | bytes 4612
  6.5 21.2 %copy-start.16 = (s32[4,27]{1,0:T(4,128)S(1)}, s32[4,27]{1,0:T(4,128)}, u32[]{:S(2)}) copy-start(s32[4,27]{1,0:T(4,128)} %param.11) | copy-start | bytes 1300
  6.5 77.2 %all-gather.2.cloned.1.call-start = ((), (), s32[]{:S(2)}) async-start(), calls=%async_computation | async-start | bytes 2949120 | tf_op jit(solution)/shard_map/all_gather | solution.py:80
  8.8 47.4 %collective-permute-start.2 = (bf16[384,640]{1,0:T(8,128)(2,1)}, bf16[384,640]{1,0:T(8,128)(2,1)}, u32[]{:S(2)}, u32[]{:S(2)}) collective-permute-start(bf16[384,640]{1,0:T(8,128)(2,1)} %param.8), channel_id=1, source_target_pairs={{0,4},{4,8},{8,12},{1,5},{5,9},{9,13},{2,6},{6,10},{10,14},{3,7},{... | collective-permute-start | bytes 1474568 | tf_op jit(solution)/shard_map/ppermute | solution.py:18
  14.5 43.3 %collective-permute-start.3 = (bf16[384,640]{1,0:T(8,128)(2,1)}, bf16[384,640]{1,0:T(8,128)(2,1)}, u32[]{:S(2)}, u32[]{:S(2)}) collective-permute-start(bf16[384,640]{1,0:T(8,128)(2,1)} %param.8), channel_id=1, source_target_pairs={{4,0},{8,4},{12,8},{5,1},{9,5},{13,9},{6,2},{10,6},{14,10},{7,3},{... | collective-permute-start | bytes 1474568 | tf_op jit(solution)/shard_map/ppermute | solution.py:18
  15.8 44.6 %collective-permute-start.4 = (bf16[384,640]{1,0:T(8,128)(2,1)}, bf16[384,640]{1,0:T(8,128)(2,1)}, u32[]{:S(2)}, u32[]{:S(2)}) collective-permute-start(bf16[384,640]{1,0:T(8,128)(2,1)} %param.9), channel_id=1, source_target_pairs={{0,4},{4,8},{8,12},{1,5},{5,9},{9,13},{2,6},{6,10},{10,14},{3,7},{... | collective-permute-start | bytes 1474568 | tf_op jit(solution)/shard_map/ppermute | solution.py:18
  21.1 39.2 %collective-permute-start.5 = (bf16[384,640]{1,0:T(8,128)(2,1)}, bf16[384,640]{1,0:T(8,128)(2,1)}, u32[]{:S(2)}, u32[]{:S(2)}) collective-permute-start(bf16[384,640]{1,0:T(8,128)(2,1)} %param.9), channel_id=1, source_target_pairs={{4,0},{8,4},{12,8},{5,1},{9,5},{13,9},{6,2},{10,6},{14,10},{7,3},{... | collective-permute-start | bytes 1474568 | tf_op jit(solution)/shard_map/ppermute | solution.py:18
  22.4 23.1 %collective-permute-start.6 = (s32[384]{0:T(512)}, s32[384]{0:T(512)S(1)}, u32[]{:S(2)}, u32[]{:S(2)}) collective-permute-start(s32[384]{0:T(512)} %param.12), channel_id=1, source_target_pairs={{0,4},{4,8},{8,12},{1,5},{5,9},{9,13},{2,6},{6,10},{10,14},{3,7},{... | collective-permute-start | bytes 4616 | tf_op jit(solution)/shard_map/ppermute | solution.py:18
  27.7 32.7 %copy-start.4 = (bf16[384,640]{1,0:T(8,128)(2,1)S(1)}, bf16[384,640]{1,0:T(8,128)(2,1)}, u32[]{:S(2)}) copy-start(bf16[384,640]{1,0:T(8,128)(2,1)} %param.9) | copy-start | bytes 1474564
  45.6 5.9 %collective-permute-start.7 = (s32[384]{0:T(512)S(1)}, s32[384]{0:T(512)S(1)}, u32[]{:S(2)}, u32[]{:S(2)}) collective-permute-start(s32[384]{0:T(512)S(1)} %copy-done.13), channel_id=1, source_target_pairs={{4,0},{8,4},{12,8},{5,1},{9,5},{13,9},{6,2},{10,6},{14,10},{7,3},{... | collective-permute-start | bytes 4616 | tf_op jit(solution)/shard_map/ppermute | solution.py:18
  51.5 25.0 %collective-permute-start = (bf16[640,384]{1,0:T(8,128)(2,1)S(1)}, bf16[640,384]{1,0:T(8,128)(2,1)}, u32[]{:S(2)}, u32[]{:S(2)}) collective-permute-start(bf16[640,384]{1,0:T(8,128)(2,1)S(1)} %constant_dynamic-slice_fusion), channel_id=1, source_target_pairs={{0,4},{4,8},{8,12},{1,5},{5,9},{9,13},{2,6},{6,10},{10,14},{3,7},{... | collective-permute-start | bytes 1474568 | tf_op jit(solution)/shard_map/ppermute | solution.py:18
  56.2 27.6 %collective-permute-start.1 = (bf16[640,384]{1,0:T(8,128)(2,1)S(1)}, bf16[640,384]{1,0:T(8,128)(2,1)}, u32[]{:S(2)}, u32[]{:S(2)}) collective-permute-start(bf16[640,384]{1,0:T(8,128)(2,1)S(1)} %constant_dynamic-slice_fusion), channel_id=1, source_target_pairs={{4,0},{8,4},{12,8},{5,1},{9,5},{13,9},{6,2},{10,6},{14,10},{7,3},{... | collective-permute-start | bytes 1474568 | tf_op jit(solution)/shard_map/ppermute | solution.py:18
  60.3 23.5 %copy-start.15 = (bf16[384,640]{1,0:T(8,128)(2,1)S(1)}, bf16[384,640]{1,0:T(8,128)(2,1)}, u32[]{:S(2)}) copy-start(bf16[384,640]{1,0:T(8,128)(2,1)} %param.7) | copy-start | bytes 1474564
  83.8 2.1 %copy-start.2 = (bf16[3,384,640]{2,1,0:T(8,128)(2,1)S(1)}, bf16[3,384,640]{2,1,0:T(8,128)(2,1)}, u32[]{:S(2)}) copy-start(bf16[3,384,640]{2,1,0:T(8,128)(2,1)} %pad_maximum_fusion.1) | copy-start | bytes 4423684
  88.4 19.6 %collective-permute-start.8 = (bf16[640,384]{1,0:T(8,128)(2,1)}, bf16[640,384]{1,0:T(8,128)(2,1)S(1)}, u32[]{:S(2)}, u32[]{:S(2)}) collective-permute-start(bf16[640,384]{1,0:T(8,128)(2,1)} %collective-permute-done), channel_id=1, source_target_pairs={{0,4},{4,8},{8,12},{1,5},{5,9},{9,13},{2,6},{6,10},{10,14},{3,7},{... | collective-permute-start | bytes 1474568 | tf_op jit(solution)/shard_map/ppermute | solution.py:18
  92.5 23.8 %collective-permute-start.12 = (bf16[640,384]{1,0:T(8,128)(2,1)}, bf16[640,384]{1,0:T(8,128)(2,1)S(1)}, u32[]{:S(2)}, u32[]{:S(2)}) collective-permute-start(bf16[640,384]{1,0:T(8,128)(2,1)} %collective-permute-done), channel_id=1, source_target_pairs={{4,20},{8,24},{12,28},{20,4},{24,8},{28,12},{5,21},{9,25},{13,29},... | collective-permute-start | bytes 1474568 | tf_op jit(solution)/shard_map/ppermute | solution.py:26
  93.2 16.7 %collective-permute-start.9 = (bf16[640,384]{1,0:T(8,128)(2,1)}, bf16[640,384]{1,0:T(8,128)(2,1)S(1)}, u32[]{:S(2)}, u32[]{:S(2)}) collective-permute-start(bf16[640,384]{1,0:T(8,128)(2,1)} %collective-permute-done.1), channel_id=1, source_target_pairs={{4,0},{8,4},{12,8},{5,1},{9,5},{13,9},{6,2},{10,6},{14,10},{7,3},{... | collective-permute-start | bytes 1474568 | tf_op jit(solution)/shard_map/ppermute | solution.py:18
  94.5 25.2 %collective-permute-start.13 = (bf16[640,384]{1,0:T(8,128)(2,1)}, bf16[640,384]{1,0:T(8,128)(2,1)S(1)}, u32[]{:S(2)}, u32[]{:S(2)}) collective-permute-start(bf16[640,384]{1,0:T(8,128)(2,1)} %collective-permute-done.1), channel_id=1, source_target_pairs={{0,16},{4,20},{8,24},{16,0},{20,4},{24,8},{1,17},{5,21},{9,25},{17... | collective-permute-start | bytes 1474568 | tf_op jit(solution)/shard_map/ppermute | solution.py:26
  97.9 2.3 %copy-start.1 = (bf16[3,384,640]{2,1,0:T(8,128)(2,1)S(1)}, bf16[3,384,640]{2,1,0:T(8,128)(2,1)}, u32[]{:S(2)}) copy-start(bf16[3,384,640]{2,1,0:T(8,128)(2,1)} %pad_maximum_fusion.2) | copy-start | bytes 4423684
  109.9 20.2 %copy-start.7 = (bf16[640,384]{1,0:T(8,128)(2,1)}, bf16[640,384]{1,0:T(8,128)(2,1)S(1)}, u32[]{:S(2)}) copy-start(bf16[640,384]{1,0:T(8,128)(2,1)S(1)} %collective-permute-done.9) | copy-start | bytes 1474564
  109.9 13.3 %collective-permute-start.10 = (bf16[640,384]{1,0:T(8,128)(2,1)S(1)}, bf16[640,384]{1,0:T(8,128)(2,1)}, u32[]{:S(2)}, u32[]{:S(2)}) collective-permute-start(bf16[640,384]{1,0:T(8,128)(2,1)S(1)} %collective-permute-done.8), channel_id=1, source_target_pairs={{0,4},{4,8},{8,12},{1,5},{5,9},{9,13},{2,6},{6,10},{10,14},{3,7},{... | collective-permute-start | bytes 1474568 | tf_op jit(solution)/shard_map/ppermute | solution.py:18
  114.4 14.5 %collective-permute-start.14 = (bf16[640,384]{1,0:T(8,128)(2,1)S(1)}, bf16[640,384]{1,0:T(8,128)(2,1)S(1)}, u32[]{:S(2)}, u32[]{:S(2)}) collective-permute-start(bf16[640,384]{1,0:T(8,128)(2,1)S(1)} %collective-permute-done.8), channel_id=1, source_target_pairs={{8,24},{12,28},{24,8},{28,12},{9,25},{13,29},{25,9},{29,13},{10,26... | collective-permute-start | bytes 1474568 | tf_op jit(solution)/shard_map/ppermute | solution.py:26
  115.0 13.8 %collective-permute-start.11 = (bf16[640,384]{1,0:T(8,128)(2,1)S(1)}, bf16[640,384]{1,0:T(8,128)(2,1)}, u32[]{:S(2)}, u32[]{:S(2)}) collective-permute-start(bf16[640,384]{1,0:T(8,128)(2,1)S(1)} %collective-permute-done.9), channel_id=1, source_target_pairs={{4,0},{8,4},{12,8},{5,1},{9,5},{13,9},{6,2},{10,6},{14,10},{7,3},{... | collective-permute-start | bytes 1474568 | tf_op jit(solution)/shard_map/ppermute | solution.py:18
  116.4 13.7 %collective-permute-start.15 = (bf16[640,384]{1,0:T(8,128)(2,1)S(1)}, bf16[640,384]{1,0:T(8,128)(2,1)S(1)}, u32[]{:S(2)}, u32[]{:S(2)}) collective-permute-start(bf16[640,384]{1,0:T(8,128)(2,1)S(1)} %collective-permute-done.9), channel_id=1, source_target_pairs={{0,16},{4,20},{16,0},{20,4},{1,17},{5,21},{17,1},{21,5},{2,18},{6,... | collective-permute-start | bytes 1474568 | tf_op jit(solution)/shard_map/ppermute | solution.py:26
  119.7 9.2 %copy-start.5 = (bf16[640,384]{1,0:T(8,128)(2,1)}, bf16[640,384]{1,0:T(8,128)(2,1)S(1)}, u32[]{:S(2)}) copy-start(bf16[640,384]{1,0:T(8,128)(2,1)S(1)} %collective-permute-done.13) | copy-start | bytes 1474564
  128.9 1.2 copy-start.9
  130.1 1.5 copy-start.11
  130.1 10.9 %collective-permute-start.16 = (bf16[384,640]{0,1:T(8,128)(2,1)}, bf16[384,640]{0,1:T(8,128)(2,1)}, u32[]{:S(2)}, u32[]{:S(2)}) collective-permute-start(bf16[384,640]{0,1:T(8,128)(2,1)} %fusion.41), channel_id=1, source_target_pairs={{0,3},{1,0},{2,1},{3,2},{4,7},{5,4},{6,5},{7,6},{8,11},{9,8},{10,9... | collective-permute-start | bytes 1474568 | tf_op jit(solution)/shard_map/ppermute | solution.py:47
  130.1 24.3 %collective-permute-start.17 = (bf16[384,640]{0,1:T(8,128)(2,1)}, bf16[384,640]{0,1:T(8,128)(2,1)}, u32[]{:S(2)}, u32[]{:S(2)}) collective-permute-start(bf16[384,640]{0,1:T(8,128)(2,1)} %fusion.41), channel_id=1, source_target_pairs={{0,2},{1,3},{2,0},{3,1},{4,6},{5,7},{6,4},{7,5},{8,10},{9,11},{10,... | collective-permute-start | bytes 1474568 | tf_op jit(solution)/shard_map/ppermute | solution.py:47
  131.6 22.8 %collective-permute-start.18 = (bf16[384,640]{0,1:T(8,128)(2,1)}, bf16[384,640]{0,1:T(8,128)(2,1)}, u32[]{:S(2)}, u32[]{:S(2)}) collective-permute-start(bf16[384,640]{0,1:T(8,128)(2,1)} %fusion.41), channel_id=1, source_target_pairs={{0,1},{1,2},{2,3},{3,0},{4,5},{5,6},{6,7},{7,4},{8,9},{9,10},{10,1... | collective-permute-start | bytes 1474568 | tf_op jit(solution)/shard_map/ppermute | solution.py:47
  131.8 35.7 %collective-permute-start.19 = (bf16[640,384]{1,0:T(8,128)(2,1)}, bf16[640,384]{1,0:T(8,128)(2,1)S(1)}, u32[]{:S(2)}, u32[]{:S(2)}) collective-permute-start(bf16[640,384]{1,0:T(8,128)(2,1)} %collective-permute-done.10), channel_id=1, source_target_pairs={{12,28},{28,12},{13,29},{29,13},{14,30},{30,14},{15,31},{31,15}} | collective-permute-start | bytes 1474568 | tf_op jit(solution)/shard_map/ppermute | solution.py:26
  132.5 36.5 %collective-permute-start.20 = (bf16[640,384]{1,0:T(8,128)(2,1)}, bf16[640,384]{1,0:T(8,128)(2,1)S(1)}, u32[]{:S(2)}, u32[]{:S(2)}) collective-permute-start(bf16[640,384]{1,0:T(8,128)(2,1)} %collective-permute-done.11), channel_id=1, source_target_pairs={{0,16},{16,0},{1,17},{17,1},{2,18},{18,2},{3,19},{19,3}} | collective-permute-start | bytes 1474568 | tf_op jit(solution)/shard_map/ppermute | solution.py:26
  158.0 2.1 %copy-start.8 = (bf16[640,384]{1,0:T(8,128)(2,1)S(1)}, bf16[640,384]{1,0:T(8,128)(2,1)}, u32[]{:S(2)}) copy-start(bf16[640,384]{1,0:T(8,128)(2,1)} %copy-done.7) | copy-start | bytes 1474564
  162.2 2.1 %copy-start.6 = (bf16[640,384]{1,0:T(8,128)(2,1)S(1)}, bf16[640,384]{1,0:T(8,128)(2,1)}, u32[]{:S(2)}) copy-start(bf16[640,384]{1,0:T(8,128)(2,1)} %copy-done.5) | copy-start | bytes 1474564
  163.8 1.0 copy-start.10
  164.3 1.1 copy-start.12
  164.9 1.8 copy-start.14
Sparse Core Ops, SparseCore 0:
  9.5 72.7 all-gather.1

commit v10 on v6

--- a/solution.py
+++ b/solution.py
@@ -142,16 +142,17 @@
     for step in range(2, seq_count):
         from_left = from_behind(from_left, "seq", 1)
         from_right = from_behind(from_right, "seq", -1)
-        if step == seq_count - 1:
-            twins = [twin for _, _, twin in arrivals]
-            from_left, from_right, attended, twins = lax.optimization_barrier(
-                (from_left, from_right, attended, twins)
+        earlier = [arrivals[-2][2], arrivals[-1][2]]
+        if step == 2:
+            from_left, from_right, attended, earlier = lax.optimization_barrier(
+                (from_left, from_right, attended, earlier)
             )
-            arrivals = [(a, b, twin) for (a, b, _), twin in zip(arrivals, twins)]
         else:
-            from_left, from_right, attended = lax.optimization_barrier(
-                (from_left, from_right, attended)
+            from_left, from_right, earlier = lax.optimization_barrier(
+                (from_left, from_right, earlier)
             )
+        arrivals[-2] = arrivals[-2][:2] + (earlier[0],)
+        arrivals[-1] = arrivals[-1][:2] + (earlier[1],)
         arrivals.append((-step, from_left, to_twin(from_left, seq_count, range(step, seq_count))))
         arrivals.append(
             (step, from_right, to_twin(from_right, seq_count, range(seq_count - step)))

time: 163 us -> 164 us (level)
  the two profiles are of different devices: /device:TPU:8 before, /device:TPU:0 now
where the time goes in v10:
time: 164 us; the launch traced here: 162 us
  waiting for transfers between devices  67.7 us (41%)
  starting transfers between devices  53.7 us (33%)
  matrix products  23 us (14%)
  other arithmetic  12.2 us (7%)
  local copies, waits for them, and re-layouts  4.86 us (3%)
    ppermute x12, starting transfers between devices, from_behind(): return lax.ppermute(value, axis, pairs)  40.5 us
    ppermute x12, waiting for transfers between devices, from_behind(): return lax.ppermute(value, axis, pairs)  40 us
    ppermute x6, waiting for transfers between devices, to_twin(): return lax.ppermute(value, ('rep', 'seq'), pairs)  20.4 us
    ppermute x6, starting transfers between devices, to_twin(): return lax.ppermute(value, ('rep', 'seq'), pairs)  11.5 us
    dot_general x5, matrix products, attend_head(): jnp.dot(weights, value_head, preferred_element_type=jnp.float32)  7.78 us
    ppermute x3, waiting for transfers between devices, exchange_heads(): received.append(lax.ppermute(attended, 'head', pairs))  7.33 us
    dot_general x6, matrix products, on_device(): jnp.dot(rows, own_block, preferred_element_type=jnp.float32)  4.99 us
    dot_general x5, matrix products, attend_head(): lax.dot_general(query_head, key_head, (((1,), (1,)), ((), ())), preferred...  4.69 us
  transfers between devices with their start and end apart: 21, of which 9 were waited for; matrix products, arithmetic and copies ran while one was open for 18% of the time, Pallas kernels for 0%

profile of v10, /device:TPU:0, one launch (start us, length us, event | category | flops | bytes accessed | tf_op | source)
XLA Modules:
  0.0 162.0 jit_solution(832977608078645412)
XLA Ops:
  0.0 5.8 %collective-permute-start.2 = (bf16[384,640]{1,0:T(8,128)(2,1)}, bf16[384,640]{1,0:T(8,128)(2,1)}, u32[]{:S(2)}, u32[]{:S(2)}) collective-permute-start(bf16[384,640]{1,0:T(8,128)(2,1)} %param.8), channel_id=1, source_target_pairs={{0,4},{4,8},{8,12},{1,5},{5,9},{9,13},{2,6},{6,10},{10,14},{3,7},{... | collective-permute-start | bytes 1474568 | tf_op jit(solution)/shard_map/ppermute | solution.py:17
  5.8 2.7 %collective-permute-start.6 = (s32[384]{0:T(512)}, s32[384]{0:T(512)S(1)}, u32[]{:S(2)}, u32[]{:S(2)}) collective-permute-start(s32[384]{0:T(512)} %param.12), channel_id=1, source_target_pairs={{0,4},{4,8},{8,12},{1,5},{5,9},{9,13},{2,6},{6,10},{10,14},{3,7},{... | collective-permute-start | bytes 4616 | tf_op jit(solution)/shard_map/ppermute | solution.py:17
  8.7 3.5 %collective-permute-start = (bf16[640,640]{1,0:T(8,128)(2,1)S(1)}, bf16[640,640]{1,0:T(8,128)(2,1)S(1)}, u32[]{:S(2)}, u32[]{:S(2)}) collective-permute-start(bf16[640,640]{1,0:T(8,128)(2,1)S(1)} %constant_dynamic-slice_fusion.1), channel_id=1, source_target_pairs={{0,4},{4,8},{8,12},{1,5},{5,9},{9,13},{2,6},{6,10},{10,14},{3,7},{... | collective-permute-start | bytes 2457608 | tf_op jit(solution)/shard_map/ppermute | solution.py:17
  12.2 1.3 collective-permute-start.1
  13.5 1.3 collective-permute-start.3
  14.8 2.2 %collective-permute-done.6 = s32[384]{0:T(512)S(1)} collective-permute-done((s32[384]{0:T(512)}, s32[384]{0:T(512)S(1)}, u32[]{:S(2)}, u32[]{:S(2)}) %collective-permute-start.6) | collective-permute-done | bytes 1568 | tf_op jit(solution)/shard_map/ppermute | solution.py:17
  17.0 1.3 collective-permute-start.7
  18.9 25.0 %collective-permute-done.7 = s32[384]{0:T(512)S(1)} collective-permute-done((s32[384]{0:T(512)}, s32[384]{0:T(512)S(1)}, u32[]{:S(2)}, u32[]{:S(2)}) %collective-permute-start.7) | collective-permute-done | bytes 1568 | tf_op jit(solution)/shard_map/ppermute | solution.py:17
  43.9 2.9 %collective-permute-start.4 = (bf16[384,640]{1,0:T(8,128)(2,1)}, bf16[384,640]{1,0:T(8,128)(2,1)}, u32[]{:S(2)}, u32[]{:S(2)}) collective-permute-start(bf16[384,640]{1,0:T(8,128)(2,1)} %param.9), channel_id=1, source_target_pairs={{0,4},{4,8},{8,12},{1,5},{5,9},{9,13},{2,6},{6,10},{10,14},{3,7},{... | collective-permute-start | bytes 1474568 | tf_op jit(solution)/shard_map/ppermute | solution.py:17
  46.8 1.3 collective-permute-start.5
  48.1 0.7 compare_bitcast_fusion
  48.8 0.7 stack.44
  49.5 0.7 fusion.88
  50.5 2.7 %pad_maximum_fusion.1 = bf16[3,384,640]{2,1,0:T(8,128)(2,1)} fusion(bf16[1,384,640]{2,1,0:T(8,128)(2,1)} %bitcast.2, bf16[1,384,640]{2,1,0:T(8,128)(2,1)} %bitcast.1, bf16[1,384,640]{2,1,0:T(8,128)(2,1)} %bitcast.55), kind=kLoop, calls=%fused_computation.27 | loop fusion | flops 1474560 | bytes 2949120 | tf_op jit(solution)/shard_map/stack | solution.py:98
  53.2 2.1 %collective-permute-done.4 = bf16[384,640]{1,0:T(8,128)(2,1)} collective-permute-done((bf16[384,640]{1,0:T(8,128)(2,1)}, bf16[384,640]{1,0:T(8,128)(2,1)}, u32[]{:S(2)}, u32[]{:S(2)}) %collective-permute-start.4) | collective-permute-done | bytes 491552 | tf_op jit(solution)/shard_map/ppermute | solution.py:17
  55.4 4.9 %collective-permute-done.5 = bf16[384,640]{1,0:T(8,128)(2,1)} collective-permute-done((bf16[384,640]{1,0:T(8,128)(2,1)}, bf16[384,640]{1,0:T(8,128)(2,1)}, u32[]{:S(2)}, u32[]{:S(2)}) %collective-permute-start.5) | collective-permute-done | bytes 491552 | tf_op jit(solution)/shard_map/ppermute | solution.py:17
  60.3 2.5 %pad_maximum_fusion.2 = bf16[3,384,640]{2,1,0:T(8,128)(2,1)} fusion(bf16[1,384,640]{2,1,0:T(8,128)(2,1)} %bitcast.5, bf16[1,384,640]{2,1,0:T(8,128)(2,1)} %bitcast.4, bf16[1,384,640]{2,1,0:T(8,128)(2,1)S(1)} %bitcast.56), kind=kLoop, calls=%fused_computation.28 | loop fusion | flops 1474560 | bytes 2949120 | tf_op jit(solution)/shard_map/stack | solution.py:99
  62.8 2.2 %fusion.97 = (f32[384]{0:T(512)S(1)}, f32[384,1152]{0,1:T(8,128)S(1)}) fusion(bf16[384,640]{1,0:T(8,128)(2,1)} %param.7, bf16[1152,640]{1,0:T(8,128)(2,1)} %bitcast.50, s32[1152]{0:T(1024)S(1)} %eq.89, s32[384]{0:T(512)S(1)} %copy-done.12, pred[1152]{0:T(1024)(128)(4,1)S(1)} %and.49), kind=kOutput, calls=%fused_computation.134 | convolution fusion | flops 115457664 | bytes 2171520 | tf_op jit(solution)/shard_map/dot_general | solution.py:29
  67.5 0.7 collective-permute-start.10
  68.2 4.5 %collective-permute-start.8 = (bf16[640,640]{1,0:T(8,128)(2,1)S(1)}, bf16[640,640]{1,0:T(8,128)(2,1)S(1)}, u32[]{:S(2)}, u32[]{:S(2)}) collective-permute-start(bf16[640,640]{1,0:T(8,128)(2,1)S(1)} %collective-permute-done), channel_id=1, source_target_pairs={{0,4},{4,8},{8,12},{1,5},{5,9},{9,13},{2,6},{6,10},{10,14},{3,7},{... | collective-permute-start | bytes 2457608 | tf_op jit(solution)/shard_map/ppermute | solution.py:17
  72.7 2.4 %collective-permute-start.11 = (bf16[640,640]{1,0:T(8,128)(2,1)}, bf16[640,640]{1,0:T(8,128)(2,1)S(1)}, u32[]{:S(2)}, u32[]{:S(2)}) collective-permute-start(bf16[640,640]{1,0:T(8,128)(2,1)} %collective-permute-done.1), channel_id=1, source_target_pairs={{0,16},{4,20},{8,24},{16,0},{20,4},{24,8},{1,17},{5,21},{9,25},{17... | collective-permute-start | bytes 2457608 | tf_op jit(solution)/shard_map/ppermute | solution.py:25
  75.2 1.3 collective-permute-start.9
  76.5 2.3 %fusion.26 = (f32[384]{0:T(512)S(1)}, f32[384]{0:T(512)S(1)}, f32[384]{0:T(512)S(1)}, f32[384]{0:T(512)S(1)}, f32[384]{0:T(512)S(1)}) fusion(f32[384,1152]{0,1:T(8,128)S(1)} %get-tuple-element.43, f32[384]{0:T(512)S(1)} %get-tuple-element.42, s32[384]{0:T(512)S(1)} %copy-done.12, s32[1152]{0:T(1024)S(1)} %eq.89, pred[1152]{0:T(1024)(128)(4,1)S(1)} %and.49, ...), kind=kLoop, calls=%fused_computation.47 | loop fusion | flops 7518336 | bytes 8870016 | tf_op jit(solution)/shard_map/reduce_sum | solution.py:35
  78.8 1.6 fusion.27
  80.3 1.6 fusion.28
  81.9 1.6 fusion.29
  83.4 1.6 fusion.30
  85.0 1.5 fusion.31
  86.5 5.3 %collective-permute-done.11 = bf16[640,640]{1,0:T(8,128)(2,1)S(1)} collective-permute-done((bf16[640,640]{1,0:T(8,128)(2,1)}, bf16[640,640]{1,0:T(8,128)(2,1)S(1)}, u32[]{:S(2)}, u32[]{:S(2)}) %collective-permute-start.11) | collective-permute-done | bytes 819232 | tf_op jit(solution)/shard_map/ppermute | solution.py:25
  91.9 0.9 copy-done.3
  92.8 1.2 collective-permute-done.9
  94.0 0.9 copy-done.5
  94.9 1.5 collective-permute-start.13
  96.7 13.2 %collective-permute-start.15 = (bf16[640,640]{1,0:T(8,128)(2,1)}, bf16[640,640]{1,0:T(8,128)(2,1)S(1)}, u32[]{:S(2)}, u32[]{:S(2)}) collective-permute-start(bf16[640,640]{1,0:T(8,128)(2,1)} %copy-done.3), channel_id=1, source_target_pairs={{0,4},{4,8},{8,12},{1,5},{5,9},{9,13},{2,6},{6,10},{10,14},{3,7},{... | collective-permute-start | bytes 2457608 | tf_op jit(solution)/shard_map/ppermute | solution.py:17
  109.9 0.7 collective-permute-start.17
  110.6 1.3 collective-permute-start.16
  111.9 7.3 %collective-permute-done.13 = bf16[384,640]{0,1:T(8,128)(2,1)} collective-permute-done((bf16[384,640]{0,1:T(8,128)(2,1)}, bf16[384,640]{0,1:T(8,128)(2,1)}, u32[]{:S(2)}, u32[]{:S(2)}) %collective-permute-start.13) | collective-permute-done | bytes 491552 | tf_op jit(solution)/shard_map/ppermute | solution.py:46
  119.3 3.6 %collective-permute-start.18 = (bf16[640,640]{1,0:T(8,128)(2,1)}, bf16[640,640]{1,0:T(8,128)(2,1)S(1)}, u32[]{:S(2)}, u32[]{:S(2)}) collective-permute-start(bf16[640,640]{1,0:T(8,128)(2,1)} %copy-done.5), channel_id=1, source_target_pairs={{0,16},{4,20},{16,0},{20,4},{1,17},{5,21},{17,1},{21,5},{2,18},{6,... | collective-permute-start | bytes 2457608 | tf_op jit(solution)/shard_map/ppermute | solution.py:25
  122.9 1.8 %select_select_fusion.3 = (bf16[384,640]{0,1:T(8,128)(2,1)S(1)}, bf16[384,640]{0,1:T(8,128)(2,1)S(1)}, bf16[384,640]{0,1:T(8,128)(2,1)S(1)}, bf16[384,640]{0,1:T(8,128)(2,1)S(1)}) fusion(bf16[384,640]{0,1:T(8,128)(2,1)} %collective-permute-done.12, bf16[384,640]{0,1:T(8,128)(2,1)} %collective-permute-done.13, bf16[384,640]{0,1:T(8,128)(2,1)} %collective-permute-done.14, ...), kind=kLoop, calls=%fused_computation.63 | loop fusion | flops 2949120 | bytes 3932172 | tf_op jit(solution)/shard_map/jit(_where)/select_n | solution.py:51
  124.9 0.9 copy-done.4
  127.6 1.8 %fusion.51 = f32[384,640]{1,0:T(8,128)S(1)} fusion(bf16[640,640]{1,0:T(8,128)(2,1)} %collective-permute-done.1, bf16[384,2560]{0,1:T(8,128)(2,1)S(1)} %pad_maximum_fusion, s32[]{:T(128)S(6)} %select_n.219), kind=kOutput, calls=%fused_computation.82 | convolution fusion | flops 314572800 | bytes 2293764 | tf_op jit(solution)/shard_map/dot_general | solution.py:168
  131.5 4.6 %collective-permute-done.16 = bf16[640,640]{1,0:T(8,128)(2,1)S(1)} collective-permute-done((bf16[640,640]{1,0:T(8,128)(2,1)}, bf16[640,640]{1,0:T(8,128)(2,1)S(1)}, u32[]{:S(2)}, u32[]{:S(2)}) %collective-permute-start.16) | collective-permute-done | bytes 819232 | tf_op jit(solution)/shard_map/ppermute | solution.py:17
  136.1 0.7 collective-permute-start.19
  137.4 3.4 %collective-permute-start.20 = (bf16[640,640]{1,0:T(8,128)(2,1)S(1)}, bf16[640,640]{1,0:T(8,128)(2,1)S(1)}, u32[]{:S(2)}, u32[]{:S(2)}) collective-permute-start(bf16[640,640]{1,0:T(8,128)(2,1)S(1)} %collective-permute-done.16), channel_id=1, source_target_pairs={{0,16},{16,0},{1,17},{17,1},{2,18},{18,2},{3,19},{19,3}} | collective-permute-start | bytes 2457608 | tf_op jit(solution)/shard_map/ppermute | solution.py:25
  142.7 0.9 fusion.20
  144.3 15.0 %collective-permute-done.20 = bf16[640,640]{1,0:T(8,128)(2,1)S(1)} collective-permute-done((bf16[640,640]{1,0:T(8,128)(2,1)S(1)}, bf16[640,640]{1,0:T(8,128)(2,1)S(1)}, u32[]{:S(2)}, u32[]{:S(2)}) %collective-permute-start.20) | collective-permute-done | bytes 819232 | tf_op jit(solution)/shard_map/ppermute | solution.py:25
  159.9 0.9 fusion.21
  160.8 1.2 maximum_select_fusion
  (64 shorter events, 11.5 us)
Async XLA Ops:
  0.0 8.6 %copy-start = (bf16[640,1280]{1,0:T(8,128)(2,1)S(1)}, bf16[640,1280]{1,0:T(8,128)(2,1)}, u32[]{:S(2)}) copy-start(bf16[640,1280]{1,0:T(8,128)(2,1)} %param.10) | copy-start | bytes 4915204
  0.0 46.8 %collective-permute-start.2 = (bf16[384,640]{1,0:T(8,128)(2,1)}, bf16[384,640]{1,0:T(8,128)(2,1)}, u32[]{:S(2)}, u32[]{:S(2)}) collective-permute-start(bf16[384,640]{1,0:T(8,128)(2,1)} %param.8), channel_id=1, source_target_pairs={{0,4},{4,8},{8,12},{1,5},{5,9},{9,13},{2,6},{6,10},{10,14},{3,7},{... | collective-permute-start | bytes 1474568 | tf_op jit(solution)/shard_map/ppermute | solution.py:17
  5.8 11.1 %collective-permute-start.6 = (s32[384]{0:T(512)}, s32[384]{0:T(512)S(1)}, u32[]{:S(2)}, u32[]{:S(2)}) collective-permute-start(s32[384]{0:T(512)} %param.12), channel_id=1, source_target_pairs={{0,4},{4,8},{8,12},{1,5},{5,9},{9,13},{2,6},{6,10},{10,14},{3,7},{... | collective-permute-start | bytes 4616 | tf_op jit(solution)/shard_map/ppermute | solution.py:17
  8.7 54.1 %collective-permute-start = (bf16[640,640]{1,0:T(8,128)(2,1)S(1)}, bf16[640,640]{1,0:T(8,128)(2,1)S(1)}, u32[]{:S(2)}, u32[]{:S(2)}) collective-permute-start(bf16[640,640]{1,0:T(8,128)(2,1)S(1)} %constant_dynamic-slice_fusion.1), channel_id=1, source_target_pairs={{0,4},{4,8},{8,12},{1,5},{5,9},{9,13},{2,6},{6,10},{10,14},{3,7},{... | collective-permute-start | bytes 2457608 | tf_op jit(solution)/shard_map/ppermute | solution.py:17
  12.2 50.6 %collective-permute-start.1 = (bf16[640,640]{1,0:T(8,128)(2,1)S(1)}, bf16[640,640]{1,0:T(8,128)(2,1)}, u32[]{:S(2)}, u32[]{:S(2)}) collective-permute-start(bf16[640,640]{1,0:T(8,128)(2,1)S(1)} %constant_dynamic-slice_fusion.1), channel_id=1, source_target_pairs={{4,0},{8,4},{12,8},{5,1},{9,5},{13,9},{6,2},{10,6},{14,10},{7,3},{... | collective-permute-start | bytes 2457608 | tf_op jit(solution)/shard_map/ppermute | solution.py:17
  13.5 37.0 %collective-permute-start.3 = (bf16[384,640]{1,0:T(8,128)(2,1)}, bf16[384,640]{1,0:T(8,128)(2,1)}, u32[]{:S(2)}, u32[]{:S(2)}) collective-permute-start(bf16[384,640]{1,0:T(8,128)(2,1)} %param.8), channel_id=1, source_target_pairs={{4,0},{8,4},{12,8},{5,1},{9,5},{13,9},{6,2},{10,6},{14,10},{7,3},{... | collective-permute-start | bytes 1474568 | tf_op jit(solution)/shard_map/ppermute | solution.py:17
  17.0 26.9 %collective-permute-start.7 = (s32[384]{0:T(512)}, s32[384]{0:T(512)S(1)}, u32[]{:S(2)}, u32[]{:S(2)}) collective-permute-start(s32[384]{0:T(512)} %param.12), channel_id=1, source_target_pairs={{4,0},{8,4},{12,8},{5,1},{9,5},{13,9},{6,2},{10,6},{14,10},{7,3},{... | collective-permute-start | bytes 4616 | tf_op jit(solution)/shard_map/ppermute | solution.py:17
  43.9 11.5 %collective-permute-start.4 = (bf16[384,640]{1,0:T(8,128)(2,1)}, bf16[384,640]{1,0:T(8,128)(2,1)}, u32[]{:S(2)}, u32[]{:S(2)}) collective-permute-start(bf16[384,640]{1,0:T(8,128)(2,1)} %param.9), channel_id=1, source_target_pairs={{0,4},{4,8},{8,12},{1,5},{5,9},{9,13},{2,6},{6,10},{10,14},{3,7},{... | collective-permute-start | bytes 1474568 | tf_op jit(solution)/shard_map/ppermute | solution.py:17
  46.8 13.4 %collective-permute-start.5 = (bf16[384,640]{1,0:T(8,128)(2,1)}, bf16[384,640]{1,0:T(8,128)(2,1)}, u32[]{:S(2)}, u32[]{:S(2)}) collective-permute-start(bf16[384,640]{1,0:T(8,128)(2,1)} %param.9), channel_id=1, source_target_pairs={{4,0},{8,4},{12,8},{5,1},{9,5},{13,9},{6,2},{10,6},{14,10},{7,3},{... | collective-permute-start | bytes 1474568 | tf_op jit(solution)/shard_map/ppermute | solution.py:17
  50.5 9.8 %copy-start.11 = (bf16[384,640]{1,0:T(8,128)(2,1)S(1)}, bf16[384,640]{1,0:T(8,128)(2,1)}, u32[]{:S(2)}) copy-start(bf16[384,640]{1,0:T(8,128)(2,1)} %param.9) | copy-start | bytes 1474564
  53.2 9.6 %copy-start.12 = (s32[384]{0:T(512)S(1)}, s32[384]{0:T(512)}, u32[]{:S(2)}) copy-start(s32[384]{0:T(512)} %param.12) | copy-start | bytes 4612
  62.8 2.2 %copy-start.2 = (bf16[3,384,640]{2,1,0:T(8,128)(2,1)S(1)}, bf16[3,384,640]{2,1,0:T(8,128)(2,1)}, u32[]{:S(2)}) copy-start(bf16[3,384,640]{2,1,0:T(8,128)(2,1)} %pad_maximum_fusion.1) | copy-start | bytes 4423684
  62.8 2.2 %copy-start.13 = (bf16[384,640]{1,0:T(8,128)(2,1)S(1)}, bf16[384,640]{1,0:T(8,128)(2,1)}, u32[]{:S(2)}) copy-start(bf16[384,640]{1,0:T(8,128)(2,1)} %param.7) | copy-start | bytes 1474564
  67.5 19.0 %collective-permute-start.10 = (bf16[640,640]{1,0:T(8,128)(2,1)S(1)}, bf16[640,640]{1,0:T(8,128)(2,1)S(1)}, u32[]{:S(2)}, u32[]{:S(2)}) collective-permute-start(bf16[640,640]{1,0:T(8,128)(2,1)S(1)} %collective-permute-done), channel_id=1, source_target_pairs={{4,20},{8,24},{12,28},{20,4},{24,8},{28,12},{5,21},{9,25},{13,29},... | collective-permute-start | bytes 2457608 | tf_op jit(solution)/shard_map/ppermute | solution.py:25
  68.2 23.7 %collective-permute-start.8 = (bf16[640,640]{1,0:T(8,128)(2,1)S(1)}, bf16[640,640]{1,0:T(8,128)(2,1)S(1)}, u32[]{:S(2)}, u32[]{:S(2)}) collective-permute-start(bf16[640,640]{1,0:T(8,128)(2,1)S(1)} %collective-permute-done), channel_id=1, source_target_pairs={{0,4},{4,8},{8,12},{1,5},{5,9},{9,13},{2,6},{6,10},{10,14},{3,7},{... | collective-permute-start | bytes 2457608 | tf_op jit(solution)/shard_map/ppermute | solution.py:17
  72.7 19.2 %collective-permute-start.11 = (bf16[640,640]{1,0:T(8,128)(2,1)}, bf16[640,640]{1,0:T(8,128)(2,1)S(1)}, u32[]{:S(2)}, u32[]{:S(2)}) collective-permute-start(bf16[640,640]{1,0:T(8,128)(2,1)} %collective-permute-done.1), channel_id=1, source_target_pairs={{0,16},{4,20},{8,24},{16,0},{20,4},{24,8},{1,17},{5,21},{9,25},{17... | collective-permute-start | bytes 2457608 | tf_op jit(solution)/shard_map/ppermute | solution.py:25
  75.2 18.9 %collective-permute-start.9 = (bf16[640,640]{1,0:T(8,128)(2,1)}, bf16[640,640]{1,0:T(8,128)(2,1)S(1)}, u32[]{:S(2)}, u32[]{:S(2)}) collective-permute-start(bf16[640,640]{1,0:T(8,128)(2,1)} %collective-permute-done.1), channel_id=1, source_target_pairs={{4,0},{8,4},{12,8},{5,1},{9,5},{13,9},{6,2},{10,6},{14,10},{7,3},{... | collective-permute-start | bytes 2457608 | tf_op jit(solution)/shard_map/ppermute | solution.py:17
  76.5 2.3 %copy-start.1 = (bf16[3,384,640]{2,1,0:T(8,128)(2,1)S(1)}, bf16[3,384,640]{2,1,0:T(8,128)(2,1)}, u32[]{:S(2)}) copy-start(bf16[3,384,640]{2,1,0:T(8,128)(2,1)} %pad_maximum_fusion.2) | copy-start | bytes 4423684
  86.5 8.4 %copy-start.7 = (bf16[640,640]{1,0:T(8,128)(2,1)}, bf16[640,640]{1,0:T(8,128)(2,1)S(1)}, u32[]{:S(2)}) copy-start(bf16[640,640]{1,0:T(8,128)(2,1)S(1)} %collective-permute-done.10) | copy-start | bytes 2457604
  91.9 4.5 %copy-start.9 = (bf16[640,640]{1,0:T(8,128)(2,1)}, bf16[640,640]{1,0:T(8,128)(2,1)S(1)}, u32[]{:S(2)}) copy-start(bf16[640,640]{1,0:T(8,128)(2,1)S(1)} %collective-permute-done.11) | copy-start | bytes 2457604
  91.9 0.9 copy-start.3
  94.0 0.9 copy-start.5
  94.9 15.7 %collective-permute-start.12 = (bf16[384,640]{0,1:T(8,128)(2,1)}, bf16[384,640]{0,1:T(8,128)(2,1)}, u32[]{:S(2)}, u32[]{:S(2)}) collective-permute-start(bf16[384,640]{0,1:T(8,128)(2,1)} %fusion.31), channel_id=1, source_target_pairs={{0,3},{1,0},{2,1},{3,2},{4,7},{5,4},{6,5},{7,6},{8,11},{9,8},{10,9... | collective-permute-start | bytes 1474568 | tf_op jit(solution)/shard_map/ppermute | solution.py:46
  94.9 24.3 %collective-permute-start.13 = (bf16[384,640]{0,1:T(8,128)(2,1)}, bf16[384,640]{0,1:T(8,128)(2,1)}, u32[]{:S(2)}, u32[]{:S(2)}) collective-permute-start(bf16[384,640]{0,1:T(8,128)(2,1)} %fusion.31), channel_id=1, source_target_pairs={{0,2},{1,3},{2,0},{3,1},{4,6},{5,7},{6,4},{7,5},{8,10},{9,11},{10,... | collective-permute-start | bytes 1474568 | tf_op jit(solution)/shard_map/ppermute | solution.py:46
  96.4 26.4 %collective-permute-start.14 = (bf16[384,640]{0,1:T(8,128)(2,1)}, bf16[384,640]{0,1:T(8,128)(2,1)}, u32[]{:S(2)}, u32[]{:S(2)}) collective-permute-start(bf16[384,640]{0,1:T(8,128)(2,1)} %fusion.31), channel_id=1, source_target_pairs={{0,1},{1,2},{2,3},{3,0},{4,5},{5,6},{6,7},{7,4},{8,9},{9,10},{10,1... | collective-permute-start | bytes 1474568 | tf_op jit(solution)/shard_map/ppermute | solution.py:46
  96.7 34.8 %collective-permute-start.15 = (bf16[640,640]{1,0:T(8,128)(2,1)}, bf16[640,640]{1,0:T(8,128)(2,1)S(1)}, u32[]{:S(2)}, u32[]{:S(2)}) collective-permute-start(bf16[640,640]{1,0:T(8,128)(2,1)} %copy-done.3), channel_id=1, source_target_pairs={{0,4},{4,8},{8,12},{1,5},{5,9},{9,13},{2,6},{6,10},{10,14},{3,7},{... | collective-permute-start | bytes 2457608 | tf_op jit(solution)/shard_map/ppermute | solution.py:17
  109.9 26.1 %collective-permute-start.17 = (bf16[640,640]{1,0:T(8,128)(2,1)}, bf16[640,640]{1,0:T(8,128)(2,1)S(1)}, u32[]{:S(2)}, u32[]{:S(2)}) collective-permute-start(bf16[640,640]{1,0:T(8,128)(2,1)} %copy-done.3), channel_id=1, source_target_pairs={{8,24},{12,28},{24,8},{28,12},{9,25},{13,29},{25,9},{29,13},{10,26... | collective-permute-start | bytes 2457608 | tf_op jit(solution)/shard_map/ppermute | solution.py:25
  110.6 25.4 %collective-permute-start.16 = (bf16[640,640]{1,0:T(8,128)(2,1)}, bf16[640,640]{1,0:T(8,128)(2,1)S(1)}, u32[]{:S(2)}, u32[]{:S(2)}) collective-permute-start(bf16[640,640]{1,0:T(8,128)(2,1)} %copy-done.5), channel_id=1, source_target_pairs={{4,0},{8,4},{12,8},{5,1},{9,5},{13,9},{6,2},{10,6},{14,10},{7,3},{... | collective-permute-start | bytes 2457608 | tf_op jit(solution)/shard_map/ppermute | solution.py:17
  119.3 16.8 %collective-permute-start.18 = (bf16[640,640]{1,0:T(8,128)(2,1)}, bf16[640,640]{1,0:T(8,128)(2,1)S(1)}, u32[]{:S(2)}, u32[]{:S(2)}) collective-permute-start(bf16[640,640]{1,0:T(8,128)(2,1)} %copy-done.5), channel_id=1, source_target_pairs={{0,16},{4,20},{16,0},{20,4},{1,17},{5,21},{17,1},{21,5},{2,18},{6,... | collective-permute-start | bytes 2457608 | tf_op jit(solution)/shard_map/ppermute | solution.py:25
  124.7 1.1 copy-start.4
  125.9 1.1 copy-start.6
  127.6 2.5 %copy-start.8 = (bf16[640,640]{1,0:T(8,128)(2,1)S(1)}, bf16[640,640]{1,0:T(8,128)(2,1)}, u32[]{:S(2)}) copy-start(bf16[640,640]{1,0:T(8,128)(2,1)} %copy-done.7) | copy-start | bytes 2457604
  129.5 1.3 copy-start.10
  136.1 7.6 %collective-permute-start.19 = (bf16[640,640]{1,0:T(8,128)(2,1)S(1)}, bf16[640,640]{1,0:T(8,128)(2,1)S(1)}, u32[]{:S(2)}, u32[]{:S(2)}) collective-permute-start(bf16[640,640]{1,0:T(8,128)(2,1)S(1)} %collective-permute-done.15), channel_id=1, source_target_pairs={{12,28},{28,12},{13,29},{29,13},{14,30},{30,14},{15,31},{31,15}} | collective-permute-start | bytes 2457608 | tf_op jit(solution)/shard_map/ppermute | solution.py:25
  137.4 21.9 %collective-permute-start.20 = (bf16[640,640]{1,0:T(8,128)(2,1)S(1)}, bf16[640,640]{1,0:T(8,128)(2,1)S(1)}, u32[]{:S(2)}, u32[]{:S(2)}) collective-permute-start(bf16[640,640]{1,0:T(8,128)(2,1)S(1)} %collective-permute-done.16), channel_id=1, source_target_pairs={{0,16},{16,0},{1,17},{17,1},{2,18},{18,2},{3,19},{19,3}} | collective-permute-start | bytes 2457608 | tf_op jit(solution)/shard_map/ppermute | solution.py:25

commit v11 on v7

--- a/solution.py
+++ b/solution.py
@@ -58,9 +58,10 @@
                 every_offset.add(layer_step * layer_tiles + row_step * TGW + col_step)
     distances = [offset for offset in sorted(every_offset) if 0 < offset < seq_count]
 
-    half_width = out_weight.shape[1] // lax.axis_size("rep")
-    own_half = lax.dynamic_slice_in_dim(out_weight, rep_position * half_width, half_width, axis=1)
-    both_halves = lax.all_gather(own_half, ("rep", "seq"), axis=0, tiled=True)
+    rep_count = lax.axis_size("rep")
+    part_rows = out_weight.shape[0] // rep_count
+    own_part = lax.dynamic_slice_in_dim(out_weight, rep_position * part_rows, part_rows, axis=0)
+    both_parts = lax.all_gather(own_part, ("rep", "seq"), axis=0, tiled=True)
 
     key_list = [keys]
     value_list = [values]
@@ -105,14 +106,10 @@
     attended = jnp.concatenate(head_outputs, axis=1)
 
     features = exchange_heads(attended)
-    rows = features.shape[1]
-    pieces = []
-    for rep_index in range(lax.axis_size("rep")):
-        weight_half = lax.slice_in_dim(both_halves, rep_index * rows, (rep_index + 1) * rows, axis=0)
-        pieces.append(
-            jnp.dot(features, weight_half, preferred_element_type=jnp.float32).astype(jnp.bfloat16)
-        )
-    return jnp.concatenate(pieces, axis=1)
+    regrouped = features.reshape(tile_rows, seq_count, rep_count, part_rows)
+    regrouped = jnp.swapaxes(regrouped, 1, 2).reshape(tile_rows, features.shape[1])
+    projected = jnp.dot(regrouped, both_parts, preferred_element_type=jnp.float32)
+    return projected.astype(jnp.bfloat16)
 
 
 def solution(mesh):

time: 146 us -> 145 us (level)
  other arithmetic: 8.64 us -> 6.69 us
    reshape x0 -> x1, local copies, waits for them, and re-layouts: none -> 1.52 us  [on_device(): regrouped = features.reshape(tile_rows, seq_count, rep_count, part_rows)]
    dot_general x2 -> x1, matrix products: 6.15 us -> 7.15 us  [on_device(): jnp.dot(regrouped, both_parts, preferred_element_type=jnp.float32)]
where the time goes in v11:
time: 145 us
  waiting for transfers between devices  81.5 us (56%)
  starting transfers between devices  20.4 us (14%)
  matrix products  18.1 us (12%)
  between operations  13.6 us (9%)
  other arithmetic  6.69 us (5%)
  local copies, waits for them, and re-layouts  4.28 us (3%)
    ppermute x6, waiting for transfers between devices, from_behind(): return lax.ppermute(value, axis, pairs)  38.2 us
    ppermute x3, waiting for transfers between devices, exchange_heads(): received.append(lax.ppermute(attended, 'head', pairs))  22.6 us
    all_gather x1, waiting for transfers between devices, on_device(): both_parts = lax.all_gather(own_part, ('rep', 'seq'), axis=0, tiled=True)  20.7 us
    ppermute x6, starting transfers between devices, from_behind(): return lax.ppermute(value, axis, pairs)  18.7 us
    dot_general x5, matrix products, attend_head(): jnp.dot(weights, value_head, preferred_element_type=jnp.float32)  7.77 us
    dot_general x1, matrix products, on_device(): jnp.dot(regrouped, both_parts, preferred_element_type=jnp.float32)  7.15 us
    dot_general x5, matrix products, attend_head(): lax.dot_general(query_head, key_head, (((1,), (1,)), ((), ())), preferred...  3.18 us
  transfers between devices with their start and end apart: 10, of which 6 were waited for; matrix products, arithmetic and copies ran while one was open for 13% of the time, Pallas kernels for 0%

profile of v11, /device:TPU:0, one launch (start us, length us, event | category | flops | bytes accessed | tf_op | source)
XLA Modules:
  0.0 144.6 jit_solution(4421870948088875219)
XLA Ops:
  6.5 0.0 copy-start
  6.5 0.0 copy-start.5
  6.6 0.0 all-gather.2.cloned.1.call-start
  6.6 1.7 %copy-done = bf16[640,1280]{1,0:T(8,128)(2,1)S(1)} copy-done((bf16[640,1280]{1,0:T(8,128)(2,1)S(1)}, bf16[640,1280]{1,0:T(8,128)(2,1)}, u32[]{:S(2)}) %copy-start) | copy-done | bytes 1638424
  8.3 0.9 constant_dynamic-slice_fusion
  9.2 0.0 all-gather.2.cloned.1.call-update
  9.2 0.0 copy-done.1
  9.3 5.7 %collective-permute-start.2 = (bf16[384,640]{1,0:T(8,128)(2,1)S(1)}, bf16[384,640]{1,0:T(8,128)(2,1)}, u32[]{:S(2)}, u32[]{:S(2)}) collective-permute-start(bf16[384,640]{1,0:T(8,128)(2,1)S(1)} %copy-done.1), channel_id=1, source_target_pairs={{0,4},{4,8},{8,12},{1,5},{5,9},{9,13},{2,6},{6,10},{10,14},{3,7},{... | collective-permute-start | bytes 1474568 | tf_op jit(solution)/shard_map/ppermute | solution.py:16
  15.0 1.3 collective-permute-start.3
  16.3 4.6 %collective-permute-start.4 = (bf16[384,640]{1,0:T(8,128)(2,1)S(1)}, bf16[384,640]{1,0:T(8,128)(2,1)S(1)}, u32[]{:S(2)}, u32[]{:S(2)}) collective-permute-start(bf16[384,640]{1,0:T(8,128)(2,1)S(1)} %copy-done.2), channel_id=1, source_target_pairs={{0,4},{4,8},{8,12},{1,5},{5,9},{9,13},{2,6},{6,10},{10,14},{3,7},{... | collective-permute-start | bytes 1474568 | tf_op jit(solution)/shard_map/ppermute | solution.py:16
  20.9 1.3 collective-permute-start.5
  22.2 0.0 copy-done.3
  22.2 4.5 %collective-permute-start = (s32[384]{0:T(512)S(1)}, s32[384]{0:T(512)S(1)}, u32[]{:S(2)}, u32[]{:S(2)}) collective-permute-start(s32[384]{0:T(512)S(1)} %copy-done.3), channel_id=1, source_target_pairs={{0,4},{4,8},{8,12},{1,5},{5,9},{9,13},{2,6},{6,10},{10,14},{3,7},{... | collective-permute-start | bytes 4616 | tf_op jit(solution)/shard_map/ppermute | solution.py:16
  26.7 0.0 copy-done.6
  26.8 23.3 %collective-permute-done = s32[384]{0:T(512)S(1)} collective-permute-done((s32[384]{0:T(512)S(1)}, s32[384]{0:T(512)S(1)}, u32[]{:S(2)}, u32[]{:S(2)}) %collective-permute-start) | collective-permute-done | bytes 1568 | tf_op jit(solution)/shard_map/ppermute | solution.py:16
  50.1 1.3 collective-permute-start.1
  51.4 0.2 and_reduce_fusion
  51.6 0.1 broadcast_in_dim.32
  51.7 14.9 %collective-permute-done.1 = s32[384]{0:T(512)S(1)} collective-permute-done((s32[384]{0:T(512)S(1)}, s32[384]{0:T(512)S(1)}, u32[]{:S(2)}, u32[]{:S(2)}) %collective-permute-start.1) | collective-permute-done | bytes 1568 | tf_op jit(solution)/shard_map/ppermute | solution.py:16
  66.6 0.0 collective-permute-done.2
  66.6 0.0 collective-permute-done.3
  66.6 1.4 pad_maximum_fusion.1
  68.0 0.0 copy-start.4
  68.0 0.0 collective-permute-done.4
  68.0 0.0 collective-permute-done.5
  68.0 1.3 pad_maximum_fusion.2
  69.3 0.6 fusion.41
  70.0 0.6 fusion.42
  70.6 0.6 fusion.43
  71.2 0.6 fusion.44
  71.9 0.6 fusion.45
  72.5 2.3 %fusion.14 = (f32[384]{0:T(512)S(1)}, f32[384]{0:T(512)S(1)}, f32[384]{0:T(512)S(1)}, f32[384]{0:T(512)S(1)}, f32[384]{0:T(512)S(1)}) fusion(f32[384,1152]{0,1:T(8,128)S(1)} %get-tuple-element.15, f32[384]{0:T(512)S(1)} %get-tuple-element.14, s32[384]{0:T(512)S(1)} %copy-done.3, s32[1152]{0:T(1024)S(1)} %eq.85, pred[1152]{0:T(1024)(128)(4,1)S(1)} %and.49, ...), kind=kLoop, calls=%fused_computation.34 | loop fusion | flops 7518336 | bytes 8870016 | tf_op jit(solution)/shard_map/reduce_sum | solution.py:26
  74.8 1.6 %fusion.15 = bf16[384,640]{0,1:T(8,128)(2,1)} fusion(f32[384,1152]{0,1:T(8,128)S(1)} %get-tuple-element.23, f32[384]{0:T(512)S(1)} %get-tuple-element.9, f32[384]{0:T(512)S(1)} %get-tuple-element.22, s32[384]{0:T(512)S(1)} %copy-done.3, s32[1152]{0:T(1024)S(1)} %eq.85, pred[1152]{0:T(1024)(128)(4,1)S(1)} %and.49, bf16[1152,640]{1,0:T(8,128)(2,1)S(1)} %bitcast.40), kind=kOutput, calls=%fused_computation.40 | convolution fusion | flops 115949568 | bytes 2179072 | tf_op jit(solution)/shard_map/dot_general | solution.py:28
  76.3 1.6 %fusion.16 = bf16[384,640]{0,1:T(8,128)(2,1)} fusion(bf16[384,640]{0,1:T(8,128)(2,1)} %fusion.15, f32[384,1152]{0,1:T(8,128)S(1)} %get-tuple-element.21, f32[384]{0:T(512)S(1)} %get-tuple-element.8, f32[384]{0:T(512)S(1)} %get-tuple-element.20, s32[384]{0:T(512)S(1)} %copy-done.3, s32[1152]{0:T(1024)S(1)} %eq.85, pred[1152]{0:T(1024)(128)(4,1)S(1)} %and.49, ...), kind=kOutput, calls=%fused_computation.41 | convolution fusion | flops 115949568 | bytes 2179072 | tf_op jit(solution)/shard_map/dot_general | solution.py:28
  77.9 1.6 %fusion.17 = bf16[384,640]{0,1:T(8,128)(2,1)} fusion(bf16[384,640]{0,1:T(8,128)(2,1)} %fusion.16, f32[384,1152]{0,1:T(8,128)S(1)} %get-tuple-element.19, f32[384]{0:T(512)S(1)} %get-tuple-element.7, f32[384]{0:T(512)S(1)} %get-tuple-element.18, s32[384]{0:T(512)S(1)} %copy-done.3, s32[1152]{0:T(1024)S(1)} %eq.85, pred[1152]{0:T(1024)(128)(4,1)S(1)} %and.49, ...), kind=kOutput, calls=%fused_computation.42 | convolution fusion | flops 115949568 | bytes 2179072 | tf_op jit(solution)/shard_map/dot_general | solution.py:28
  79.5 1.5 %fusion.18 = bf16[384,640]{0,1:T(8,128)(2,1)} fusion(bf16[384,640]{0,1:T(8,128)(2,1)} %fusion.17, f32[384,1152]{0,1:T(8,128)S(1)} %get-tuple-element.17, f32[384]{0:T(512)S(1)} %get-tuple-element.6, f32[384]{0:T(512)S(1)} %get-tuple-element.16, s32[384]{0:T(512)S(1)} %copy-done.3, s32[1152]{0:T(1024)S(1)} %eq.85, pred[1152]{0:T(1024)(128)(4,1)S(1)} %and.49, ...), kind=kOutput, calls=%fused_computation.43 | convolution fusion | flops 115949568 | bytes 2179072 | tf_op jit(solution)/shard_map/dot_general | solution.py:28
  81.0 1.6 %fusion.19 = bf16[384,640]{0,1:T(8,128)(2,1)} fusion(bf16[384,640]{0,1:T(8,128)(2,1)} %fusion.18, f32[384,1152]{0,1:T(8,128)S(1)} %get-tuple-element.15, f32[384]{0:T(512)S(1)} %get-tuple-element.5, f32[384]{0:T(512)S(1)} %get-tuple-element.14, s32[384]{0:T(512)S(1)} %copy-done.3, s32[1152]{0:T(1024)S(1)} %eq.85, pred[1152]{0:T(1024)(128)(4,1)S(1)} %and.49, ...), kind=kOutput, calls=%fused_computation.44 | convolution fusion | flops 115949568 | bytes 2179072 | tf_op jit(solution)/shard_map/dot_general | solution.py:28
  82.6 0.0 collective-permute-start.6
  82.6 1.5 %collective-permute-start.7 = (bf16[384,640]{0,1:T(8,128)(2,1)}, bf16[384,640]{0,1:T(8,128)(2,1)S(1)}, u32[]{:S(2)}, u32[]{:S(2)}) collective-permute-start(bf16[384,640]{0,1:T(8,128)(2,1)} %fusion.19), channel_id=1, source_target_pairs={{0,2},{1,3},{2,0},{3,1},{4,6},{5,7},{6,4},{7,5},{8,10},{9,11},{10,... | collective-permute-start | bytes 1474568 | tf_op jit(solution)/shard_map/ppermute | solution.py:37
  84.0 0.2 collective-permute-start.8
  84.3 9.2 %collective-permute-done.6 = bf16[384,640]{0,1:T(8,128)(2,1)S(1)} collective-permute-done((bf16[384,640]{0,1:T(8,128)(2,1)}, bf16[384,640]{0,1:T(8,128)(2,1)S(1)}, u32[]{:S(2)}, u32[]{:S(2)}) %collective-permute-start.6) | collective-permute-done | bytes 491552 | tf_op jit(solution)/shard_map/ppermute | solution.py:37
  93.5 13.3 %collective-permute-done.7 = bf16[384,640]{0,1:T(8,128)(2,1)S(1)} collective-permute-done((bf16[384,640]{0,1:T(8,128)(2,1)}, bf16[384,640]{0,1:T(8,128)(2,1)S(1)}, u32[]{:S(2)}, u32[]{:S(2)}) %collective-permute-start.7) | collective-permute-done | bytes 491552 | tf_op jit(solution)/shard_map/ppermute | solution.py:37
  106.8 0.1 collective-permute-done.8
  106.9 1.4 select_select_fusion.3
  108.2 0.2 pad_maximum_fusion
  108.4 1.5 %copy.9 = bf16[384,4,2,320]{0,3,1,2:T(8,128)(2,1)} copy(bf16[384,4,2,320]{0,3,2,1:T(8,128)(2,1)S(1)} %bitcast.38) | data formatting | bytes 3932160 | tf_op jit(solution)/shard_map/reshape | solution.py:109
  110.0 20.7 %all-gather.2.cloned.1.call-done = bf16[2560,1280]{1,0:T(8,128)(2,1)} async-done(((bf16[320,1280]{1,0:T(8,128)(2,1)}), bf16[2560,1280]{1,0:T(8,128)(2,1)}) %all-gather.2.cloned.1.call-update) | async-done | bytes 6553616 | tf_op jit(solution)/shard_map/all_gather | solution.py:64
  130.6 7.2 %convolution_convert_fusion = bf16[384,1280]{1,0:T(8,128)(2,1)} fusion(bf16[384,2560]{0,1:T(8,128)(2,1)} %bitcast.39, bf16[2560,1280]{1,0:T(8,128)(2,1)} %all-gather.2.cloned.1.call-done), kind=kOutput, calls=%fused_computation.15 | convolution fusion | flops 2517073920 | bytes 9502720 | tf_op jit(solution)/shard_map/dot_general | solution.py:111
  (16 shorter events, 0.1 us)
Async XLA Ops:
  6.5 1.7 %copy-start = (bf16[640,1280]{1,0:T(8,128)(2,1)S(1)}, bf16[640,1280]{1,0:T(8,128)(2,1)}, u32[]{:S(2)}) copy-start(bf16[640,1280]{1,0:T(8,128)(2,1)} %param.10) | copy-start | bytes 4915204
  6.5 20.2 %copy-start.6 = (s32[3]{0:T(128)S(1)}, s32[3]{0:T(128)}, u32[]{:S(2)}) copy-start(s32[3]{0:T(128)} %constant.86) | copy-start | bytes 40
  6.5 2.7 %copy-start.1 = (bf16[384,640]{1,0:T(8,128)(2,1)S(1)}, bf16[384,640]{1,0:T(8,128)(2,1)}, u32[]{:S(2)}) copy-start(bf16[384,640]{1,0:T(8,128)(2,1)} %param.8) | copy-start | bytes 1474564
  6.5 9.7 %copy-start.2 = (bf16[384,640]{1,0:T(8,128)(2,1)S(1)}, bf16[384,640]{1,0:T(8,128)(2,1)}, u32[]{:S(2)}) copy-start(bf16[384,640]{1,0:T(8,128)(2,1)} %param.9) | copy-start | bytes 1474564
  6.5 15.6 %copy-start.3 = (s32[384]{0:T(512)S(1)}, s32[384]{0:T(512)}, u32[]{:S(2)}) copy-start(s32[384]{0:T(512)} %param.12) | copy-start | bytes 4612
  6.5 20.2 %copy-start.5 = (s32[4,27]{1,0:T(4,128)S(1)}, s32[4,27]{1,0:T(4,128)}, u32[]{:S(2)}) copy-start(s32[4,27]{1,0:T(4,128)} %param.11) | copy-start | bytes 1300
  6.6 124.1 %all-gather.2.cloned.1.call-start = ((), (), s32[]{:S(2)}) async-start(), calls=%async_computation | async-start | bytes 7372800 | tf_op jit(solution)/shard_map/all_gather | solution.py:64
  9.3 57.4 %collective-permute-start.2 = (bf16[384,640]{1,0:T(8,128)(2,1)S(1)}, bf16[384,640]{1,0:T(8,128)(2,1)}, u32[]{:S(2)}, u32[]{:S(2)}) collective-permute-start(bf16[384,640]{1,0:T(8,128)(2,1)S(1)} %copy-done.1), channel_id=1, source_target_pairs={{0,4},{4,8},{8,12},{1,5},{5,9},{9,13},{2,6},{6,10},{10,14},{3,7},{... | collective-permute-start | bytes 1474568 | tf_op jit(solution)/shard_map/ppermute | solution.py:16
  15.0 51.7 %collective-permute-start.3 = (bf16[384,640]{1,0:T(8,128)(2,1)S(1)}, bf16[384,640]{1,0:T(8,128)(2,1)}, u32[]{:S(2)}, u32[]{:S(2)}) collective-permute-start(bf16[384,640]{1,0:T(8,128)(2,1)S(1)} %copy-done.1), channel_id=1, source_target_pairs={{4,0},{8,4},{12,8},{5,1},{9,5},{13,9},{6,2},{10,6},{14,10},{7,3},{... | collective-permute-start | bytes 1474568 | tf_op jit(solution)/shard_map/ppermute | solution.py:16
  16.3 51.8 %collective-permute-start.4 = (bf16[384,640]{1,0:T(8,128)(2,1)S(1)}, bf16[384,640]{1,0:T(8,128)(2,1)S(1)}, u32[]{:S(2)}, u32[]{:S(2)}) collective-permute-start(bf16[384,640]{1,0:T(8,128)(2,1)S(1)} %copy-done.2), channel_id=1, source_target_pairs={{0,4},{4,8},{8,12},{1,5},{5,9},{9,13},{2,6},{6,10},{10,14},{3,7},{... | collective-permute-start | bytes 1474568 | tf_op jit(solution)/shard_map/ppermute | solution.py:16
  20.9 47.2 %collective-permute-start.5 = (bf16[384,640]{1,0:T(8,128)(2,1)S(1)}, bf16[384,640]{1,0:T(8,128)(2,1)}, u32[]{:S(2)}, u32[]{:S(2)}) collective-permute-start(bf16[384,640]{1,0:T(8,128)(2,1)S(1)} %copy-done.2), channel_id=1, source_target_pairs={{4,0},{8,4},{12,8},{5,1},{9,5},{13,9},{6,2},{10,6},{14,10},{7,3},{... | collective-permute-start | bytes 1474568 | tf_op jit(solution)/shard_map/ppermute | solution.py:16
  22.2 27.9 %collective-permute-start = (s32[384]{0:T(512)S(1)}, s32[384]{0:T(512)S(1)}, u32[]{:S(2)}, u32[]{:S(2)}) collective-permute-start(s32[384]{0:T(512)S(1)} %copy-done.3), channel_id=1, source_target_pairs={{0,4},{4,8},{8,12},{1,5},{5,9},{9,13},{2,6},{6,10},{10,14},{3,7},{... | collective-permute-start | bytes 4616 | tf_op jit(solution)/shard_map/ppermute | solution.py:16
  50.1 16.5 %collective-permute-start.1 = (s32[384]{0:T(512)S(1)}, s32[384]{0:T(512)S(1)}, u32[]{:S(2)}, u32[]{:S(2)}) collective-permute-start(s32[384]{0:T(512)S(1)} %copy-done.3), channel_id=1, source_target_pairs={{4,0},{8,4},{12,8},{5,1},{9,5},{13,9},{6,2},{10,6},{14,10},{7,3},{... | collective-permute-start | bytes 4616 | tf_op jit(solution)/shard_map/ppermute | solution.py:16
  68.0 1.3 copy-start.4
  82.6 10.9 %collective-permute-start.6 = (bf16[384,640]{0,1:T(8,128)(2,1)}, bf16[384,640]{0,1:T(8,128)(2,1)S(1)}, u32[]{:S(2)}, u32[]{:S(2)}) collective-permute-start(bf16[384,640]{0,1:T(8,128)(2,1)} %fusion.19), channel_id=1, source_target_pairs={{0,3},{1,0},{2,1},{3,2},{4,7},{5,4},{6,5},{7,6},{8,11},{9,8},{10,9... | collective-permute-start | bytes 1474568 | tf_op jit(solution)/shard_map/ppermute | solution.py:37
  82.6 24.2 %collective-permute-start.7 = (bf16[384,640]{0,1:T(8,128)(2,1)}, bf16[384,640]{0,1:T(8,128)(2,1)S(1)}, u32[]{:S(2)}, u32[]{:S(2)}) collective-permute-start(bf16[384,640]{0,1:T(8,128)(2,1)} %fusion.19), channel_id=1, source_target_pairs={{0,2},{1,3},{2,0},{3,1},{4,6},{5,7},{6,4},{7,5},{8,10},{9,11},{10,... | collective-permute-start | bytes 1474568 | tf_op jit(solution)/shard_map/ppermute | solution.py:37
  84.0 22.8 %collective-permute-start.8 = (bf16[384,640]{0,1:T(8,128)(2,1)}, bf16[384,640]{0,1:T(8,128)(2,1)S(1)}, u32[]{:S(2)}, u32[]{:S(2)}) collective-permute-start(bf16[384,640]{0,1:T(8,128)(2,1)} %fusion.19), channel_id=1, source_target_pairs={{0,1},{1,2},{2,3},{3,0},{4,5},{5,6},{6,7},{7,4},{8,9},{9,10},{10,1... | collective-permute-start | bytes 1474568 | tf_op jit(solution)/shard_map/ppermute | solution.py:37
Sparse Core Ops, SparseCore 0:
  9.5 121.0 all-gather.1

commit v12 on v11

--- a/solution.py
+++ b/solution.py
@@ -67,17 +67,14 @@
     value_list = [values]
     clip_list = [clip_ids]
     offsets = [0]
+    joined = jnp.concatenate([keys, values], axis=1)
     for distance in distances:
-        below_keys, below_values, below_clips = from_behind(
-            (keys, values, clip_ids), "seq", distance
-        )
-        above_keys, above_values, above_clips = from_behind(
-            (keys, values, clip_ids), "seq", -distance
-        )
-        key_list += [below_keys, above_keys]
-        value_list += [below_values, above_values]
-        clip_list += [below_clips, above_clips]
-        offsets += [distance, -distance]
+        for signed in (distance, -distance):
+            moved = from_behind(joined, "seq", signed)
+            key_list.append(moved[:, :feature_width])
+            value_list.append(moved[:, feature_width:])
+            clip_list.append(from_behind(clip_ids, "seq", signed))
+            offsets.append(signed)
     key_stack = jnp.stack(key_list)
     value_stack = jnp.stack(value_list)
     clip_stack = jnp.stack(clip_list)

time: 145 us -> 147 us (1.014)
  starting transfers between devices: 20.4 us -> 14.8 us
  waiting for transfers between devices: 81.5 us -> 86.5 us
  local copies, waits for them, and re-layouts: 4.28 us -> 8.87 us
  other arithmetic: 6.69 us -> 4.45 us
    ppermute x6 -> x4, waiting for transfers between devices: 38.2 us -> 44.3 us  [from_behind(): return lax.ppermute(value, axis, pairs)]
    ppermute x6 -> x4, starting transfers between devices: 18.7 us -> 13 us  [from_behind(): return lax.ppermute(value, axis, pairs)]
    another operation x0 -> x2, local copies, waits for them, and re-layouts: none -> 2.53 us  [on_device(): value_stack = jnp.stack(value_list)]
  transfers between devices with their start and end apart: 10 -> 8, of which waited for: 6 -> 6; matrix products, arithmetic and copies ran while one was open for 13% -> 15% of each run, Pallas kernels for 0% -> 0%
where the time goes in v12:
time: 147 us; the launch traced here: 146 us
  waiting for transfers between devices  86.5 us (59%)
  matrix products  18.1 us (12%)
  starting transfers between devices  14.8 us (10%)
  between operations  13.6 us (9%)
  local copies, waits for them, and re-layouts  8.87 us (6%)
  other arithmetic  4.45 us (3%)
    ppermute x4, waiting for transfers between devices, from_behind(): return lax.ppermute(value, axis, pairs)  44.3 us
    ppermute x3, waiting for transfers between devices, exchange_heads(): received.append(lax.ppermute(attended, 'head', pairs))  22.6 us
    all_gather x1, waiting for transfers between devices, on_device(): both_parts = lax.all_gather(own_part, ('rep', 'seq'), axis=0, tiled=True)  19.6 us
    ppermute x4, starting transfers between devices, from_behind(): return lax.ppermute(value, axis, pairs)  13 us
    dot_general x5, matrix products, attend_head(): jnp.dot(weights, value_head, preferred_element_type=jnp.float32)  7.79 us
    dot_general x1, matrix products, on_device(): jnp.dot(regrouped, both_parts, preferred_element_type=jnp.float32)  7.16 us
    dot_general x5, matrix products, attend_head(): lax.dot_general(query_head, key_head, (((1,), (1,)), ((), ())), preferred...  3.15 us
  transfers between devices with their start and end apart: 8, of which 6 were waited for; matrix products, arithmetic and copies ran while one was open for 15% of the time, Pallas kernels for 0%

profile of v12, /device:TPU:0, one launch (start us, length us, event | category | flops | bytes accessed | tf_op | source)
XLA Modules:
  0.0 146.2 jit_solution(3383550594420871527)
XLA Ops:
  6.5 0.0 copy-start
  6.5 0.0 all-gather.2.cloned.1.call-start
  6.6 1.4 copy-done
  8.0 1.0 constant_dynamic-slice_fusion
  9.0 0.0 all-gather.2.cloned.1.call-update
  9.0 0.0 copy-done.1
  9.0 0.8 constant_dynamic-update-slice_fusion.1
  9.8 0.0 copy-done.2
  9.8 0.8 constant_dynamic-update-slice_fusion
  10.7 5.9 %collective-permute-start.2 = (bf16[384,1280]{1,0:T(8,128)(2,1)}, bf16[384,1280]{1,0:T(8,128)(2,1)}, u32[]{:S(2)}, u32[]{:S(2)}) collective-permute-start(bf16[384,1280]{1,0:T(8,128)(2,1)} %constant_dynamic-update-slice_fusion), channel_id=1, source_target_pairs={{0,4},{4,8},{8,12},{1,5},{5,9},{9,13},{2,6},{6,10},{10,14},{3,7},{... | collective-permute-start | bytes 2949128 | tf_op jit(solution)/shard_map/ppermute | solution.py:16
  16.6 1.3 collective-permute-start.3
  17.9 0.0 copy-done.3
  17.9 4.5 %collective-permute-start = (s32[384]{0:T(512)S(1)}, s32[384]{0:T(512)S(1)}, u32[]{:S(2)}, u32[]{:S(2)}) collective-permute-start(s32[384]{0:T(512)S(1)} %copy-done.3), channel_id=1, source_target_pairs={{0,4},{4,8},{8,12},{1,5},{5,9},{9,13},{2,6},{6,10},{10,14},{3,7},{... | collective-permute-start | bytes 4616 | tf_op jit(solution)/shard_map/ppermute | solution.py:16
  22.4 1.3 collective-permute-start.1
  23.8 0.0 copy-done.6
  23.8 0.2 and_reduce_fusion
  24.0 0.1 broadcast_in_dim.32
  24.1 29.3 %collective-permute-done = s32[384]{0:T(512)S(1)} collective-permute-done((s32[384]{0:T(512)S(1)}, s32[384]{0:T(512)S(1)}, u32[]{:S(2)}, u32[]{:S(2)}) %collective-permute-start) | collective-permute-done | bytes 1568 | tf_op jit(solution)/shard_map/ppermute | solution.py:16
  53.4 15.0 %collective-permute-done.1 = s32[384]{0:T(512)S(1)} collective-permute-done((s32[384]{0:T(512)S(1)}, s32[384]{0:T(512)S(1)}, u32[]{:S(2)}, u32[]{:S(2)}) %collective-permute-start.1) | collective-permute-done | bytes 1568 | tf_op jit(solution)/shard_map/ppermute | solution.py:16
  68.4 0.0 collective-permute-done.2
  68.4 1.3 slice_bitcast_fusion.1
  69.6 0.0 collective-permute-done.3
  69.7 1.3 slice_bitcast_fusion
  70.9 0.0 copy-start.4
  70.9 0.4 pad_maximum_fusion.1
  71.3 0.6 copy-done.4
  72.0 0.6 fusion.41
  72.6 0.6 fusion.42
  73.2 0.6 fusion.43
  73.8 0.6 fusion.44
  74.5 0.6 fusion.45
  75.1 2.3 %fusion.14 = (f32[384]{0:T(512)S(1)}, f32[384]{0:T(512)S(1)}, f32[384]{0:T(512)S(1)}, f32[384]{0:T(512)S(1)}, f32[384]{0:T(512)S(1)}) fusion(f32[384,1152]{0,1:T(8,128)S(1)} %get-tuple-element.19, f32[384]{0:T(512)S(1)} %get-tuple-element.18, s32[384]{0:T(512)S(1)} %copy-done.3, s32[1152]{0:T(1024)S(1)} %eq.85, pred[1152]{0:T(1024)(128)(4,1)S(1)} %and.49, ...), kind=kLoop, calls=%fused_computation.34 | loop fusion | flops 7518336 | bytes 8870016 | tf_op jit(solution)/shard_map/reduce_sum | solution.py:26
  77.4 1.6 %fusion.15 = bf16[384,640]{0,1:T(8,128)(2,1)} fusion(f32[384,1152]{0,1:T(8,128)S(1)} %get-tuple-element.27, f32[384]{0:T(512)S(1)} %get-tuple-element.9, f32[384]{0:T(512)S(1)} %get-tuple-element.26, s32[384]{0:T(512)S(1)} %copy-done.3, s32[1152]{0:T(1024)S(1)} %eq.85, pred[1152]{0:T(1024)(128)(4,1)S(1)} %and.49, bf16[1152,640]{1,0:T(8,128)(2,1)S(1)} %bitcast.46), kind=kOutput, calls=%fused_computation.40 | convolution fusion | flops 115949568 | bytes 2179072 | tf_op jit(solution)/shard_map/dot_general | solution.py:28
  78.9 1.6 %fusion.16 = bf16[384,640]{0,1:T(8,128)(2,1)} fusion(bf16[384,640]{0,1:T(8,128)(2,1)} %fusion.15, f32[384,1152]{0,1:T(8,128)S(1)} %get-tuple-element.25, f32[384]{0:T(512)S(1)} %get-tuple-element.8, f32[384]{0:T(512)S(1)} %get-tuple-element.24, s32[384]{0:T(512)S(1)} %copy-done.3, s32[1152]{0:T(1024)S(1)} %eq.85, pred[1152]{0:T(1024)(128)(4,1)S(1)} %and.49, ...), kind=kOutput, calls=%fused_computation.41 | convolution fusion | flops 115949568 | bytes 2179072 | tf_op jit(solution)/shard_map/dot_general | solution.py:28
  80.5 1.6 %fusion.17 = bf16[384,640]{0,1:T(8,128)(2,1)} fusion(bf16[384,640]{0,1:T(8,128)(2,1)} %fusion.16, f32[384,1152]{0,1:T(8,128)S(1)} %get-tuple-element.23, f32[384]{0:T(512)S(1)} %get-tuple-element.7, f32[384]{0:T(512)S(1)} %get-tuple-element.22, s32[384]{0:T(512)S(1)} %copy-done.3, s32[1152]{0:T(1024)S(1)} %eq.85, pred[1152]{0:T(1024)(128)(4,1)S(1)} %and.49, ...), kind=kOutput, calls=%fused_computation.42 | convolution fusion | flops 115949568 | bytes 2179072 | tf_op jit(solution)/shard_map/dot_general | solution.py:28
  82.1 1.6 %fusion.18 = bf16[384,640]{0,1:T(8,128)(2,1)} fusion(bf16[384,640]{0,1:T(8,128)(2,1)} %fusion.17, f32[384,1152]{0,1:T(8,128)S(1)} %get-tuple-element.21, f32[384]{0:T(512)S(1)} %get-tuple-element.6, f32[384]{0:T(512)S(1)} %get-tuple-element.20, s32[384]{0:T(512)S(1)} %copy-done.3, s32[1152]{0:T(1024)S(1)} %eq.85, pred[1152]{0:T(1024)(128)(4,1)S(1)} %and.49, ...), kind=kOutput, calls=%fused_computation.43 | convolution fusion | flops 115949568 | bytes 2179072 | tf_op jit(solution)/shard_map/dot_general | solution.py:28
  83.6 1.6 %fusion.19 = bf16[384,640]{0,1:T(8,128)(2,1)} fusion(bf16[384,640]{0,1:T(8,128)(2,1)} %fusion.18, f32[384,1152]{0,1:T(8,128)S(1)} %get-tuple-element.19, f32[384]{0:T(512)S(1)} %get-tuple-element.5, f32[384]{0:T(512)S(1)} %get-tuple-element.18, s32[384]{0:T(512)S(1)} %copy-done.3, s32[1152]{0:T(1024)S(1)} %eq.85, pred[1152]{0:T(1024)(128)(4,1)S(1)} %and.49, ...), kind=kOutput, calls=%fused_computation.44 | convolution fusion | flops 115949568 | bytes 2179072 | tf_op jit(solution)/shard_map/dot_general | solution.py:28
  85.2 0.0 collective-permute-start.4
  85.2 1.5 %collective-permute-start.5 = (bf16[384,640]{0,1:T(8,128)(2,1)}, bf16[384,640]{0,1:T(8,128)(2,1)S(1)}, u32[]{:S(2)}, u32[]{:S(2)}) collective-permute-start(bf16[384,640]{0,1:T(8,128)(2,1)} %fusion.19), channel_id=1, source_target_pairs={{0,2},{1,3},{2,0},{3,1},{4,6},{5,7},{6,4},{7,5},{8,10},{9,11},{10,... | collective-permute-start | bytes 1474568 | tf_op jit(solution)/shard_map/ppermute | solution.py:37
  86.7 0.2 collective-permute-start.6
  86.9 9.2 %collective-permute-done.4 = bf16[384,640]{0,1:T(8,128)(2,1)S(1)} collective-permute-done((bf16[384,640]{0,1:T(8,128)(2,1)}, bf16[384,640]{0,1:T(8,128)(2,1)S(1)}, u32[]{:S(2)}, u32[]{:S(2)}) %collective-permute-start.4) | collective-permute-done | bytes 491552 | tf_op jit(solution)/shard_map/ppermute | solution.py:37
  96.1 13.3 %collective-permute-done.5 = bf16[384,640]{0,1:T(8,128)(2,1)S(1)} collective-permute-done((bf16[384,640]{0,1:T(8,128)(2,1)}, bf16[384,640]{0,1:T(8,128)(2,1)S(1)}, u32[]{:S(2)}, u32[]{:S(2)}) %collective-permute-start.5) | collective-permute-done | bytes 491552 | tf_op jit(solution)/shard_map/ppermute | solution.py:37
  109.4 0.1 collective-permute-done.6
  109.5 1.4 select_select_fusion.3
  110.9 0.2 pad_maximum_fusion
  111.1 1.5 %copy.9 = bf16[384,4,2,320]{0,3,1,2:T(8,128)(2,1)} copy(bf16[384,4,2,320]{0,3,2,1:T(8,128)(2,1)S(1)} %bitcast.42) | data formatting | bytes 3932160 | tf_op jit(solution)/shard_map/reshape | solution.py:106
  112.6 19.6 %all-gather.2.cloned.1.call-done = bf16[2560,1280]{1,0:T(8,128)(2,1)} async-done(((bf16[320,1280]{1,0:T(8,128)(2,1)}), bf16[2560,1280]{1,0:T(8,128)(2,1)}) %all-gather.2.cloned.1.call-update) | async-done | bytes 6553616 | tf_op jit(solution)/shard_map/all_gather | solution.py:64
  132.2 7.2 %convolution_convert_fusion = bf16[384,1280]{1,0:T(8,128)(2,1)} fusion(bf16[384,2560]{0,1:T(8,128)(2,1)} %bitcast.43, bf16[2560,1280]{1,0:T(8,128)(2,1)} %all-gather.2.cloned.1.call-done), kind=kOutput, calls=%fused_computation.15 | convolution fusion | flops 2517073920 | bytes 9502720 | tf_op jit(solution)/shard_map/dot_general | solution.py:108
  (15 shorter events, 0.1 us)
Async XLA Ops:
  6.5 1.4 copy-start
  6.5 2.5 %copy-start.1 = (bf16[384,640]{1,0:T(8,128)(2,1)S(1)}, bf16[384,640]{1,0:T(8,128)(2,1)}, u32[]{:S(2)}) copy-start(bf16[384,640]{1,0:T(8,128)(2,1)} %param.8) | copy-start | bytes 1474564
  6.5 3.3 %copy-start.2 = (bf16[384,640]{1,0:T(8,128)(2,1)S(1)}, bf16[384,640]{1,0:T(8,128)(2,1)}, u32[]{:S(2)}) copy-start(bf16[384,640]{1,0:T(8,128)(2,1)} %param.9) | copy-start | bytes 1474564
  6.5 125.7 %all-gather.2.cloned.1.call-start = ((), (), s32[]{:S(2)}) async-start(), calls=%async_computation | async-start | bytes 7372800 | tf_op jit(solution)/shard_map/all_gather | solution.py:64
  9.0 8.9 %copy-start.3 = (s32[384]{0:T(512)S(1)}, s32[384]{0:T(512)}, u32[]{:S(2)}) copy-start(s32[384]{0:T(512)} %param.12) | copy-start | bytes 4612
  9.0 14.8 %copy-start.5 = (s32[4,27]{1,0:T(4,128)S(1)}, s32[4,27]{1,0:T(4,128)}, u32[]{:S(2)}) copy-start(s32[4,27]{1,0:T(4,128)} %param.11) | copy-start | bytes 1300
  9.0 14.8 %copy-start.6 = (s32[3]{0:T(128)S(1)}, s32[3]{0:T(128)}, u32[]{:S(2)}) copy-start(s32[3]{0:T(128)} %constant.86) | copy-start | bytes 40
  10.7 57.7 %collective-permute-start.2 = (bf16[384,1280]{1,0:T(8,128)(2,1)}, bf16[384,1280]{1,0:T(8,128)(2,1)}, u32[]{:S(2)}, u32[]{:S(2)}) collective-permute-start(bf16[384,1280]{1,0:T(8,128)(2,1)} %constant_dynamic-update-slice_fusion), channel_id=1, source_target_pairs={{0,4},{4,8},{8,12},{1,5},{5,9},{9,13},{2,6},{6,10},{10,14},{3,7},{... | collective-permute-start | bytes 2949128 | tf_op jit(solution)/shard_map/ppermute | solution.py:16
  16.6 53.1 %collective-permute-start.3 = (bf16[384,1280]{1,0:T(8,128)(2,1)}, bf16[384,1280]{1,0:T(8,128)(2,1)}, u32[]{:S(2)}, u32[]{:S(2)}) collective-permute-start(bf16[384,1280]{1,0:T(8,128)(2,1)} %constant_dynamic-update-slice_fusion), channel_id=1, source_target_pairs={{4,0},{8,4},{12,8},{5,1},{9,5},{13,9},{6,2},{10,6},{14,10},{7,3},{... | collective-permute-start | bytes 2949128 | tf_op jit(solution)/shard_map/ppermute | solution.py:16
  17.9 35.5 %collective-permute-start = (s32[384]{0:T(512)S(1)}, s32[384]{0:T(512)S(1)}, u32[]{:S(2)}, u32[]{:S(2)}) collective-permute-start(s32[384]{0:T(512)S(1)} %copy-done.3), channel_id=1, source_target_pairs={{0,4},{4,8},{8,12},{1,5},{5,9},{9,13},{2,6},{6,10},{10,14},{3,7},{... | collective-permute-start | bytes 4616 | tf_op jit(solution)/shard_map/ppermute | solution.py:16
  22.4 45.9 %collective-permute-start.1 = (s32[384]{0:T(512)S(1)}, s32[384]{0:T(512)S(1)}, u32[]{:S(2)}, u32[]{:S(2)}) collective-permute-start(s32[384]{0:T(512)S(1)} %copy-done.3), channel_id=1, source_target_pairs={{4,0},{8,4},{12,8},{5,1},{9,5},{13,9},{6,2},{10,6},{14,10},{7,3},{... | collective-permute-start | bytes 4616 | tf_op jit(solution)/shard_map/ppermute | solution.py:16
  70.9 1.0 copy-start.4
  85.2 10.9 %collective-permute-start.4 = (bf16[384,640]{0,1:T(8,128)(2,1)}, bf16[384,640]{0,1:T(8,128)(2,1)S(1)}, u32[]{:S(2)}, u32[]{:S(2)}) collective-permute-start(bf16[384,640]{0,1:T(8,128)(2,1)} %fusion.19), channel_id=1, source_target_pairs={{0,3},{1,0},{2,1},{3,2},{4,7},{5,4},{6,5},{7,6},{8,11},{9,8},{10,9... | collective-permute-start | bytes 1474568 | tf_op jit(solution)/shard_map/ppermute | solution.py:37
  85.2 24.2 %collective-permute-start.5 = (bf16[384,640]{0,1:T(8,128)(2,1)}, bf16[384,640]{0,1:T(8,128)(2,1)S(1)}, u32[]{:S(2)}, u32[]{:S(2)}) collective-permute-start(bf16[384,640]{0,1:T(8,128)(2,1)} %fusion.19), channel_id=1, source_target_pairs={{0,2},{1,3},{2,0},{3,1},{4,6},{5,7},{6,4},{7,5},{8,10},{9,11},{10,... | collective-permute-start | bytes 1474568 | tf_op jit(solution)/shard_map/ppermute | solution.py:37
  86.7 22.8 %collective-permute-start.6 = (bf16[384,640]{0,1:T(8,128)(2,1)}, bf16[384,640]{0,1:T(8,128)(2,1)S(1)}, u32[]{:S(2)}, u32[]{:S(2)}) collective-permute-start(bf16[384,640]{0,1:T(8,128)(2,1)} %fusion.19), channel_id=1, source_target_pairs={{0,1},{1,2},{2,3},{3,0},{4,5},{5,6},{6,7},{7,4},{8,9},{9,10},{10,1... | collective-permute-start | bytes 1474568 | tf_op jit(solution)/shard_map/ppermute | solution.py:37
Sparse Core Ops, SparseCore 0:
  9.5 122.7 all-gather.1

commit v13 on v11

--- a/solution.py
+++ b/solution.py
@@ -60,7 +60,13 @@
 
     rep_count = lax.axis_size("rep")
     part_rows = out_weight.shape[0] // rep_count
-    own_part = lax.dynamic_slice_in_dim(out_weight, rep_position * part_rows, part_rows, axis=0)
+    own_part = out_weight[:part_rows]
+    for rep_index in range(1, rep_count):
+        own_part = jnp.where(
+            rep_position == rep_index,
+            out_weight[rep_index * part_rows : (rep_index + 1) * part_rows],
+            own_part,
+        )
     both_parts = lax.all_gather(own_part, ("rep", "seq"), axis=0, tiled=True)
 
     key_list = [keys]

time: 145 us -> 144 us (level)
  waiting for transfers between devices: 81.5 us -> 89.1 us
  matrix products: 18.1 us -> 14.3 us
  local copies, waits for them, and re-layouts: 4.28 us -> 1.15 us
    all_gather x1, waiting for transfers between devices: 20.7 us -> 27.8 us  [on_device(): both_parts = lax.all_gather(own_part, ('rep', 'seq'), axis=0, tiled=True)]
    dot_general x5, matrix products: 7.77 us -> 4.61 us  [attend_head(): jnp.dot(weights, value_head, preferred_element_type=jnp.float32)]
    select_n x0 -> x1, other arithmetic: none -> 2.45 us  [on_device(): jnp.where(rep_position == rep_index, out_weight[rep_index * part_rows:(re...]
  transfers between devices with their start and end apart: 10 -> 10, of which waited for: 6 -> 6; matrix products, arithmetic and copies ran while one was open for 13% -> 8% of each run, Pallas kernels for 0% -> 0%
where the time goes in v13:
time: 144 us
  waiting for transfers between devices  89.1 us (62%)
  starting transfers between devices  19.8 us (14%)
  matrix products  14.3 us (10%)
  between operations  13.6 us (9%)
  other arithmetic  5.85 us (4%)
    ppermute x6, waiting for transfers between devices, from_behind(): return lax.ppermute(value, axis, pairs)  39 us
    all_gather x1, waiting for transfers between devices, on_device(): both_parts = lax.all_gather(own_part, ('rep', 'seq'), axis=0, tiled=True)  27.8 us
    ppermute x3, waiting for transfers between devices, exchange_heads(): received.append(lax.ppermute(attended, 'head', pairs))  22.4 us
    ppermute x6, starting transfers between devices, from_behind(): return lax.ppermute(value, axis, pairs)  17.9 us
    dot_general x1, matrix products, on_device(): jnp.dot(regrouped, both_parts, preferred_element_type=jnp.float32)  6.55 us
    dot_general x5, matrix products, attend_head(): jnp.dot(weights, value_head, preferred_element_type=jnp.float32)  4.61 us
    dot_general x5, matrix products, attend_head(): lax.dot_general(query_head, key_head, (((1,), (1,)), ((), ())), preferred...  3.17 us
  transfers between devices with their start and end apart: 10, of which 6 were waited for; matrix products, arithmetic and copies ran while one was open for 8% of the time, Pallas kernels for 0%

profile of v13, /device:TPU:0, one launch (start us, length us, event | category | flops | bytes accessed | tf_op | source)
XLA Modules:
  0.0 143.8 jit_solution(10430558124561533073)
XLA Ops:
  6.5 0.0 all-gather.2.cloned.1.call-start
  6.6 2.4 %slice_select_fusion = bf16[320,1280]{1,0:T(8,128)(2,1)} fusion(bf16[640,1280]{1,0:T(8,128)(2,1)} %param.10, pred[]{:T(512)S(6)} %eq.102), kind=kLoop, calls=%fused_computation.45 | loop fusion | flops 409600 | bytes 2457601 | tf_op jit(solution)/shard_map/jit(_where)/select_n | solution.py:65
  9.0 0.0 all-gather.2.cloned.1.call-update
  9.1 0.0 copy-done
  9.1 5.0 %collective-permute-start.2 = (bf16[384,640]{1,0:T(8,128)(2,1)S(1)}, bf16[384,640]{1,0:T(8,128)(2,1)S(1)}, u32[]{:S(2)}, u32[]{:S(2)}) collective-permute-start(bf16[384,640]{1,0:T(8,128)(2,1)S(1)} %copy-done), channel_id=1, source_target_pairs={{0,4},{4,8},{8,12},{1,5},{5,9},{9,13},{2,6},{6,10},{10,14},{3,7},{... | collective-permute-start | bytes 1474568 | tf_op jit(solution)/shard_map/ppermute | solution.py:16
  14.0 1.3 collective-permute-start.3
  15.3 0.0 copy-done.1
  15.4 4.6 %collective-permute-start.4 = (bf16[384,640]{1,0:T(8,128)(2,1)S(1)}, bf16[384,640]{1,0:T(8,128)(2,1)S(1)}, u32[]{:S(2)}, u32[]{:S(2)}) collective-permute-start(bf16[384,640]{1,0:T(8,128)(2,1)S(1)} %copy-done.1), channel_id=1, source_target_pairs={{0,4},{4,8},{8,12},{1,5},{5,9},{9,13},{2,6},{6,10},{10,14},{3,7},{... | collective-permute-start | bytes 1474568 | tf_op jit(solution)/shard_map/ppermute | solution.py:16
  19.9 1.3 collective-permute-start.5
  21.2 0.0 copy-done.2
  21.2 4.5 %collective-permute-start = (s32[384]{0:T(512)S(1)}, s32[384]{0:T(512)S(1)}, u32[]{:S(2)}, u32[]{:S(2)}) collective-permute-start(s32[384]{0:T(512)S(1)} %copy-done.2), channel_id=1, source_target_pairs={{0,4},{4,8},{8,12},{1,5},{5,9},{9,13},{2,6},{6,10},{10,14},{3,7},{... | collective-permute-start | bytes 4616 | tf_op jit(solution)/shard_map/ppermute | solution.py:16
  25.8 0.0 copy-done.5
  25.8 0.0 copy-done.4
  25.9 23.9 %collective-permute-done = s32[384]{0:T(512)S(1)} collective-permute-done((s32[384]{0:T(512)S(1)}, s32[384]{0:T(512)S(1)}, u32[]{:S(2)}, u32[]{:S(2)}) %collective-permute-start) | collective-permute-done | bytes 1568 | tf_op jit(solution)/shard_map/ppermute | solution.py:16
  49.7 1.3 collective-permute-start.1
  51.0 0.2 and_reduce_fusion
  51.2 0.1 broadcast_in_dim.32
  51.3 15.1 %collective-permute-done.1 = s32[384]{0:T(512)S(1)} collective-permute-done((s32[384]{0:T(512)S(1)}, s32[384]{0:T(512)S(1)}, u32[]{:S(2)}, u32[]{:S(2)}) %collective-permute-start.1) | collective-permute-done | bytes 1568 | tf_op jit(solution)/shard_map/ppermute | solution.py:16
  66.4 0.0 collective-permute-done.2
  66.5 0.0 collective-permute-done.3
  66.5 0.2 pad_maximum_fusion.1
  66.7 0.0 copy-start.3
  66.7 0.0 collective-permute-done.4
  66.7 0.0 collective-permute-done.5
  66.7 0.2 pad_maximum_fusion.2
  66.9 0.8 copy-done.3
  67.7 0.6 fusion.41
  68.3 0.6 fusion.42
  69.0 0.6 fusion.43
  69.6 0.6 fusion.44
  70.2 0.6 fusion.45
  70.9 2.3 %fusion.14 = (f32[384]{0:T(512)S(1)}, f32[384]{0:T(512)S(1)}, f32[384]{0:T(512)S(1)}, f32[384]{0:T(512)S(1)}, f32[384]{0:T(512)S(1)}) fusion(f32[384,1152]{0,1:T(8,128)S(1)} %get-tuple-element.15, f32[384]{0:T(512)S(1)} %get-tuple-element.14, s32[384]{0:T(512)S(1)} %copy-done.2, s32[1152]{0:T(1024)S(1)} %eq.88, pred[1152]{0:T(1024)(128)(4,1)S(1)} %and.49, ...), kind=kLoop, calls=%fused_computation.34 | loop fusion | flops 7518336 | bytes 8870016 | tf_op jit(solution)/shard_map/reduce_sum | solution.py:26
  73.2 0.9 fusion.15
  74.1 0.9 fusion.16
  75.0 0.9 fusion.17
  75.9 0.9 fusion.18
  76.9 0.9 fusion.19
  77.8 0.1 collective-permute-start.6
  77.9 1.5 %collective-permute-start.7 = (bf16[384,640]{0,1:T(8,128)(2,1)S(1)}, bf16[384,640]{0,1:T(8,128)(2,1)S(1)}, u32[]{:S(2)}, u32[]{:S(2)}) collective-permute-start(bf16[384,640]{0,1:T(8,128)(2,1)S(1)} %fusion.19), channel_id=1, source_target_pairs={{0,2},{1,3},{2,0},{3,1},{4,6},{5,7},{6,4},{7,5},{8,10},{9,11},{10,... | collective-permute-start | bytes 1474568 | tf_op jit(solution)/shard_map/ppermute | solution.py:37
  79.4 0.2 collective-permute-start.8
  79.6 8.9 %collective-permute-done.6 = bf16[384,640]{0,1:T(8,128)(2,1)S(1)} collective-permute-done((bf16[384,640]{0,1:T(8,128)(2,1)S(1)}, bf16[384,640]{0,1:T(8,128)(2,1)S(1)}, u32[]{:S(2)}, u32[]{:S(2)}) %collective-permute-start.6) | collective-permute-done | bytes 491552 | tf_op jit(solution)/shard_map/ppermute | solution.py:37
  88.4 13.4 %collective-permute-done.7 = bf16[384,640]{0,1:T(8,128)(2,1)S(1)} collective-permute-done((bf16[384,640]{0,1:T(8,128)(2,1)S(1)}, bf16[384,640]{0,1:T(8,128)(2,1)S(1)}, u32[]{:S(2)}, u32[]{:S(2)}) %collective-permute-start.7) | collective-permute-done | bytes 491552 | tf_op jit(solution)/shard_map/ppermute | solution.py:37
  101.8 0.1 collective-permute-done.8
  101.9 0.3 select_select_fusion.3
  102.3 0.2 pad_maximum_fusion
  102.5 0.2 copy.9
  102.7 27.8 %all-gather.2.cloned.1.call-done = bf16[2560,1280]{1,0:T(8,128)(2,1)} async-done(((bf16[320,1280]{1,0:T(8,128)(2,1)}), bf16[2560,1280]{1,0:T(8,128)(2,1)}) %all-gather.2.cloned.1.call-update) | async-done | bytes 6553616 | tf_op jit(solution)/shard_map/all_gather | solution.py:70
  130.4 6.6 %convolution_convert_fusion = bf16[384,1280]{1,0:T(8,128)(2,1)} fusion(bf16[384,2560]{0,1:T(8,128)(2,1)S(1)} %bitcast.39, bf16[2560,1280]{1,0:T(8,128)(2,1)} %all-gather.2.cloned.1.call-done), kind=kOutput, calls=%fused_computation.15 | convolution fusion | flops 2517073920 | bytes 9502720 | tf_op jit(solution)/shard_map/dot_general | solution.py:117
  (14 shorter events, 0.1 us)
Async XLA Ops:
  6.5 19.3 %copy-start.5 = (s32[3]{0:T(128)S(1)}, s32[3]{0:T(128)}, u32[]{:S(2)}) copy-start(s32[3]{0:T(128)} %constant.82) | copy-start | bytes 40
  6.5 2.5 %copy-start = (bf16[384,640]{1,0:T(8,128)(2,1)S(1)}, bf16[384,640]{1,0:T(8,128)(2,1)}, u32[]{:S(2)}) copy-start(bf16[384,640]{1,0:T(8,128)(2,1)} %param.8) | copy-start | bytes 1474564
  6.5 8.8 %copy-start.1 = (bf16[384,640]{1,0:T(8,128)(2,1)S(1)}, bf16[384,640]{1,0:T(8,128)(2,1)}, u32[]{:S(2)}) copy-start(bf16[384,640]{1,0:T(8,128)(2,1)} %param.9) | copy-start | bytes 1474564
  6.5 14.7 %copy-start.2 = (s32[384]{0:T(512)S(1)}, s32[384]{0:T(512)}, u32[]{:S(2)}) copy-start(s32[384]{0:T(512)} %param.12) | copy-start | bytes 4612
  6.5 19.3 %copy-start.4 = (s32[4,27]{1,0:T(4,128)S(1)}, s32[4,27]{1,0:T(4,128)}, u32[]{:S(2)}) copy-start(s32[4,27]{1,0:T(4,128)} %param.11) | copy-start | bytes 1300
  6.5 123.9 %all-gather.2.cloned.1.call-start = ((), (), s32[]{:S(2)}) async-start(), calls=%async_computation | async-start | bytes 7372800 | tf_op jit(solution)/shard_map/all_gather | solution.py:70
  9.1 57.4 %collective-permute-start.2 = (bf16[384,640]{1,0:T(8,128)(2,1)S(1)}, bf16[384,640]{1,0:T(8,128)(2,1)S(1)}, u32[]{:S(2)}, u32[]{:S(2)}) collective-permute-start(bf16[384,640]{1,0:T(8,128)(2,1)S(1)} %copy-done), channel_id=1, source_target_pairs={{0,4},{4,8},{8,12},{1,5},{5,9},{9,13},{2,6},{6,10},{10,14},{3,7},{... | collective-permute-start | bytes 1474568 | tf_op jit(solution)/shard_map/ppermute | solution.py:16
  14.0 52.4 %collective-permute-start.3 = (bf16[384,640]{1,0:T(8,128)(2,1)S(1)}, bf16[384,640]{1,0:T(8,128)(2,1)S(1)}, u32[]{:S(2)}, u32[]{:S(2)}) collective-permute-start(bf16[384,640]{1,0:T(8,128)(2,1)S(1)} %copy-done), channel_id=1, source_target_pairs={{4,0},{8,4},{12,8},{5,1},{9,5},{13,9},{6,2},{10,6},{14,10},{7,3},{... | collective-permute-start | bytes 1474568 | tf_op jit(solution)/shard_map/ppermute | solution.py:16
  15.4 51.3 %collective-permute-start.4 = (bf16[384,640]{1,0:T(8,128)(2,1)S(1)}, bf16[384,640]{1,0:T(8,128)(2,1)S(1)}, u32[]{:S(2)}, u32[]{:S(2)}) collective-permute-start(bf16[384,640]{1,0:T(8,128)(2,1)S(1)} %copy-done.1), channel_id=1, source_target_pairs={{0,4},{4,8},{8,12},{1,5},{5,9},{9,13},{2,6},{6,10},{10,14},{3,7},{... | collective-permute-start | bytes 1474568 | tf_op jit(solution)/shard_map/ppermute | solution.py:16
  19.9 46.8 %collective-permute-start.5 = (bf16[384,640]{1,0:T(8,128)(2,1)S(1)}, bf16[384,640]{1,0:T(8,128)(2,1)S(1)}, u32[]{:S(2)}, u32[]{:S(2)}) collective-permute-start(bf16[384,640]{1,0:T(8,128)(2,1)S(1)} %copy-done.1), channel_id=1, source_target_pairs={{4,0},{8,4},{12,8},{5,1},{9,5},{13,9},{6,2},{10,6},{14,10},{7,3},{... | collective-permute-start | bytes 1474568 | tf_op jit(solution)/shard_map/ppermute | solution.py:16
  21.2 28.5 %collective-permute-start = (s32[384]{0:T(512)S(1)}, s32[384]{0:T(512)S(1)}, u32[]{:S(2)}, u32[]{:S(2)}) collective-permute-start(s32[384]{0:T(512)S(1)} %copy-done.2), channel_id=1, source_target_pairs={{0,4},{4,8},{8,12},{1,5},{5,9},{9,13},{2,6},{6,10},{10,14},{3,7},{... | collective-permute-start | bytes 4616 | tf_op jit(solution)/shard_map/ppermute | solution.py:16
  49.7 16.7 %collective-permute-start.1 = (s32[384]{0:T(512)S(1)}, s32[384]{0:T(512)S(1)}, u32[]{:S(2)}, u32[]{:S(2)}) collective-permute-start(s32[384]{0:T(512)S(1)} %copy-done.2), channel_id=1, source_target_pairs={{4,0},{8,4},{12,8},{5,1},{9,5},{13,9},{6,2},{10,6},{14,10},{7,3},{... | collective-permute-start | bytes 4616 | tf_op jit(solution)/shard_map/ppermute | solution.py:16
  66.7 1.0 copy-start.3
  77.8 10.6 %collective-permute-start.6 = (bf16[384,640]{0,1:T(8,128)(2,1)S(1)}, bf16[384,640]{0,1:T(8,128)(2,1)S(1)}, u32[]{:S(2)}, u32[]{:S(2)}) collective-permute-start(bf16[384,640]{0,1:T(8,128)(2,1)S(1)} %fusion.19), channel_id=1, source_target_pairs={{0,3},{1,0},{2,1},{3,2},{4,7},{5,4},{6,5},{7,6},{8,11},{9,8},{10,9... | collective-permute-start | bytes 1474568 | tf_op jit(solution)/shard_map/ppermute | solution.py:37
  77.9 24.0 %collective-permute-start.7 = (bf16[384,640]{0,1:T(8,128)(2,1)S(1)}, bf16[384,640]{0,1:T(8,128)(2,1)S(1)}, u32[]{:S(2)}, u32[]{:S(2)}) collective-permute-start(bf16[384,640]{0,1:T(8,128)(2,1)S(1)} %fusion.19), channel_id=1, source_target_pairs={{0,2},{1,3},{2,0},{3,1},{4,6},{5,7},{6,4},{7,5},{8,10},{9,11},{10,... | collective-permute-start | bytes 1474568 | tf_op jit(solution)/shard_map/ppermute | solution.py:37
  79.4 22.5 %collective-permute-start.8 = (bf16[384,640]{0,1:T(8,128)(2,1)S(1)}, bf16[384,640]{0,1:T(8,128)(2,1)S(1)}, u32[]{:S(2)}, u32[]{:S(2)}) collective-permute-start(bf16[384,640]{0,1:T(8,128)(2,1)S(1)} %fusion.19), channel_id=1, source_target_pairs={{0,1},{1,2},{2,3},{3,0},{4,5},{5,6},{6,7},{7,4},{8,9},{9,10},{10,1... | collective-permute-start | bytes 1474568 | tf_op jit(solution)/shard_map/ppermute | solution.py:37
Sparse Core Ops, SparseCore 0:
  9.5 120.9 all-gather.1

commit v14 on v11

--- a/solution.py
+++ b/solution.py
@@ -60,7 +60,9 @@
 
     rep_count = lax.axis_size("rep")
     part_rows = out_weight.shape[0] // rep_count
-    own_part = lax.dynamic_slice_in_dim(out_weight, rep_position * part_rows, part_rows, axis=0)
+    own_part = jnp.take(
+        out_weight.reshape(rep_count, part_rows, out_weight.shape[1]), rep_position, axis=0
+    )
     both_parts = lax.all_gather(own_part, ("rep", "seq"), axis=0, tiled=True)
 
     key_list = [keys]

time: 145 us -> 144 us (level)
  waiting for transfers between devices: 81.5 us -> 89.1 us
  matrix products: 18.1 us -> 14.3 us
  local copies, waits for them, and re-layouts: 4.28 us -> 1.15 us
    all_gather x1, waiting for transfers between devices: 20.7 us -> 27.7 us  [on_device(): both_parts = lax.all_gather(own_part, ('rep', 'seq'), axis=0, tiled=True)]
    dot_general x5, matrix products: 7.77 us -> 4.61 us  [attend_head(): jnp.dot(weights, value_head, preferred_element_type=jnp.float32)]
    select_n x0 -> x1, other arithmetic: none -> 2.19 us  [on_device(): jnp.take(out_weight.reshape(rep_count, part_rows, out_weight.shape[1]), r...]
  transfers between devices with their start and end apart: 10 -> 10, of which waited for: 6 -> 6; matrix products, arithmetic and copies ran while one was open for 13% -> 8% of each run, Pallas kernels for 0% -> 0%
where the time goes in v14:
time: 144 us
  waiting for transfers between devices  89.1 us (62%)
  starting transfers between devices  19.8 us (14%)
  matrix products  14.3 us (10%)
  between operations  13.6 us (9%)
  other arithmetic  5.59 us (4%)
    ppermute x6, waiting for transfers between devices, from_behind(): return lax.ppermute(value, axis, pairs)  39 us
    all_gather x1, waiting for transfers between devices, on_device(): both_parts = lax.all_gather(own_part, ('rep', 'seq'), axis=0, tiled=True)  27.7 us
    ppermute x3, waiting for transfers between devices, exchange_heads(): received.append(lax.ppermute(attended, 'head', pairs))  22.4 us
    ppermute x6, starting transfers between devices, from_behind(): return lax.ppermute(value, axis, pairs)  17.9 us
    dot_general x1, matrix products, on_device(): jnp.dot(regrouped, both_parts, preferred_element_type=jnp.float32)  6.56 us
    dot_general x5, matrix products, attend_head(): jnp.dot(weights, value_head, preferred_element_type=jnp.float32)  4.61 us
    dot_general x5, matrix products, attend_head(): lax.dot_general(query_head, key_head, (((1,), (1,)), ((), ())), preferred...  3.17 us
  transfers between devices with their start and end apart: 10, of which 6 were waited for; matrix products, arithmetic and copies ran while one was open for 8% of the time, Pallas kernels for 0%

profile of v14, /device:TPU:0, one launch (start us, length us, event | category | flops | bytes accessed | tf_op | source)
XLA Modules:
  0.0 143.6 jit_solution(12430091760108453416)
XLA Ops:
  6.5 0.0 all-gather.3.cloned.1.call-start
  6.6 2.2 %dynamic-slice_select_fusion = bf16[1,320,1280]{2,1,0:T(8,128)(2,1)} fusion(bf16[2,320,1280]{2,1,0:T(8,128)(2,1)} %bitcast.61, s32[]{:T(128)S(6)} %select_n.188, pred[]{:T(512)S(6)} %and.59), kind=kLoop, calls=%fused_computation.47 | loop fusion | flops 409600 | bytes 1638405 | tf_op jit(solution)/shard_map/jit(_take)/select_n | solution.py:63
  8.8 0.0 all-gather.3.cloned.1.call-update
  8.8 0.0 copy-done
  8.8 5.0 %collective-permute-start.2 = (bf16[384,640]{1,0:T(8,128)(2,1)S(1)}, bf16[384,640]{1,0:T(8,128)(2,1)S(1)}, u32[]{:S(2)}, u32[]{:S(2)}) collective-permute-start(bf16[384,640]{1,0:T(8,128)(2,1)S(1)} %copy-done), channel_id=1, source_target_pairs={{0,4},{4,8},{8,12},{1,5},{5,9},{9,13},{2,6},{6,10},{10,14},{3,7},{... | collective-permute-start | bytes 1474568 | tf_op jit(solution)/shard_map/ppermute | solution.py:16
  13.8 1.3 collective-permute-start.3
  15.1 0.0 copy-done.1
  15.1 4.6 %collective-permute-start.4 = (bf16[384,640]{1,0:T(8,128)(2,1)S(1)}, bf16[384,640]{1,0:T(8,128)(2,1)S(1)}, u32[]{:S(2)}, u32[]{:S(2)}) collective-permute-start(bf16[384,640]{1,0:T(8,128)(2,1)S(1)} %copy-done.1), channel_id=1, source_target_pairs={{0,4},{4,8},{8,12},{1,5},{5,9},{9,13},{2,6},{6,10},{10,14},{3,7},{... | collective-permute-start | bytes 1474568 | tf_op jit(solution)/shard_map/ppermute | solution.py:16
  19.7 1.3 collective-permute-start.5
  21.0 0.0 copy-done.2
  21.0 4.5 %collective-permute-start = (s32[384]{0:T(512)S(1)}, s32[384]{0:T(512)S(1)}, u32[]{:S(2)}, u32[]{:S(2)}) collective-permute-start(s32[384]{0:T(512)S(1)} %copy-done.2), channel_id=1, source_target_pairs={{0,4},{4,8},{8,12},{1,5},{5,9},{9,13},{2,6},{6,10},{10,14},{3,7},{... | collective-permute-start | bytes 4616 | tf_op jit(solution)/shard_map/ppermute | solution.py:16
  25.6 0.0 copy-done.5
  25.6 0.0 copy-done.4
  25.6 23.6 %collective-permute-done = s32[384]{0:T(512)S(1)} collective-permute-done((s32[384]{0:T(512)S(1)}, s32[384]{0:T(512)S(1)}, u32[]{:S(2)}, u32[]{:S(2)}) %collective-permute-start) | collective-permute-done | bytes 1568 | tf_op jit(solution)/shard_map/ppermute | solution.py:16
  49.2 1.3 collective-permute-start.1
  50.5 0.2 and_reduce_fusion
  50.7 0.1 broadcast_in_dim.44
  50.8 15.3 %collective-permute-done.1 = s32[384]{0:T(512)S(1)} collective-permute-done((s32[384]{0:T(512)S(1)}, s32[384]{0:T(512)S(1)}, u32[]{:S(2)}, u32[]{:S(2)}) %collective-permute-start.1) | collective-permute-done | bytes 1568 | tf_op jit(solution)/shard_map/ppermute | solution.py:16
  66.2 0.0 collective-permute-done.2
  66.2 0.0 collective-permute-done.3
  66.2 0.2 pad_maximum_fusion.1
  66.4 0.0 copy-start.3
  66.4 0.0 collective-permute-done.4
  66.4 0.0 collective-permute-done.5
  66.5 0.2 pad_maximum_fusion.2
  66.7 0.8 copy-done.3
  67.5 0.6 fusion.46
  68.1 0.6 fusion.47
  68.7 0.6 fusion.48
  69.4 0.6 fusion.49
  70.0 0.6 fusion.50
  70.6 2.3 %fusion.19 = (f32[384]{0:T(512)S(1)}, f32[384]{0:T(512)S(1)}, f32[384]{0:T(512)S(1)}, f32[384]{0:T(512)S(1)}, f32[384]{0:T(512)S(1)}) fusion(f32[384,1152]{0,1:T(8,128)S(1)} %get-tuple-element.26, f32[384]{0:T(512)S(1)} %get-tuple-element.25, s32[384]{0:T(512)S(1)} %copy-done.2, s32[1152]{0:T(1024)S(1)} %eq.85, pred[1152]{0:T(1024)(128)(4,1)S(1)} %and.53, ...), kind=kLoop, calls=%fused_computation.36 | loop fusion | flops 7518336 | bytes 8870016 | tf_op jit(solution)/shard_map/reduce_sum | solution.py:26
  72.9 0.9 fusion.20
  73.8 0.9 fusion.21
  74.8 0.9 fusion.22
  75.7 0.9 fusion.23
  76.6 0.9 fusion.24
  77.5 0.1 collective-permute-start.6
  77.6 1.6 %collective-permute-start.7 = (bf16[384,640]{0,1:T(8,128)(2,1)S(1)}, bf16[384,640]{0,1:T(8,128)(2,1)S(1)}, u32[]{:S(2)}, u32[]{:S(2)}) collective-permute-start(bf16[384,640]{0,1:T(8,128)(2,1)S(1)} %fusion.24), channel_id=1, source_target_pairs={{0,2},{1,3},{2,0},{3,1},{4,6},{5,7},{6,4},{7,5},{8,10},{9,11},{10,... | collective-permute-start | bytes 1474568 | tf_op jit(solution)/shard_map/ppermute | solution.py:37
  79.2 0.2 collective-permute-start.8
  79.3 8.8 %collective-permute-done.6 = bf16[384,640]{0,1:T(8,128)(2,1)S(1)} collective-permute-done((bf16[384,640]{0,1:T(8,128)(2,1)S(1)}, bf16[384,640]{0,1:T(8,128)(2,1)S(1)}, u32[]{:S(2)}, u32[]{:S(2)}) %collective-permute-start.6) | collective-permute-done | bytes 491552 | tf_op jit(solution)/shard_map/ppermute | solution.py:37
  88.2 13.5 %collective-permute-done.7 = bf16[384,640]{0,1:T(8,128)(2,1)S(1)} collective-permute-done((bf16[384,640]{0,1:T(8,128)(2,1)S(1)}, bf16[384,640]{0,1:T(8,128)(2,1)S(1)}, u32[]{:S(2)}, u32[]{:S(2)}) %collective-permute-start.7) | collective-permute-done | bytes 491552 | tf_op jit(solution)/shard_map/ppermute | solution.py:37
  101.6 0.1 collective-permute-done.8
  101.7 0.3 select_select_fusion.3
  102.0 0.2 pad_maximum_fusion
  102.2 0.2 copy.9
  102.4 27.7 %all-gather.3.cloned.1.call-done = bf16[1,2560,1280]{2,1,0:T(8,128)(2,1)} async-done(((bf16[1,320,1280]{2,1,0:T(8,128)(2,1)}), bf16[1,2560,1280]{2,1,0:T(8,128)(2,1)}) %all-gather.3.cloned.1.call-update) | async-done | bytes 6553616 | tf_op jit(solution)/shard_map/all_gather | solution.py:66
  130.2 6.6 %fusion.12 = bf16[384,1280]{1,0:T(8,128)(2,1)} fusion(bf16[384,2560]{0,1:T(8,128)(2,1)S(1)} %bitcast.44, bf16[1,2560,1280]{2,1,0:T(8,128)(2,1)} %all-gather.3.cloned.1.call-done), kind=kOutput, calls=%fused_computation.17 | convolution fusion | flops 2517073920 | bytes 9502720 | tf_op jit(solution)/shard_map/dot_general | solution.py:113
  (14 shorter events, 0.1 us)
Async XLA Ops:
  6.5 19.0 %copy-start.5 = (s32[3]{0:T(128)S(1)}, s32[3]{0:T(128)}, u32[]{:S(2)}) copy-start(s32[3]{0:T(128)} %constant.116) | copy-start | bytes 40
  6.5 2.3 %copy-start = (bf16[384,640]{1,0:T(8,128)(2,1)S(1)}, bf16[384,640]{1,0:T(8,128)(2,1)}, u32[]{:S(2)}) copy-start(bf16[384,640]{1,0:T(8,128)(2,1)} %param.8) | copy-start | bytes 1474564
  6.5 8.6 %copy-start.1 = (bf16[384,640]{1,0:T(8,128)(2,1)S(1)}, bf16[384,640]{1,0:T(8,128)(2,1)}, u32[]{:S(2)}) copy-start(bf16[384,640]{1,0:T(8,128)(2,1)} %param.9) | copy-start | bytes 1474564
  6.5 14.5 %copy-start.2 = (s32[384]{0:T(512)S(1)}, s32[384]{0:T(512)}, u32[]{:S(2)}) copy-start(s32[384]{0:T(512)} %param.12) | copy-start | bytes 4612
  6.5 19.0 %copy-start.4 = (s32[4,27]{1,0:T(4,128)S(1)}, s32[4,27]{1,0:T(4,128)}, u32[]{:S(2)}) copy-start(s32[4,27]{1,0:T(4,128)} %param.11) | copy-start | bytes 1300
  6.5 123.6 %all-gather.3.cloned.1.call-start = ((), (), s32[]{:S(2)}) async-start(), calls=%async_computation | async-start | bytes 7372800 | tf_op jit(solution)/shard_map/all_gather | solution.py:66
  8.8 57.4 %collective-permute-start.2 = (bf16[384,640]{1,0:T(8,128)(2,1)S(1)}, bf16[384,640]{1,0:T(8,128)(2,1)S(1)}, u32[]{:S(2)}, u32[]{:S(2)}) collective-permute-start(bf16[384,640]{1,0:T(8,128)(2,1)S(1)} %copy-done), channel_id=1, source_target_pairs={{0,4},{4,8},{8,12},{1,5},{5,9},{9,13},{2,6},{6,10},{10,14},{3,7},{... | collective-permute-start | bytes 1474568 | tf_op jit(solution)/shard_map/ppermute | solution.py:16
  13.8 52.4 %collective-permute-start.3 = (bf16[384,640]{1,0:T(8,128)(2,1)S(1)}, bf16[384,640]{1,0:T(8,128)(2,1)S(1)}, u32[]{:S(2)}, u32[]{:S(2)}) collective-permute-start(bf16[384,640]{1,0:T(8,128)(2,1)S(1)} %copy-done), channel_id=1, source_target_pairs={{4,0},{8,4},{12,8},{5,1},{9,5},{13,9},{6,2},{10,6},{14,10},{7,3},{... | collective-permute-start | bytes 1474568 | tf_op jit(solution)/shard_map/ppermute | solution.py:16
  15.1 51.3 %collective-permute-start.4 = (bf16[384,640]{1,0:T(8,128)(2,1)S(1)}, bf16[384,640]{1,0:T(8,128)(2,1)S(1)}, u32[]{:S(2)}, u32[]{:S(2)}) collective-permute-start(bf16[384,640]{1,0:T(8,128)(2,1)S(1)} %copy-done.1), channel_id=1, source_target_pairs={{0,4},{4,8},{8,12},{1,5},{5,9},{9,13},{2,6},{6,10},{10,14},{3,7},{... | collective-permute-start | bytes 1474568 | tf_op jit(solution)/shard_map/ppermute | solution.py:16
  19.7 46.8 %collective-permute-start.5 = (bf16[384,640]{1,0:T(8,128)(2,1)S(1)}, bf16[384,640]{1,0:T(8,128)(2,1)S(1)}, u32[]{:S(2)}, u32[]{:S(2)}) collective-permute-start(bf16[384,640]{1,0:T(8,128)(2,1)S(1)} %copy-done.1), channel_id=1, source_target_pairs={{4,0},{8,4},{12,8},{5,1},{9,5},{13,9},{6,2},{10,6},{14,10},{7,3},{... | collective-permute-start | bytes 1474568 | tf_op jit(solution)/shard_map/ppermute | solution.py:16
  21.0 28.2 %collective-permute-start = (s32[384]{0:T(512)S(1)}, s32[384]{0:T(512)S(1)}, u32[]{:S(2)}, u32[]{:S(2)}) collective-permute-start(s32[384]{0:T(512)S(1)} %copy-done.2), channel_id=1, source_target_pairs={{0,4},{4,8},{8,12},{1,5},{5,9},{9,13},{2,6},{6,10},{10,14},{3,7},{... | collective-permute-start | bytes 4616 | tf_op jit(solution)/shard_map/ppermute | solution.py:16
  49.2 16.9 %collective-permute-start.1 = (s32[384]{0:T(512)S(1)}, s32[384]{0:T(512)S(1)}, u32[]{:S(2)}, u32[]{:S(2)}) collective-permute-start(s32[384]{0:T(512)S(1)} %copy-done.2), channel_id=1, source_target_pairs={{4,0},{8,4},{12,8},{5,1},{9,5},{13,9},{6,2},{10,6},{14,10},{7,3},{... | collective-permute-start | bytes 4616 | tf_op jit(solution)/shard_map/ppermute | solution.py:16
  66.4 1.0 copy-start.3
  77.5 10.6 %collective-permute-start.6 = (bf16[384,640]{0,1:T(8,128)(2,1)S(1)}, bf16[384,640]{0,1:T(8,128)(2,1)S(1)}, u32[]{:S(2)}, u32[]{:S(2)}) collective-permute-start(bf16[384,640]{0,1:T(8,128)(2,1)S(1)} %fusion.24), channel_id=1, source_target_pairs={{0,3},{1,0},{2,1},{3,2},{4,7},{5,4},{6,5},{7,6},{8,11},{9,8},{10,9... | collective-permute-start | bytes 1474568 | tf_op jit(solution)/shard_map/ppermute | solution.py:37
  77.6 24.0 %collective-permute-start.7 = (bf16[384,640]{0,1:T(8,128)(2,1)S(1)}, bf16[384,640]{0,1:T(8,128)(2,1)S(1)}, u32[]{:S(2)}, u32[]{:S(2)}) collective-permute-start(bf16[384,640]{0,1:T(8,128)(2,1)S(1)} %fusion.24), channel_id=1, source_target_pairs={{0,2},{1,3},{2,0},{3,1},{4,6},{5,7},{6,4},{7,5},{8,10},{9,11},{10,... | collective-permute-start | bytes 1474568 | tf_op jit(solution)/shard_map/ppermute | solution.py:37
  79.2 22.5 %collective-permute-start.8 = (bf16[384,640]{0,1:T(8,128)(2,1)S(1)}, bf16[384,640]{0,1:T(8,128)(2,1)S(1)}, u32[]{:S(2)}, u32[]{:S(2)}) collective-permute-start(bf16[384,640]{0,1:T(8,128)(2,1)S(1)} %fusion.24), channel_id=1, source_target_pairs={{0,1},{1,2},{2,3},{3,0},{4,5},{5,6},{6,7},{7,4},{8,9},{9,10},{10,1... | collective-permute-start | bytes 1474568 | tf_op jit(solution)/shard_map/ppermute | solution.py:37
Sparse Core Ops, SparseCore 0:
  9.5 120.6 all-gather.2
